TPU v7x, 32 devices: a whole 2x2x4 slice. The times are simulated.
32 devices in a mesh: src: 8 (over z, x), tgt: 4 (over y, core).
Axes of the slice: x: 2, y: 2, z: 4, core: 2. Of those that a mesh axis runs over, the one named last changes fastest.
Arguments:
- src_emb: bfloat16 [64, 16384], P(None, 'src'), may hold values from -2.75 to 2.75
- tgt_emb: bfloat16 [64, 32768], P(None, 'tgt'), may hold values from -2.75 to 2.75
- target_features: bfloat16 [128, 32768], P(None, 'tgt'), may hold values from -6 to 6
- src_mass: float32 [16384], P('src'), may hold values from 1 to 10
- tgt_mass: float32 [32768], P('tgt'), may hold values from 1 to 10
- kept_blocks: int32 [64, 32], P('src', 'tgt'), may hold values from 0 to 31, as said below
- kept_count: int32 [64, 4], P('src', 'tgt'), may hold values from 1 to 8
Outputs:
- projected: float32 [16384, 128], P(('src', 'tgt'))
- src_potential: float32 [16384], P('src')
- tgt_potential: float32 [32768], P('tgt')
Inputs may be any that keep to these rules, and one draw needn't show every extreme that they name: `kept_blocks`: entry [r, t * 8 + k] is a block number within target shard t; the 8 entries of one group are distinct; the first kept_count[r, t] of them are kept, the others are unused; every target block is kept by some source block row.
All inputs are finite; a program needn't handle non-finite values.
Results may differ from a plain program's by a relative error of at most 0.00075.
Values sent between devices are 32-bit elements; how exact they have to be, the bound alone decides.
No kernel may reach another device: no remote copies, remote signals or barrier semaphores. Data moves between devices by JAX's collectives and lax.ppermute only.
A program may use at most 64 MiB of HBM per device.

v0:
```python
import functools
import math

import jax
import jax.numpy as jnp
from jax import lax
from jax.experimental import pallas as pl
from jax.experimental.pallas import tpu as pltpu
from jax.sharding import PartitionSpec as P

BLOCK = 256
ITERS = 2


SENTINEL = -1e30
EPSILON = 0.1
SCALE = 1.0 / EPSILON
BASE2 = SCALE / math.log(2.0)


def lse_pair(value, other):
    overall = jnp.maximum(value, other)
    return overall + jnp.log(jnp.exp(value - overall) + jnp.exp(other - overall))


def butterfly_lse(value, axis):
    size = lax.axis_size(axis)
    step = 1
    while step < size:
        pairs = [(i, i ^ step) for i in range(size)]
        value = lse_pair(value, lax.ppermute(value, axis, pairs))
        step *= 2
    return value


def halving_merge(small, numerator, axis):
    size = lax.axis_size(axis)
    me = lax.axis_index(axis)
    rows = small.shape[1] // size
    small = small.reshape(2, size, rows)
    numerator = numerator.reshape(size, rows, numerator.shape[-1])
    step = 1
    while step < size:
        pairs = [(i, i ^ step) for i in range(size)]
        keep = (me // step) % 2
        count = numerator.shape[0] // 2

        def split(x, axis_at):
            x = x.reshape(x.shape[:axis_at] + (count, 2) + x.shape[axis_at + 1:])
            return (
                lax.dynamic_index_in_dim(x, keep, axis=axis_at + 1, keepdims=False),
                lax.dynamic_index_in_dim(x, 1 - keep, axis=axis_at + 1, keepdims=False),
            )

        small_keep, small_send = split(small, 1)
        num_keep, num_send = split(numerator, 0)
        small_other = lax.ppermute(small_send, axis, pairs)
        num_other = lax.ppermute(num_send, axis, pairs)
        overall = jnp.maximum(small_keep[0], small_other[0])
        mine = jnp.exp(small_keep[0] - overall)
        theirs = jnp.exp(small_other[0] - overall)
        numerator = num_keep * mine[..., None] + num_other * theirs[..., None]
        small = jnp.stack([overall, small_keep[1] * mine + small_other[1] * theirs])
        step *= 2
    return (numerator.reshape(rows, -1), small[1].reshape(rows))


CHUNK = 64
EXTRA = 16
VMEM_LIMIT = 24 * 1024 * 1024


def tile_slice(ref, b):
    return ref[:, pl.ds(pl.multiple_of(b * BLOCK, BLOCK), BLOCK)]


def row_slice(ref, r):
    return ref[pl.ds(pl.multiple_of(r * BLOCK, BLOCK), BLOCK), :]


def doubled_source(src_ref, r):
    exact = tile_slice(src_ref, r).astype(jnp.float32)
    return (exact * 2.0).astype(jnp.bfloat16), jnp.sum(exact * exact, axis=0, keepdims=True)


def products(doubled, tgt_ref, b):
    return lax.dot_general(doubled, tile_slice(tgt_ref, b), (((0,), (0,)), ((), ())),
                           preferred_element_type=jnp.float32)


def as_row(column, scratch):
    scratch[...] = jnp.broadcast_to(column, scratch.shape)
    return jnp.transpose(scratch[...])[0:1, :]


def as_column(row, scratch):
    scratch[...] = jnp.broadcast_to(row, scratch.shape)
    return jnp.transpose(scratch[...])[:, 0:1]


def by_count(live, slots, body):
    for count in range(1, slots + 1):
        pl.when(live == count)(functools.partial(body, count))


def over_rows(rows, body):
    lax.fori_loop(0, rows, lambda r, c: (body(r), c)[1], 0)


def fill_shifted(blocks_ref, r, count, doubled, tgt_ref, tnorm_ref, tpot_ref, held):
    for k in range(count):
        b = blocks_ref[r, k]
        shift = tile_slice(tpot_ref, b) - tile_slice(tnorm_ref, b)
        held[k] = products(doubled, tgt_ref, b) + shift


def chunk_peak(held, count, rows):
    peak = held[0, rows, :]
    for k in range(1, count):
        peak = jnp.maximum(peak, held[k, rows, :])
    return jnp.max(peak, axis=1, keepdims=True)


def row_kernel(blocks_ref, count_ref, src_ref, tgt_ref, tnorm_ref, tpot_ref,
               lse_ref, held, tgt_aug, rhs, peak_row, total_row):
    width = tgt_ref.shape[0]
    tgt_aug[0:width, :] = tgt_ref[...]
    tgt_aug[width:, :] = split_rows(tpot_ref[...] - tnorm_ref[...], False)

    def per_row(r):
        doubled, snorm = doubled_source(src_ref, r)
        rhs[0:width, :] = doubled
        rhs[width:, :] = split_rows(snorm, True)
        augmented = rhs[...]

        def body(count):
            for k in range(count):
                held[k] = lax.dot_general(tile_slice(tgt_aug, blocks_ref[r, k]), augmented,
                                          (((0,), (0,)), ((), ())),
                                          preferred_element_type=jnp.float32)
            folded = None
            for chunk in range(BLOCK // CHUNK):
                rows = pl.ds(chunk * CHUNK, CHUNK)
                peak = held[0, rows, :]
                for k in range(1, count):
                    peak = jnp.maximum(peak, held[k, rows, :])
                peak = jnp.max(peak.reshape(CHUNK // 8, 8, BLOCK), axis=0)
                folded = peak if folded is None else jnp.maximum(folded, peak)
            peak = jnp.max(folded, axis=0, keepdims=True)
            folded = None
            for chunk in range(BLOCK // CHUNK):
                rows = pl.ds(chunk * CHUNK, CHUNK)
                acc = jnp.exp2((held[0, rows, :] - peak) * BASE2)
                for k in range(1, count):
                    acc = acc + jnp.exp2((held[k, rows, :] - peak) * BASE2)
                acc = jnp.sum(acc.reshape(CHUNK // 8, 8, BLOCK), axis=0)
                folded = acc if folded is None else folded + acc
            peak_row[...] = peak
            total_row[...] = jnp.sum(folded, axis=0, keepdims=True)

        by_count(count_ref[r], held.shape[0], body)
        lanes = pl.ds(pl.multiple_of(r * BLOCK, BLOCK), BLOCK)
        lse_ref[:, lanes] = (peak_row[...] - snorm) * SCALE + jnp.log(total_row[...])

    over_rows(count_ref.shape[0], per_row)


def split_rows(row, ones):
    high = row.astype(jnp.bfloat16).astype(jnp.float32)
    middle = (row - high).astype(jnp.bfloat16).astype(jnp.float32)
    low = row - high - middle
    index = lax.broadcasted_iota(jnp.int32, (EXTRA, row.shape[1]), 0)
    if ones:
        rows = jnp.where(index < 3, 1.0, 0.0)
    else:
        rows = jnp.where(index == 0, high, jnp.where(index == 1, middle,
                                                     jnp.where(index == 2, low, 0.0)))
    return rows.astype(jnp.bfloat16)


def column_kernel(blocks_ref, count_ref, src_ref, spot_ref, tgt_ref, tnorm_ref,
                  lse_ref, top_ref, sum_ref, lhs):
    top_ref[...] = jnp.full(top_ref.shape, SENTINEL, jnp.float32)
    sum_ref[...] = jnp.zeros(sum_ref.shape, jnp.float32)
    width = src_ref.shape[0]

    def per_row(r):
        doubled, snorm = doubled_source(src_ref, r)
        lhs[0:width, :] = doubled
        lhs[width:, :] = split_rows(tile_slice(spot_ref, r) - snorm, False)
        augmented = lhs[...]

        def body(count):
            for k in range(count):
                b = blocks_ref[r, k]
                lanes = pl.ds(pl.multiple_of(b * BLOCK, BLOCK), BLOCK)
                shifted = products(augmented, tgt_ref, b)
                peak = jnp.max(shifted, axis=0, keepdims=True)
                totals = jnp.sum(jnp.exp2((shifted - peak) * BASE2), axis=0, keepdims=True)
                highest = (peak - tnorm_ref[:, lanes]) * SCALE
                old_top = top_ref[:, lanes]
                new_top = jnp.maximum(old_top, highest)
                sum_ref[:, lanes] = (sum_ref[:, lanes] * jnp.exp(old_top - new_top)
                                     + totals * jnp.exp(highest - new_top))
                top_ref[:, lanes] = new_top

        by_count(count_ref[r], blocks_ref.shape[1], body)

    over_rows(count_ref.shape[0], per_row)
    totals = sum_ref[...]
    lse_ref[...] = jnp.where(totals > 0.0, top_ref[...] + jnp.log(totals), SENTINEL)


def project_kernel(blocks_ref, count_ref, src_ref, tgt_ref, tnorm_ref, tpot_ref, feat_ref,
                   small_ref, num_ref, held, weights, high_col, den_col, wide):
    def per_row(r):
        doubled, snorm = doubled_source(src_ref, r)

        def body(count):
            fill_shifted(blocks_ref, r, count, doubled, tgt_ref, tnorm_ref, tpot_ref, held)
            for chunk in range(BLOCK // CHUNK):
                rows = pl.ds(chunk * CHUNK, CHUNK)
                peak = chunk_peak(held, count, rows)
                acc = jnp.zeros((CHUNK, BLOCK), jnp.float32)
                for k in range(count):
                    rounded = jnp.exp2((held[k, rows, :] - peak) * BASE2).astype(jnp.bfloat16)
                    weights[k, rows, :] = rounded
                    acc = acc + rounded.astype(jnp.float32)
                high_col[rows, :] = peak
                den_col[rows, :] = jnp.sum(acc, axis=1, keepdims=True)
            total = None
            for k in range(count):
                part = lax.dot_general(weights[k], tile_slice(feat_ref, blocks_ref[r, k]),
                                       (((1,), (1,)), ((), ())),
                                       preferred_element_type=jnp.float32)
                total = part if total is None else total + part
            num_ref[pl.ds(pl.multiple_of(r * BLOCK, BLOCK), BLOCK), :] = total

        by_count(count_ref[r], held.shape[0], body)
        lanes = pl.ds(pl.multiple_of(r * BLOCK, BLOCK), BLOCK)
        small_ref[0:1, lanes] = (as_row(high_col[...], wide) - snorm) * SCALE
        small_ref[1:2, lanes] = as_row(den_col[...], wide)

    over_rows(count_ref.shape[0], per_row)


def whole(shape):
    return pl.BlockSpec(shape, lambda r, *_: (0,) * len(shape))


def resident():
    return pl.BlockSpec(memory_space=pltpu.VMEM)


def column_scratch():
    return pltpu.VMEM((BLOCK, 1), jnp.float32)


def local_call(kernel, operands, outs, scratch):
    spec = pltpu.PrefetchScalarGridSpec(
        num_scalar_prefetch=2,
        grid=(1,),
        in_specs=[resident() for x in operands[2:]],
        out_specs=[resident() for o in outs],
        scratch_shapes=scratch,
    )
    return pl.pallas_call(
        kernel, grid_spec=spec, out_shape=outs,
        compiler_params=pltpu.CompilerParams(vmem_limit_bytes=VMEM_LIMIT),
    )(*operands)


def row_pass(blocks, counts, src, tgt, tnorm, tpot):
    slots = blocks.shape[1]
    return local_call(
        row_kernel, (blocks, counts, src, tgt, tnorm, tpot),
        [jax.ShapeDtypeStruct((1, src.shape[1]), jnp.float32)],
        [pltpu.VMEM((slots, BLOCK, BLOCK), jnp.float32),
         pltpu.VMEM((tgt.shape[0] + EXTRA, tgt.shape[1]), jnp.bfloat16),
         pltpu.VMEM((src.shape[0] + EXTRA, BLOCK), jnp.bfloat16),
         pltpu.VMEM((1, BLOCK), jnp.float32), pltpu.VMEM((1, BLOCK), jnp.float32)],
    )


def column_pass(blocks, counts, src, spot, tgt_ones, tnorm):
    return local_call(
        column_kernel, (blocks, counts, src, spot, tgt_ones, tnorm),
        [jax.ShapeDtypeStruct(tnorm.shape, jnp.float32)],
        [pltpu.VMEM(tnorm.shape, jnp.float32), pltpu.VMEM(tnorm.shape, jnp.float32),
         pltpu.VMEM((src.shape[0] + EXTRA, BLOCK), jnp.bfloat16)],
    )


def project_pass(blocks, counts, src, tgt, tnorm, tpot, feat):
    rows = src.shape[1]
    slots = blocks.shape[1]
    return local_call(
        project_kernel, (blocks, counts, src, tgt, tnorm, tpot, feat),
        [jax.ShapeDtypeStruct((2, rows), jnp.float32),
         jax.ShapeDtypeStruct((rows, feat.shape[0]), jnp.float32)],
        [pltpu.VMEM((slots, BLOCK, BLOCK), jnp.float32),
         pltpu.VMEM((slots, BLOCK, BLOCK), jnp.bfloat16),
         column_scratch(), column_scratch(), pltpu.VMEM((BLOCK, 128), jnp.float32)],
    )


def shards(src_emb, tgt_emb, target_features, src_mass, tgt_mass, kept_blocks, kept_count):
    src_rows = src_emb.shape[1]
    tgt_rows = tgt_emb.shape[1]
    src_t = src_emb
    tnorm = jnp.sum(jnp.square(tgt_emb.astype(jnp.float32)), axis=0).reshape(1, tgt_rows)
    counts = kept_count.reshape(-1)
    tgt_ones = jnp.concatenate(
        [tgt_emb, split_rows(jnp.zeros((1, tgt_rows), jnp.float32), True)], axis=0
    )

    tgt_potential = jnp.zeros((tgt_rows,), jnp.float32)
    src_potential = jnp.zeros((src_rows,), jnp.float32)
    for iteration in range(ITERS):
        tpot = tgt_potential.reshape(1, tgt_rows)
        (row_lse,) = row_pass(kept_blocks, counts, src_t, tgt_emb, tnorm, tpot)
        row_lse = butterfly_lse(row_lse.reshape(src_rows), "tgt")
        src_potential = EPSILON * jnp.log(src_mass) - EPSILON * row_lse
        (column_lse,) = column_pass(
            kept_blocks, counts, src_t, src_potential.reshape(1, src_rows), tgt_ones, tnorm
        )
        column_lse = butterfly_lse(column_lse.reshape(tgt_rows), "src")
        tgt_potential = EPSILON * jnp.log(tgt_mass) - EPSILON * column_lse

    tpot = tgt_potential.reshape(1, tgt_rows)
    small, numerator = project_pass(
        kept_blocks, counts, src_t, tgt_emb, tnorm, tpot, target_features
    )
    numerator, denominator = halving_merge(small, numerator, "tgt")
    projected = numerator / denominator[:, None]
    return (projected, src_potential, tgt_potential)


def solution(mesh):
    return jax.shard_map(
        shards,
        mesh=mesh,
        in_specs=(
            P(None, "src"),
            P(None, "tgt"),
            P(None, "tgt"),
            P("src"),
            P("tgt"),
            P("src", "tgt"),
            P("src", "tgt"),
        ),
        out_specs=(P(("src", "tgt"), None), P("src"), P("tgt")),
        check_vma=False,
    )
```

profile of v0, /device:TPU:0, one launch (start us, length us, event | category | flops | bytes accessed | tf_op | source)
XLA Modules:
  0.0 93.0 jit_solution(7446403575868250946)
XLA Ops:
  0.6 1.5 %multiply_reduce_fusion = f32[8192]{0:T(1024)S(1)} fusion(bf16[64,8192]{1,0:T(8,128)(2,1)} %tgt_ref.5), kind=kLoop, calls=%fused_computation | loop fusion | flops 1564672 | bytes 1081344 | tf_op jit(solution)/shard_map/reduce_sum | solution.py:311
  5.7 5.7 %shard_map.94 = f32[1,2048]{1,0:T(1,128)S(1)} custom-call(s32[8,8]{1,0:T(8,128)S(1)} %copy-done.7, s32[8]{0:T(128)S(1)} %bitcast.66, bf16[64,2048]{1,0:T(8,128)(2,1)S(1)} %copy-done.2, bf16[64,8192]{1,0:T(8,128)(2,1)S(1)} %copy-done, f32[1,8192]{1,0:T(1,128)S(1)} %bitcast.47, f32[1,8192]{1,0:T(1,128)S(1)} %reshape.186.tpot_ref), custom_call_target="tpu_custom_call" | custom-call | tf_op jit(solution)/shard_map/pallas_call | solution.py:267
  12.6 2.8 %collective-permute-start.1 = (f32[2048]{0:T(1024)S(1)}, f32[2048]{0:T(1024)S(1)}, u32[]{:S(2)}, u32[]{:S(2)}) collective-permute-start(f32[2048]{0:T(1024)S(1)} %log_add_fusion.5), channel_id=1, source_target_pairs={{0,2},{1,3},{2,0},{3,1},{4,6},{5,7},{6,4},{7,5},{8,10},{9,11},{10,... | collective-permute-start | bytes 24584 | tf_op jit(solution)/shard_map/ppermute | solution.py:31
  15.7 1.4 %collective-permute-done.1 = f32[2048]{0:T(1024)S(1)} collective-permute-done((f32[2048]{0:T(1024)S(1)}, f32[2048]{0:T(1024)S(1)}, u32[]{:S(2)}, u32[]{:S(2)}) %collective-permute-start.1) | collective-permute-done | bytes 8224 | tf_op jit(solution)/shard_map/ppermute | solution.py:31
  17.1 5.3 %shard_map.95 = f32[1,8192]{1,0:T(1,128)S(1)} custom-call(s32[8,8]{1,0:T(8,128)S(1)} %copy-done.7, s32[8]{0:T(128)S(1)} %bitcast.67, bf16[64,2048]{1,0:T(8,128)(2,1)S(1)} %copy-done.2, f32[1,2048]{1,0:T(1,128)S(1)} %bitcast.65, bf16[80,8192]{1,0:T(8,128)(2,1)S(1)} %pad_maximum_fusion.tgt_ref, f32[1,8192]{1,0:T(1,128)S(1)} %bitcast.48), custom_call_target="tpu_custom_call" | custom-call | tf_op jit(solution)/shard_map/pallas_call | solution.py:267
  22.4 2.2 %collective-permute-start.2 = (f32[8192]{0:T(1024)S(1)}, f32[8192]{0:T(1024)S(1)}, u32[]{:S(2)}, u32[]{:S(2)}) collective-permute-start(f32[8192]{0:T(1024)S(1)} %bitcast.55), channel_id=1, source_target_pairs={{0,4},{4,0},{8,12},{12,8},{16,20},{20,16},{24,28},{28,24},{1,5},{5... | collective-permute-start | bytes 98312 | tf_op jit(solution)/shard_map/ppermute | solution.py:31
  24.7 1.9 %collective-permute-done.2 = f32[8192]{0:T(1024)S(1)} collective-permute-done((f32[8192]{0:T(1024)S(1)}, f32[8192]{0:T(1024)S(1)}, u32[]{:S(2)}, u32[]{:S(2)}) %collective-permute-start.2) | collective-permute-done | bytes 32800 | tf_op jit(solution)/shard_map/ppermute | solution.py:31
  26.6 2.8 %collective-permute-start.3 = (f32[8192]{0:T(1024)S(1)}, f32[8192]{0:T(1024)S(1)}, u32[]{:S(2)}, u32[]{:S(2)}) collective-permute-start(f32[8192]{0:T(1024)S(1)} %log_add_fusion.3), channel_id=1, source_target_pairs={{0,8},{4,12},{8,0},{12,4},{16,24},{20,28},{24,16},{28,20},{1,9},{5... | collective-permute-start | bytes 98312 | tf_op jit(solution)/shard_map/ppermute | solution.py:31
  29.4 1.9 %collective-permute-done.3 = f32[8192]{0:T(1024)S(1)} collective-permute-done((f32[8192]{0:T(1024)S(1)}, f32[8192]{0:T(1024)S(1)}, u32[]{:S(2)}, u32[]{:S(2)}) %collective-permute-start.3) | collective-permute-done | bytes 32800 | tf_op jit(solution)/shard_map/ppermute | solution.py:31
  31.3 2.1 %collective-permute-start.4 = (f32[8192]{0:T(1024)S(1)}, f32[8192]{0:T(1024)S(1)}, u32[]{:S(2)}, u32[]{:S(2)}) collective-permute-start(f32[8192]{0:T(1024)S(1)} %log_add_fusion.2), channel_id=1, source_target_pairs={{0,16},{4,20},{8,24},{12,28},{16,0},{20,4},{24,8},{28,12},{1,17},{... | collective-permute-start | bytes 98312 | tf_op jit(solution)/shard_map/ppermute | solution.py:31
  33.4 2.8 %collective-permute-done.4 = f32[8192]{0:T(1024)S(1)} collective-permute-done((f32[8192]{0:T(1024)S(1)}, f32[8192]{0:T(1024)S(1)}, u32[]{:S(2)}, u32[]{:S(2)}) %collective-permute-start.4) | collective-permute-done | bytes 32800 | tf_op jit(solution)/shard_map/ppermute | solution.py:31
  36.3 5.7 %shard_map.96 = f32[1,2048]{1,0:T(1,128)S(1)} custom-call(s32[8,8]{1,0:T(8,128)S(1)} %copy-done.7, s32[8]{0:T(128)S(1)} %bitcast.68, bf16[64,2048]{1,0:T(8,128)(2,1)S(1)} %copy-done.2, bf16[64,8192]{1,0:T(8,128)(2,1)S(1)} %copy-done.1, f32[1,8192]{1,0:T(1,128)S(1)} %bitcast.49, f32[1,8192]{1,0:T(1,128)S(1)} %bitcast.59), custom_call_target="tpu_custom_call" | custom-call | tf_op jit(solution)/shard_map/pallas_call | solution.py:267
  43.2 1.2 %collective-permute-start.6 = (f32[2048]{0:T(1024)S(1)}, f32[2048]{0:T(1024)S(1)}, u32[]{:S(2)}, u32[]{:S(2)}) collective-permute-start(f32[2048]{0:T(1024)S(1)} %log_add_fusion.4), channel_id=1, source_target_pairs={{0,2},{1,3},{2,0},{3,1},{4,6},{5,7},{6,4},{7,5},{8,10},{9,11},{10,... | collective-permute-start | bytes 24584 | tf_op jit(solution)/shard_map/ppermute | solution.py:31
  44.5 2.5 %collective-permute-done.6 = f32[2048]{0:T(1024)S(1)} collective-permute-done((f32[2048]{0:T(1024)S(1)}, f32[2048]{0:T(1024)S(1)}, u32[]{:S(2)}, u32[]{:S(2)}) %collective-permute-start.6) | collective-permute-done | bytes 8224 | tf_op jit(solution)/shard_map/ppermute | solution.py:31
  47.0 5.5 %shard_map.97 = f32[1,8192]{1,0:T(1,128)S(1)} custom-call(s32[8,8]{1,0:T(8,128)S(1)} %copy-done.7, s32[8]{0:T(128)S(1)} %bitcast.69, bf16[64,2048]{1,0:T(8,128)(2,1)S(1)} %copy-done.2, f32[1,2048]{1,0:T(1,128)S(1)} %bitcast.64, bf16[80,8192]{1,0:T(8,128)(2,1)S(1)} %pad_maximum_fusion.tgt_ref, f32[1,8192]{1,0:T(1,128)S(1)} %bitcast.50), custom_call_target="tpu_custom_call" | custom-call | tf_op jit(solution)/shard_map/pallas_call | solution.py:267
  52.5 1.5 %collective-permute-start.7 = (f32[8192]{0:T(1024)S(1)}, f32[8192]{0:T(1024)S(1)}, u32[]{:S(2)}, u32[]{:S(2)}) collective-permute-start(f32[8192]{0:T(1024)S(1)} %bitcast.57), channel_id=1, source_target_pairs={{0,4},{4,0},{8,12},{12,8},{16,20},{20,16},{24,28},{28,24},{1,5},{5... | collective-permute-start | bytes 98312 | tf_op jit(solution)/shard_map/ppermute | solution.py:31
  54.0 2.5 %collective-permute-done.7 = f32[8192]{0:T(1024)S(1)} collective-permute-done((f32[8192]{0:T(1024)S(1)}, f32[8192]{0:T(1024)S(1)}, u32[]{:S(2)}, u32[]{:S(2)}) %collective-permute-start.7) | collective-permute-done | bytes 32800 | tf_op jit(solution)/shard_map/ppermute | solution.py:31
  56.5 2.6 %collective-permute-start.8 = (f32[8192]{0:T(1024)S(1)}, f32[8192]{0:T(1024)S(1)}, u32[]{:S(2)}, u32[]{:S(2)}) collective-permute-start(f32[8192]{0:T(1024)S(1)} %log_add_fusion.1), channel_id=1, source_target_pairs={{0,8},{4,12},{8,0},{12,4},{16,24},{20,28},{24,16},{28,20},{1,9},{5... | collective-permute-start | bytes 98312 | tf_op jit(solution)/shard_map/ppermute | solution.py:31
  59.1 1.9 %collective-permute-done.8 = f32[8192]{0:T(1024)S(1)} collective-permute-done((f32[8192]{0:T(1024)S(1)}, f32[8192]{0:T(1024)S(1)}, u32[]{:S(2)}, u32[]{:S(2)}) %collective-permute-start.8) | collective-permute-done | bytes 32800 | tf_op jit(solution)/shard_map/ppermute | solution.py:31
  61.1 1.2 %collective-permute-start.9 = (f32[8192]{0:T(1024)S(1)}, f32[8192]{0:T(1024)}, u32[]{:S(2)}, u32[]{:S(2)}) collective-permute-start(f32[8192]{0:T(1024)S(1)} %log_add_fusion), channel_id=1, source_target_pairs={{0,16},{4,20},{8,24},{12,28},{16,0},{20,4},{24,8},{28,12},{1,17},{... | collective-permute-start | bytes 98312 | tf_op jit(solution)/shard_map/ppermute | solution.py:31
  62.3 3.7 %collective-permute-done.9 = f32[8192]{0:T(1024)} collective-permute-done((f32[8192]{0:T(1024)S(1)}, f32[8192]{0:T(1024)}, u32[]{:S(2)}, u32[]{:S(2)}) %collective-permute-start.9) | collective-permute-done | bytes 32800 | tf_op jit(solution)/shard_map/ppermute | solution.py:31
  66.9 10.7 %shard_map.98 = (f32[2,2048]{1,0:T(2,128)S(1)}, f32[2048,128]{1,0:T(8,128)S(1)}) custom-call(s32[8,8]{1,0:T(8,128)S(1)} %copy-done.8, s32[8]{0:T(128)S(1)} %bitcast.70, bf16[64,2048]{1,0:T(8,128)(2,1)S(1)} %copy-done.3, bf16[64,8192]{1,0:T(8,128)(2,1)S(1)} %copy-done.1, f32[1,8192]{1,0:T(1,128)S(1)} %bitcast.51, f32[1,8192]{1,0:T(1,128)S(1)} %bitcast.54, ...), custom_call_target="tpu_custom_call" | custom-call | tf_op jit(solution)/shard_map/pallas_call | solution.py:267
  81.9 1.4 %fusion = f32[2,512,128]{2,1,0:T(8,128)S(1)} fusion(f32[2,512,128]{2,1,0:T(8,128)S(1)} %collective-permute-done.11, f32[2,2,512,128]{3,2,1,0:T(8,128)} %bitcast.53, s32[]{:T(128)S(6)} %select_n.43, f32[2,512]{1,0:T(2,128)S(1)} %get-tuple-element.15, f32[2,512]{1,0:T(2,128)S(1)} %get-tuple-element.14), kind=kLoop, calls=%fused_computation.3 | loop fusion | flops 393216 | bytes 1581060 | tf_op jit(solution)/shard_map/add | solution.py:62
  84.2 7.8 %collective-permute-done.13 = f32[1,512,128]{2,1,0:T(8,128)S(1)} collective-permute-done((f32[1,512,128]{2,1,0:T(8,128)S(1)}, f32[1,512,128]{2,1,0:T(8,128)S(1)}, u32[]{:S(2)}, u32[]{:S(2)}) %collective-permute-start.13) | collective-permute-done | bytes 262176 | tf_op jit(solution)/shard_map/ppermute | solution.py:58
  (66 shorter events, 13.4 us)
Async XLA Ops:
  2.1 14.9 %copy-start.13 = (f32[2048]{0:T(1024)S(1)}, f32[2048]{0:T(1024)}, u32[]{:S(2)}) copy-start(f32[2048]{0:T(1024)} %param.10) | copy-start | bytes 24580
  2.2 1.2 %copy-start = (bf16[64,8192]{1,0:T(8,128)(2,1)S(1)}, bf16[64,8192]{1,0:T(8,128)(2,1)}, u32[]{:S(2)}) copy-start(bf16[64,8192]{1,0:T(8,128)(2,1)} %tgt_ref.5) | copy-start | bytes 3145732
  11.4 1.2 %collective-permute-start = (f32[2048]{0:T(1024)S(1)}, f32[2048]{0:T(1024)S(1)}, u32[]{:S(2)}, u32[]{:S(2)}) collective-permute-start(f32[2048]{0:T(1024)S(1)} %bitcast.60), channel_id=1, source_target_pairs={{0,1},{1,0},{2,3},{3,2},{4,5},{5,4},{6,7},{7,6},{8,9},{9,8},{10,11... | collective-permute-start | bytes 24584 | tf_op jit(solution)/shard_map/ppermute | solution.py:31
  12.6 23.6 %copy-start.12 = (f32[8192]{0:T(1024)S(1)}, f32[8192]{0:T(1024)}, u32[]{:S(2)}) copy-start(f32[8192]{0:T(1024)} %param.11) | copy-start | bytes 98308
  12.6 23.6 %copy-start.1 = (bf16[64,8192]{1,0:T(8,128)(2,1)S(1)}, bf16[64,8192]{1,0:T(8,128)(2,1)}, u32[]{:S(2)}) copy-start(bf16[64,8192]{1,0:T(8,128)(2,1)} %tgt_ref.5) | copy-start | bytes 3145732
  12.6 4.4 %collective-permute-start.1 = (f32[2048]{0:T(1024)S(1)}, f32[2048]{0:T(1024)S(1)}, u32[]{:S(2)}, u32[]{:S(2)}) collective-permute-start(f32[2048]{0:T(1024)S(1)} %log_add_fusion.5), channel_id=1, source_target_pairs={{0,2},{1,3},{2,0},{3,1},{4,6},{5,7},{6,4},{7,5},{8,10},{9,11},{10,... | collective-permute-start | bytes 24584 | tf_op jit(solution)/shard_map/ppermute | solution.py:31
  22.4 44.5 %copy-start.3 = (bf16[64,2048]{1,0:T(8,128)(2,1)S(1)}, bf16[64,2048]{1,0:T(8,128)(2,1)}, u32[]{:S(2)}) copy-start(bf16[64,2048]{1,0:T(8,128)(2,1)} %src_ref.9) | copy-start | bytes 786436
  22.4 44.5 %copy-start.4 = (bf16[128,8192]{1,0:T(8,128)(2,1)S(1)}, bf16[128,8192]{1,0:T(8,128)(2,1)}, u32[]{:S(2)}) copy-start(bf16[128,8192]{1,0:T(8,128)(2,1)} %feat_ref.1) | copy-start | bytes 6291460
  22.4 44.5 %copy-start.8 = (s32[8,8]{1,0:T(8,128)S(1)}, s32[8,8]{1,0:T(8,128)}, u32[]{:S(2)}) copy-start(s32[8,8]{1,0:T(8,128)} %blocks_ref.9) | copy-start | bytes 772
  22.4 44.5 %copy-start.11 = (s32[8,1]{0,1:T(1,128)S(1)}, s32[8,1]{0,1:T(1,128)}, u32[]{:S(2)}) copy-start(s32[8,1]{0,1:T(1,128)} %param.13) | copy-start | bytes 100
  22.4 4.1 %collective-permute-start.2 = (f32[8192]{0:T(1024)S(1)}, f32[8192]{0:T(1024)S(1)}, u32[]{:S(2)}, u32[]{:S(2)}) collective-permute-start(f32[8192]{0:T(1024)S(1)} %bitcast.55), channel_id=1, source_target_pairs={{0,4},{4,0},{8,12},{12,8},{16,20},{20,16},{24,28},{28,24},{1,5},{5... | collective-permute-start | bytes 98312 | tf_op jit(solution)/shard_map/ppermute | solution.py:31
  26.6 4.7 %collective-permute-start.3 = (f32[8192]{0:T(1024)S(1)}, f32[8192]{0:T(1024)S(1)}, u32[]{:S(2)}, u32[]{:S(2)}) collective-permute-start(f32[8192]{0:T(1024)S(1)} %log_add_fusion.3), channel_id=1, source_target_pairs={{0,8},{4,12},{8,0},{12,4},{16,24},{20,28},{24,16},{28,20},{1,9},{5... | collective-permute-start | bytes 98312 | tf_op jit(solution)/shard_map/ppermute | solution.py:31
  31.3 4.9 %collective-permute-start.4 = (f32[8192]{0:T(1024)S(1)}, f32[8192]{0:T(1024)S(1)}, u32[]{:S(2)}, u32[]{:S(2)}) collective-permute-start(f32[8192]{0:T(1024)S(1)} %log_add_fusion.2), channel_id=1, source_target_pairs={{0,16},{4,20},{8,24},{12,28},{16,0},{20,4},{24,8},{28,12},{1,17},{... | collective-permute-start | bytes 98312 | tf_op jit(solution)/shard_map/ppermute | solution.py:31
  42.0 1.2 %collective-permute-start.5 = (f32[2048]{0:T(1024)S(1)}, f32[2048]{0:T(1024)S(1)}, u32[]{:S(2)}, u32[]{:S(2)}) collective-permute-start(f32[2048]{0:T(1024)S(1)} %bitcast.62), channel_id=1, source_target_pairs={{0,1},{1,0},{2,3},{3,2},{4,5},{5,4},{6,7},{7,6},{8,9},{9,8},{10,11... | collective-permute-start | bytes 24584 | tf_op jit(solution)/shard_map/ppermute | solution.py:31
  43.2 3.7 %collective-permute-start.6 = (f32[2048]{0:T(1024)S(1)}, f32[2048]{0:T(1024)S(1)}, u32[]{:S(2)}, u32[]{:S(2)}) collective-permute-start(f32[2048]{0:T(1024)S(1)} %log_add_fusion.4), channel_id=1, source_target_pairs={{0,2},{1,3},{2,0},{3,1},{4,6},{5,7},{6,4},{7,5},{8,10},{9,11},{10,... | collective-permute-start | bytes 24584 | tf_op jit(solution)/shard_map/ppermute | solution.py:31
  47.0 30.7 %copy-start.9 = (f32[2048]{0:T(1024)}, f32[2048]{0:T(1024)S(1)}, u32[]{:S(2)}) copy-start(f32[2048]{0:T(1024)S(1)} %multiply_subtract_fusion.2) | copy-start | bytes 24580
  52.5 4.0 %collective-permute-start.7 = (f32[8192]{0:T(1024)S(1)}, f32[8192]{0:T(1024)S(1)}, u32[]{:S(2)}, u32[]{:S(2)}) collective-permute-start(f32[8192]{0:T(1024)S(1)} %bitcast.57), channel_id=1, source_target_pairs={{0,4},{4,0},{8,12},{12,8},{16,20},{20,16},{24,28},{28,24},{1,5},{5... | collective-permute-start | bytes 98312 | tf_op jit(solution)/shard_map/ppermute | solution.py:31
  56.5 4.6 %collective-permute-start.8 = (f32[8192]{0:T(1024)S(1)}, f32[8192]{0:T(1024)S(1)}, u32[]{:S(2)}, u32[]{:S(2)}) collective-permute-start(f32[8192]{0:T(1024)S(1)} %log_add_fusion.1), channel_id=1, source_target_pairs={{0,8},{4,12},{8,0},{12,4},{16,24},{20,28},{24,16},{28,20},{1,9},{5... | collective-permute-start | bytes 98312 | tf_op jit(solution)/shard_map/ppermute | solution.py:31
  61.1 5.0 %collective-permute-start.9 = (f32[8192]{0:T(1024)S(1)}, f32[8192]{0:T(1024)}, u32[]{:S(2)}, u32[]{:S(2)}) collective-permute-start(f32[8192]{0:T(1024)S(1)} %log_add_fusion), channel_id=1, source_target_pairs={{0,16},{4,20},{8,24},{12,28},{16,0},{20,4},{24,8},{28,12},{1,17},{... | collective-permute-start | bytes 98312 | tf_op jit(solution)/shard_map/ppermute | solution.py:31
  66.9 13.0 %copy-start.6 = (f32[8192]{0:T(1024)}, f32[8192]{0:T(1024)S(1)}, u32[]{:S(2)}) copy-start(f32[8192]{0:T(1024)S(1)} %multiply_subtract_fusion) | copy-start | bytes 98308
  78.7 1.7 %collective-permute-start.10 = (f32[2,2,512]{2,1,0:T(2,128)S(1)}, f32[2,2,512]{2,1,0:T(2,128)S(1)}, u32[]{:S(2)}, u32[]{:S(2)}) collective-permute-start(f32[2,2,512]{2,1,0:T(2,128)S(1)} %bitcast.71), channel_id=1, source_target_pairs={{0,1},{1,0},{2,3},{3,2},{4,5},{5,4},{6,7},{7,6},{8,9},{9,8},{10,11... | collective-permute-start | bytes 24584 | tf_op jit(solution)/shard_map/ppermute | solution.py:57
  79.9 2.1 %collective-permute-start.11 = (f32[2,512,128]{2,1,0:T(8,128)S(1)}, f32[2,512,128]{2,1,0:T(8,128)S(1)}, u32[]{:S(2)}, u32[]{:S(2)}) collective-permute-start(f32[2,512,128]{2,1,0:T(8,128)S(1)} %dynamic-slice_bitcast_fusion), channel_id=1, source_target_pairs={{0,1},{1,0},{2,3},{3,2},{4,5},{5,4},{6,7},{7,6},{8,9},{9,8},{10,11... | collective-permute-start | bytes 1572872 | tf_op jit(solution)/shard_map/ppermute | solution.py:58
  80.5 3.7 %collective-permute-start.12 = (f32[2,1,512]{2,1,0:T(1,128)S(1)}, f32[2,1,512]{2,1,0:T(1,128)S(1)}, u32[]{:S(2)}, u32[]{:S(2)}) collective-permute-start(f32[2,1,512]{2,1,0:T(1,128)S(1)} %get-tuple-element.17), channel_id=1, source_target_pairs={{0,2},{1,3},{2,0},{3,1},{4,6},{5,7},{6,4},{7,5},{8,10},{9,11},{10,... | collective-permute-start | bytes 12296 | tf_op jit(solution)/shard_map/ppermute | solution.py:57
  83.4 8.7 %collective-permute-start.13 = (f32[1,512,128]{2,1,0:T(8,128)S(1)}, f32[1,512,128]{2,1,0:T(8,128)S(1)}, u32[]{:S(2)}, u32[]{:S(2)}) collective-permute-start(f32[1,512,128]{2,1,0:T(8,128)S(1)} %constant_dynamic-slice_fusion.1), channel_id=1, source_target_pairs={{0,2},{1,3},{2,0},{3,1},{4,6},{5,7},{6,4},{7,5},{8,10},{9,11},{10,... | collective-permute-start | bytes 786440 | tf_op jit(solution)/shard_map/ppermute | solution.py:58
  (4 other events, 3.3 us)
where the time goes:
time: 94.5 us; the launch traced here: 93 us
  Pallas kernels  32.9 us (35%)
  waiting for transfers between devices  29.3 us (31%)
  starting transfers between devices  18.8 us (20%)
  local copies, waits for them, and re-layouts  5.83 us (6%)
  other arithmetic  5.17 us (5%)
    pallas_call x5, Pallas kernels, local_call(): pl.pallas_call(kernel, grid_spec=spec, out_shape=outs, compiler_params=pl...  32.9 us
    ppermute x10, waiting for transfers between devices, butterfly_lse(): value = lse_pair(value, lax.ppermute(value, axis, pairs))  20.7 us
    ppermute x10, starting transfers between devices, butterfly_lse(): value = lse_pair(value, lax.ppermute(value, axis, pairs))  16.8 us
    ppermute x2, waiting for transfers between devices, halving_merge(): num_other = lax.ppermute(num_send, axis, pairs)  8.57 us
    unnamed x29, local copies, waits for them, and re-layouts  4.56 us
  transfers between devices with their start and end apart: 14, of which 13 were waited for; matrix products, arithmetic and copies ran while one was open for 3% of the time, Pallas kernels for 0%

commit v1 on v0

--- a/solution.py
+++ b/solution.py
@@ -212,34 +212,54 @@
 
 
 def project_kernel(blocks_ref, count_ref, src_ref, tgt_ref, tnorm_ref, tpot_ref, feat_ref,
-                   small_ref, num_ref, held, weights, high_col, den_col, wide):
+                   small_ref, num_ref, held, weights, tgt_aug, rhs, peak_row, den_row):
+    width = tgt_ref.shape[0]
+    tgt_aug[0:width, :] = tgt_ref[...]
+    tgt_aug[width:, :] = split_rows(tpot_ref[...] - tnorm_ref[...], False)
+
     def per_row(r):
         doubled, snorm = doubled_source(src_ref, r)
+        rhs[0:width, :] = doubled
+        rhs[width:, :] = split_rows(snorm, True)
+        augmented = rhs[...]
 
         def body(count):
-            fill_shifted(blocks_ref, r, count, doubled, tgt_ref, tnorm_ref, tpot_ref, held)
+            for k in range(count):
+                held[k] = lax.dot_general(tile_slice(tgt_aug, blocks_ref[r, k]), augmented,
+                                          (((0,), (0,)), ((), ())),
+                                          preferred_element_type=jnp.float32)
+            folded = None
             for chunk in range(BLOCK // CHUNK):
                 rows = pl.ds(chunk * CHUNK, CHUNK)
-                peak = chunk_peak(held, count, rows)
+                peak = held[0, rows, :]
+                for k in range(1, count):
+                    peak = jnp.maximum(peak, held[k, rows, :])
+                peak = jnp.max(peak.reshape(CHUNK // 8, 8, BLOCK), axis=0)
+                folded = peak if folded is None else jnp.maximum(folded, peak)
+            peak = jnp.max(folded, axis=0, keepdims=True)
+            folded = None
+            for chunk in range(BLOCK // CHUNK):
+                rows = pl.ds(chunk * CHUNK, CHUNK)
                 acc = jnp.zeros((CHUNK, BLOCK), jnp.float32)
                 for k in range(count):
                     rounded = jnp.exp2((held[k, rows, :] - peak) * BASE2).astype(jnp.bfloat16)
                     weights[k, rows, :] = rounded
                     acc = acc + rounded.astype(jnp.float32)
-                high_col[rows, :] = peak
-                den_col[rows, :] = jnp.sum(acc, axis=1, keepdims=True)
+                acc = jnp.sum(acc.reshape(CHUNK // 8, 8, BLOCK), axis=0)
+                folded = acc if folded is None else folded + acc
             total = None
             for k in range(count):
-                part = lax.dot_general(weights[k], tile_slice(feat_ref, blocks_ref[r, k]),
-                                       (((1,), (1,)), ((), ())),
-                                       preferred_element_type=jnp.float32)
+                part = jnp.dot(tile_slice(feat_ref, blocks_ref[r, k]), weights[k],
+                               preferred_element_type=jnp.float32)
                 total = part if total is None else total + part
-            num_ref[pl.ds(pl.multiple_of(r * BLOCK, BLOCK), BLOCK), :] = total
+            num_ref[pl.ds(pl.multiple_of(r * BLOCK, BLOCK), BLOCK), :] = jnp.transpose(total)
+            peak_row[...] = peak
+            den_row[...] = jnp.sum(folded, axis=0, keepdims=True)
 
         by_count(count_ref[r], held.shape[0], body)
         lanes = pl.ds(pl.multiple_of(r * BLOCK, BLOCK), BLOCK)
-        small_ref[0:1, lanes] = (as_row(high_col[...], wide) - snorm) * SCALE
-        small_ref[1:2, lanes] = as_row(den_col[...], wide)
+        small_ref[0:1, lanes] = (peak_row[...] - snorm) * SCALE
+        small_ref[1:2, lanes] = den_row[...]
 
     over_rows(count_ref.shape[0], per_row)
 
@@ -300,7 +320,9 @@
          jax.ShapeDtypeStruct((rows, feat.shape[0]), jnp.float32)],
         [pltpu.VMEM((slots, BLOCK, BLOCK), jnp.float32),
          pltpu.VMEM((slots, BLOCK, BLOCK), jnp.bfloat16),
-         column_scratch(), column_scratch(), pltpu.VMEM((BLOCK, 128), jnp.float32)],
+         pltpu.VMEM((tgt.shape[0] + EXTRA, tgt.shape[1]), jnp.bfloat16),
+         pltpu.VMEM((src.shape[0] + EXTRA, BLOCK), jnp.bfloat16),
+         pltpu.VMEM((1, BLOCK), jnp.float32), pltpu.VMEM((1, BLOCK), jnp.float32)],
     )
 
 

time: 94.5 us -> 93.5 us (0.989)
  no operation moved by 1% of the time
where the time goes in v1:
time: 93.5 us; the launch traced here: 92.9 us
  Pallas kernels  32.7 us (35%)
  waiting for transfers between devices  29 us (31%)
  starting transfers between devices  19.3 us (21%)
  local copies, waits for them, and re-layouts  5.8 us (6%)
  other arithmetic  5.17 us (6%)
  between operations  0.96 us (1%)
    pallas_call x5, Pallas kernels, local_call(): pl.pallas_call(kernel, grid_spec=spec, out_shape=outs, compiler_params=pl...  32.7 us
    ppermute x10, waiting for transfers between devices, butterfly_lse(): value = lse_pair(value, lax.ppermute(value, axis, pairs))  20 us
    ppermute x10, starting transfers between devices, butterfly_lse(): value = lse_pair(value, lax.ppermute(value, axis, pairs))  17.6 us
    ppermute x2, waiting for transfers between devices, halving_merge(): num_other = lax.ppermute(num_send, axis, pairs)  8.94 us
    unnamed x29, local copies, waits for them, and re-layouts  4.54 us
  transfers between devices with their start and end apart: 14, of which 13 were waited for; matrix products, arithmetic and copies ran while one was open for 3% of the time, Pallas kernels for 0%

profile of v1, /device:TPU:0, one launch (start us, length us, event | category | flops | bytes accessed | tf_op | source)
XLA Modules:
  0.0 92.9 jit_solution(8802493958771899757)
XLA Ops:
  0.6 1.5 %multiply_reduce_fusion = f32[8192]{0:T(1024)S(1)} fusion(bf16[64,8192]{1,0:T(8,128)(2,1)} %tgt_ref.5), kind=kLoop, calls=%fused_computation | loop fusion | flops 1564672 | bytes 1081344 | tf_op jit(solution)/shard_map/reduce_sum | solution.py:333
  2.2 1.2 %copy-done = bf16[64,8192]{1,0:T(8,128)(2,1)S(1)} copy-done((bf16[64,8192]{1,0:T(8,128)(2,1)S(1)}, bf16[64,8192]{1,0:T(8,128)(2,1)}, u32[]{:S(2)}) %copy-start) | copy-done | bytes 1048600
  5.7 5.8 %shard_map.94 = f32[1,2048]{1,0:T(1,128)S(1)} custom-call(s32[8,8]{1,0:T(8,128)S(1)} %copy-done.7, s32[8]{0:T(128)S(1)} %bitcast.66, bf16[64,2048]{1,0:T(8,128)(2,1)S(1)} %copy-done.2, bf16[64,8192]{1,0:T(8,128)(2,1)S(1)} %copy-done, f32[1,8192]{1,0:T(1,128)S(1)} %bitcast.47, f32[1,8192]{1,0:T(1,128)S(1)} %reshape.186.tpot_ref), custom_call_target="tpu_custom_call" | custom-call | tf_op jit(solution)/shard_map/pallas_call | solution.py:287
  12.8 3.0 %collective-permute-start.1 = (f32[2048]{0:T(1024)S(1)}, f32[2048]{0:T(1024)S(1)}, u32[]{:S(2)}, u32[]{:S(2)}) collective-permute-start(f32[2048]{0:T(1024)S(1)} %log_add_fusion.5), channel_id=1, source_target_pairs={{0,2},{1,3},{2,0},{3,1},{4,6},{5,7},{6,4},{7,5},{8,10},{9,11},{10,... | collective-permute-start | bytes 24584 | tf_op jit(solution)/shard_map/ppermute | solution.py:31
  16.0 1.4 %collective-permute-done.1 = f32[2048]{0:T(1024)S(1)} collective-permute-done((f32[2048]{0:T(1024)S(1)}, f32[2048]{0:T(1024)S(1)}, u32[]{:S(2)}, u32[]{:S(2)}) %collective-permute-start.1) | collective-permute-done | bytes 8224 | tf_op jit(solution)/shard_map/ppermute | solution.py:31
  17.4 5.5 %shard_map.95 = f32[1,8192]{1,0:T(1,128)S(1)} custom-call(s32[8,8]{1,0:T(8,128)S(1)} %copy-done.7, s32[8]{0:T(128)S(1)} %bitcast.67, bf16[64,2048]{1,0:T(8,128)(2,1)S(1)} %copy-done.2, f32[1,2048]{1,0:T(1,128)S(1)} %bitcast.65, bf16[80,8192]{1,0:T(8,128)(2,1)S(1)} %pad_maximum_fusion.tgt_ref, f32[1,8192]{1,0:T(1,128)S(1)} %bitcast.48), custom_call_target="tpu_custom_call" | custom-call | tf_op jit(solution)/shard_map/pallas_call | solution.py:287
  23.0 1.4 %collective-permute-start.2 = (f32[8192]{0:T(1024)S(1)}, f32[8192]{0:T(1024)S(1)}, u32[]{:S(2)}, u32[]{:S(2)}) collective-permute-start(f32[8192]{0:T(1024)S(1)} %bitcast.55), channel_id=1, source_target_pairs={{0,4},{4,0},{8,12},{12,8},{16,20},{20,16},{24,28},{28,24},{1,5},{5... | collective-permute-start | bytes 98312 | tf_op jit(solution)/shard_map/ppermute | solution.py:31
  24.4 2.6 %collective-permute-done.2 = f32[8192]{0:T(1024)S(1)} collective-permute-done((f32[8192]{0:T(1024)S(1)}, f32[8192]{0:T(1024)S(1)}, u32[]{:S(2)}, u32[]{:S(2)}) %collective-permute-start.2) | collective-permute-done | bytes 32800 | tf_op jit(solution)/shard_map/ppermute | solution.py:31
  27.0 1.8 %collective-permute-start.3 = (f32[8192]{0:T(1024)S(1)}, f32[8192]{0:T(1024)S(1)}, u32[]{:S(2)}, u32[]{:S(2)}) collective-permute-start(f32[8192]{0:T(1024)S(1)} %log_add_fusion.3), channel_id=1, source_target_pairs={{0,8},{4,12},{8,0},{12,4},{16,24},{20,28},{24,16},{28,20},{1,9},{5... | collective-permute-start | bytes 98312 | tf_op jit(solution)/shard_map/ppermute | solution.py:31
  28.8 2.2 %collective-permute-done.3 = f32[8192]{0:T(1024)S(1)} collective-permute-done((f32[8192]{0:T(1024)S(1)}, f32[8192]{0:T(1024)S(1)}, u32[]{:S(2)}, u32[]{:S(2)}) %collective-permute-start.3) | collective-permute-done | bytes 32800 | tf_op jit(solution)/shard_map/ppermute | solution.py:31
  31.0 3.4 %collective-permute-start.4 = (f32[8192]{0:T(1024)S(1)}, f32[8192]{0:T(1024)S(1)}, u32[]{:S(2)}, u32[]{:S(2)}) collective-permute-start(f32[8192]{0:T(1024)S(1)} %log_add_fusion.2), channel_id=1, source_target_pairs={{0,16},{4,20},{8,24},{12,28},{16,0},{20,4},{24,8},{28,12},{1,17},{... | collective-permute-start | bytes 98312 | tf_op jit(solution)/shard_map/ppermute | solution.py:31
  34.4 1.9 %collective-permute-done.4 = f32[8192]{0:T(1024)S(1)} collective-permute-done((f32[8192]{0:T(1024)S(1)}, f32[8192]{0:T(1024)S(1)}, u32[]{:S(2)}, u32[]{:S(2)}) %collective-permute-start.4) | collective-permute-done | bytes 32800 | tf_op jit(solution)/shard_map/ppermute | solution.py:31
  36.4 5.8 %shard_map.96 = f32[1,2048]{1,0:T(1,128)S(1)} custom-call(s32[8,8]{1,0:T(8,128)S(1)} %copy-done.7, s32[8]{0:T(128)S(1)} %bitcast.68, bf16[64,2048]{1,0:T(8,128)(2,1)S(1)} %copy-done.2, bf16[64,8192]{1,0:T(8,128)(2,1)S(1)} %copy-done.1, f32[1,8192]{1,0:T(1,128)S(1)} %bitcast.49, f32[1,8192]{1,0:T(1,128)S(1)} %bitcast.59), custom_call_target="tpu_custom_call" | custom-call | tf_op jit(solution)/shard_map/pallas_call | solution.py:287
  43.5 1.5 %collective-permute-start.6 = (f32[2048]{0:T(1024)S(1)}, f32[2048]{0:T(1024)S(1)}, u32[]{:S(2)}, u32[]{:S(2)}) collective-permute-start(f32[2048]{0:T(1024)S(1)} %log_add_fusion.4), channel_id=1, source_target_pairs={{0,2},{1,3},{2,0},{3,1},{4,6},{5,7},{6,4},{7,5},{8,10},{9,11},{10,... | collective-permute-start | bytes 24584 | tf_op jit(solution)/shard_map/ppermute | solution.py:31
  45.0 2.2 %collective-permute-done.6 = f32[2048]{0:T(1024)S(1)} collective-permute-done((f32[2048]{0:T(1024)S(1)}, f32[2048]{0:T(1024)S(1)}, u32[]{:S(2)}, u32[]{:S(2)}) %collective-permute-start.6) | collective-permute-done | bytes 8224 | tf_op jit(solution)/shard_map/ppermute | solution.py:31
  47.2 5.7 %shard_map.97 = f32[1,8192]{1,0:T(1,128)S(1)} custom-call(s32[8,8]{1,0:T(8,128)S(1)} %copy-done.7, s32[8]{0:T(128)S(1)} %bitcast.69, bf16[64,2048]{1,0:T(8,128)(2,1)S(1)} %copy-done.2, f32[1,2048]{1,0:T(1,128)S(1)} %bitcast.64, bf16[80,8192]{1,0:T(8,128)(2,1)S(1)} %pad_maximum_fusion.tgt_ref, f32[1,8192]{1,0:T(1,128)S(1)} %bitcast.50), custom_call_target="tpu_custom_call" | custom-call | tf_op jit(solution)/shard_map/pallas_call | solution.py:287
  53.4 3.5 %collective-permute-done.7 = f32[8192]{0:T(1024)S(1)} collective-permute-done((f32[8192]{0:T(1024)S(1)}, f32[8192]{0:T(1024)S(1)}, u32[]{:S(2)}, u32[]{:S(2)}) %collective-permute-start.7) | collective-permute-done | bytes 32800 | tf_op jit(solution)/shard_map/ppermute | solution.py:31
  56.9 2.0 %collective-permute-start.8 = (f32[8192]{0:T(1024)S(1)}, f32[8192]{0:T(1024)S(1)}, u32[]{:S(2)}, u32[]{:S(2)}) collective-permute-start(f32[8192]{0:T(1024)S(1)} %log_add_fusion.1), channel_id=1, source_target_pairs={{0,8},{4,12},{8,0},{12,4},{16,24},{20,28},{24,16},{28,20},{1,9},{5... | collective-permute-start | bytes 98312 | tf_op jit(solution)/shard_map/ppermute | solution.py:31
  58.9 2.0 %collective-permute-done.8 = f32[8192]{0:T(1024)S(1)} collective-permute-done((f32[8192]{0:T(1024)S(1)}, f32[8192]{0:T(1024)S(1)}, u32[]{:S(2)}, u32[]{:S(2)}) %collective-permute-start.8) | collective-permute-done | bytes 32800 | tf_op jit(solution)/shard_map/ppermute | solution.py:31
  60.9 3.9 %collective-permute-start.9 = (f32[8192]{0:T(1024)S(1)}, f32[8192]{0:T(1024)}, u32[]{:S(2)}, u32[]{:S(2)}) collective-permute-start(f32[8192]{0:T(1024)S(1)} %log_add_fusion), channel_id=1, source_target_pairs={{0,16},{4,20},{8,24},{12,28},{16,0},{20,4},{24,8},{28,12},{1,17},{... | collective-permute-start | bytes 98312 | tf_op jit(solution)/shard_map/ppermute | solution.py:31
  64.9 2.0 %collective-permute-done.9 = f32[8192]{0:T(1024)} collective-permute-done((f32[8192]{0:T(1024)S(1)}, f32[8192]{0:T(1024)}, u32[]{:S(2)}, u32[]{:S(2)}) %collective-permute-start.9) | collective-permute-done | bytes 32800 | tf_op jit(solution)/shard_map/ppermute | solution.py:31
  67.7 9.8 %shard_map.98 = (f32[2,2048]{1,0:T(2,128)S(1)}, f32[2048,128]{1,0:T(8,128)S(1)}) custom-call(s32[8,8]{1,0:T(8,128)S(1)} %copy-done.8, s32[8]{0:T(128)S(1)} %bitcast.70, bf16[64,2048]{1,0:T(8,128)(2,1)S(1)} %copy-done.3, bf16[64,8192]{1,0:T(8,128)(2,1)S(1)} %copy-done.1, f32[1,8192]{1,0:T(1,128)S(1)} %bitcast.51, f32[1,8192]{1,0:T(1,128)S(1)} %bitcast.54, ...), custom_call_target="tpu_custom_call" | custom-call | tf_op jit(solution)/shard_map/pallas_call | solution.py:287
  81.8 1.4 %fusion = f32[2,512,128]{2,1,0:T(8,128)S(1)} fusion(f32[2,512,128]{2,1,0:T(8,128)S(1)} %collective-permute-done.11, f32[2,2,512,128]{3,2,1,0:T(8,128)} %bitcast.53, s32[]{:T(128)S(6)} %select_n.43, f32[2,512]{1,0:T(2,128)S(1)} %get-tuple-element.15, f32[2,512]{1,0:T(2,128)S(1)} %get-tuple-element.14), kind=kLoop, calls=%fused_computation.3 | loop fusion | flops 393216 | bytes 1581060 | tf_op jit(solution)/shard_map/add | solution.py:62
  84.1 7.8 %collective-permute-done.13 = f32[1,512,128]{2,1,0:T(8,128)S(1)} collective-permute-done((f32[1,512,128]{2,1,0:T(8,128)S(1)}, f32[1,512,128]{2,1,0:T(8,128)S(1)}, u32[]{:S(2)}, u32[]{:S(2)}) %collective-permute-start.13) | collective-permute-done | bytes 262176 | tf_op jit(solution)/shard_map/ppermute | solution.py:58
  (66 shorter events, 12.6 us)
Async XLA Ops:
  2.1 15.3 %copy-start.13 = (f32[2048]{0:T(1024)S(1)}, f32[2048]{0:T(1024)}, u32[]{:S(2)}) copy-start(f32[2048]{0:T(1024)} %param.10) | copy-start | bytes 24580
  2.2 1.2 %copy-start = (bf16[64,8192]{1,0:T(8,128)(2,1)S(1)}, bf16[64,8192]{1,0:T(8,128)(2,1)}, u32[]{:S(2)}) copy-start(bf16[64,8192]{1,0:T(8,128)(2,1)} %tgt_ref.5) | copy-start | bytes 3145732
  11.5 1.2 %collective-permute-start = (f32[2048]{0:T(1024)S(1)}, f32[2048]{0:T(1024)S(1)}, u32[]{:S(2)}, u32[]{:S(2)}) collective-permute-start(f32[2048]{0:T(1024)S(1)} %bitcast.60), channel_id=1, source_target_pairs={{0,1},{1,0},{2,3},{3,2},{4,5},{5,4},{6,7},{7,6},{8,9},{9,8},{10,11... | collective-permute-start | bytes 24584 | tf_op jit(solution)/shard_map/ppermute | solution.py:31
  12.8 23.5 %copy-start.12 = (f32[8192]{0:T(1024)S(1)}, f32[8192]{0:T(1024)}, u32[]{:S(2)}) copy-start(f32[8192]{0:T(1024)} %param.11) | copy-start | bytes 98308
  12.8 23.6 %copy-start.1 = (bf16[64,8192]{1,0:T(8,128)(2,1)S(1)}, bf16[64,8192]{1,0:T(8,128)(2,1)}, u32[]{:S(2)}) copy-start(bf16[64,8192]{1,0:T(8,128)(2,1)} %tgt_ref.5) | copy-start | bytes 3145732
  12.8 4.6 %collective-permute-start.1 = (f32[2048]{0:T(1024)S(1)}, f32[2048]{0:T(1024)S(1)}, u32[]{:S(2)}, u32[]{:S(2)}) collective-permute-start(f32[2048]{0:T(1024)S(1)} %log_add_fusion.5), channel_id=1, source_target_pairs={{0,2},{1,3},{2,0},{3,1},{4,6},{5,7},{6,4},{7,5},{8,10},{9,11},{10,... | collective-permute-start | bytes 24584 | tf_op jit(solution)/shard_map/ppermute | solution.py:31
  22.9 44.7 %copy-start.3 = (bf16[64,2048]{1,0:T(8,128)(2,1)S(1)}, bf16[64,2048]{1,0:T(8,128)(2,1)}, u32[]{:S(2)}) copy-start(bf16[64,2048]{1,0:T(8,128)(2,1)} %src_ref.9) | copy-start | bytes 786436
  22.9 44.7 %copy-start.4 = (bf16[128,8192]{1,0:T(8,128)(2,1)S(1)}, bf16[128,8192]{1,0:T(8,128)(2,1)}, u32[]{:S(2)}) copy-start(bf16[128,8192]{1,0:T(8,128)(2,1)} %feat_ref.1) | copy-start | bytes 6291460
  22.9 44.7 %copy-start.8 = (s32[8,8]{1,0:T(8,128)S(1)}, s32[8,8]{1,0:T(8,128)}, u32[]{:S(2)}) copy-start(s32[8,8]{1,0:T(8,128)} %blocks_ref.9) | copy-start | bytes 772
  23.0 44.7 %copy-start.11 = (s32[8,1]{0,1:T(1,128)S(1)}, s32[8,1]{0,1:T(1,128)}, u32[]{:S(2)}) copy-start(s32[8,1]{0,1:T(1,128)} %param.13) | copy-start | bytes 100
  23.0 4.0 %collective-permute-start.2 = (f32[8192]{0:T(1024)S(1)}, f32[8192]{0:T(1024)S(1)}, u32[]{:S(2)}, u32[]{:S(2)}) collective-permute-start(f32[8192]{0:T(1024)S(1)} %bitcast.55), channel_id=1, source_target_pairs={{0,4},{4,0},{8,12},{12,8},{16,20},{20,16},{24,28},{28,24},{1,5},{5... | collective-permute-start | bytes 98312 | tf_op jit(solution)/shard_map/ppermute | solution.py:31
  27.0 4.0 %collective-permute-start.3 = (f32[8192]{0:T(1024)S(1)}, f32[8192]{0:T(1024)S(1)}, u32[]{:S(2)}, u32[]{:S(2)}) collective-permute-start(f32[8192]{0:T(1024)S(1)} %log_add_fusion.3), channel_id=1, source_target_pairs={{0,8},{4,12},{8,0},{12,4},{16,24},{20,28},{24,16},{28,20},{1,9},{5... | collective-permute-start | bytes 98312 | tf_op jit(solution)/shard_map/ppermute | solution.py:31
  31.0 5.3 %collective-permute-start.4 = (f32[8192]{0:T(1024)S(1)}, f32[8192]{0:T(1024)S(1)}, u32[]{:S(2)}, u32[]{:S(2)}) collective-permute-start(f32[8192]{0:T(1024)S(1)} %log_add_fusion.2), channel_id=1, source_target_pairs={{0,16},{4,20},{8,24},{12,28},{16,0},{20,4},{24,8},{28,12},{1,17},{... | collective-permute-start | bytes 98312 | tf_op jit(solution)/shard_map/ppermute | solution.py:31
  42.2 1.2 %collective-permute-start.5 = (f32[2048]{0:T(1024)S(1)}, f32[2048]{0:T(1024)S(1)}, u32[]{:S(2)}, u32[]{:S(2)}) collective-permute-start(f32[2048]{0:T(1024)S(1)} %bitcast.62), channel_id=1, source_target_pairs={{0,1},{1,0},{2,3},{3,2},{4,5},{5,4},{6,7},{7,6},{8,9},{9,8},{10,11... | collective-permute-start | bytes 24584 | tf_op jit(solution)/shard_map/ppermute | solution.py:31
  43.5 3.7 %collective-permute-start.6 = (f32[2048]{0:T(1024)S(1)}, f32[2048]{0:T(1024)S(1)}, u32[]{:S(2)}, u32[]{:S(2)}) collective-permute-start(f32[2048]{0:T(1024)S(1)} %log_add_fusion.4), channel_id=1, source_target_pairs={{0,2},{1,3},{2,0},{3,1},{4,6},{5,7},{6,4},{7,5},{8,10},{9,11},{10,... | collective-permute-start | bytes 24584 | tf_op jit(solution)/shard_map/ppermute | solution.py:31
  47.2 30.3 %copy-start.9 = (f32[2048]{0:T(1024)}, f32[2048]{0:T(1024)S(1)}, u32[]{:S(2)}) copy-start(f32[2048]{0:T(1024)S(1)} %multiply_subtract_fusion.2) | copy-start | bytes 24580
  52.9 4.0 %collective-permute-start.7 = (f32[8192]{0:T(1024)S(1)}, f32[8192]{0:T(1024)S(1)}, u32[]{:S(2)}, u32[]{:S(2)}) collective-permute-start(f32[8192]{0:T(1024)S(1)} %bitcast.57), channel_id=1, source_target_pairs={{0,4},{4,0},{8,12},{12,8},{16,20},{20,16},{24,28},{28,24},{1,5},{5... | collective-permute-start | bytes 98312 | tf_op jit(solution)/shard_map/ppermute | solution.py:31
  56.9 4.0 %collective-permute-start.8 = (f32[8192]{0:T(1024)S(1)}, f32[8192]{0:T(1024)S(1)}, u32[]{:S(2)}, u32[]{:S(2)}) collective-permute-start(f32[8192]{0:T(1024)S(1)} %log_add_fusion.1), channel_id=1, source_target_pairs={{0,8},{4,12},{8,0},{12,4},{16,24},{20,28},{24,16},{28,20},{1,9},{5... | collective-permute-start | bytes 98312 | tf_op jit(solution)/shard_map/ppermute | solution.py:31
  60.9 5.9 %collective-permute-start.9 = (f32[8192]{0:T(1024)S(1)}, f32[8192]{0:T(1024)}, u32[]{:S(2)}, u32[]{:S(2)}) collective-permute-start(f32[8192]{0:T(1024)S(1)} %log_add_fusion), channel_id=1, source_target_pairs={{0,16},{4,20},{8,24},{12,28},{16,0},{20,4},{24,8},{28,12},{1,17},{... | collective-permute-start | bytes 98312 | tf_op jit(solution)/shard_map/ppermute | solution.py:31
  67.7 12.1 %copy-start.6 = (f32[8192]{0:T(1024)}, f32[8192]{0:T(1024)S(1)}, u32[]{:S(2)}) copy-start(f32[8192]{0:T(1024)S(1)} %multiply_subtract_fusion) | copy-start | bytes 98308
  78.6 1.7 %collective-permute-start.10 = (f32[2,2,512]{2,1,0:T(2,128)S(1)}, f32[2,2,512]{2,1,0:T(2,128)S(1)}, u32[]{:S(2)}, u32[]{:S(2)}) collective-permute-start(f32[2,2,512]{2,1,0:T(2,128)S(1)} %bitcast.71), channel_id=1, source_target_pairs={{0,1},{1,0},{2,3},{3,2},{4,5},{5,4},{6,7},{7,6},{8,9},{9,8},{10,11... | collective-permute-start | bytes 24584 | tf_op jit(solution)/shard_map/ppermute | solution.py:57
  79.8 2.1 %collective-permute-start.11 = (f32[2,512,128]{2,1,0:T(8,128)S(1)}, f32[2,512,128]{2,1,0:T(8,128)S(1)}, u32[]{:S(2)}, u32[]{:S(2)}) collective-permute-start(f32[2,512,128]{2,1,0:T(8,128)S(1)} %dynamic-slice_bitcast_fusion), channel_id=1, source_target_pairs={{0,1},{1,0},{2,3},{3,2},{4,5},{5,4},{6,7},{7,6},{8,9},{9,8},{10,11... | collective-permute-start | bytes 1572872 | tf_op jit(solution)/shard_map/ppermute | solution.py:58
  80.4 3.7 %collective-permute-start.12 = (f32[2,1,512]{2,1,0:T(1,128)S(1)}, f32[2,1,512]{2,1,0:T(1,128)S(1)}, u32[]{:S(2)}, u32[]{:S(2)}) collective-permute-start(f32[2,1,512]{2,1,0:T(1,128)S(1)} %get-tuple-element.17), channel_id=1, source_target_pairs={{0,2},{1,3},{2,0},{3,1},{4,6},{5,7},{6,4},{7,5},{8,10},{9,11},{10,... | collective-permute-start | bytes 12296 | tf_op jit(solution)/shard_map/ppermute | solution.py:57
  83.3 8.7 %collective-permute-start.13 = (f32[1,512,128]{2,1,0:T(8,128)S(1)}, f32[1,512,128]{2,1,0:T(8,128)S(1)}, u32[]{:S(2)}, u32[]{:S(2)}) collective-permute-start(f32[1,512,128]{2,1,0:T(8,128)S(1)} %constant_dynamic-slice_fusion.1), channel_id=1, source_target_pairs={{0,2},{1,3},{2,0},{3,1},{4,6},{5,7},{6,4},{7,5},{8,10},{9,11},{10,... | collective-permute-start | bytes 786440 | tf_op jit(solution)/shard_map/ppermute | solution.py:58
  (4 other events, 3.3 us)

commit v2 on v1

--- a/solution.py
+++ b/solution.py
@@ -60,9 +60,11 @@
         mine = jnp.exp(small_keep[0] - overall)
         theirs = jnp.exp(small_other[0] - overall)
         numerator = num_keep * mine[..., None] + num_other * theirs[..., None]
-        small = jnp.stack([overall, small_keep[1] * mine + small_other[1] * theirs])
+        denominator = small_keep[1] * mine + small_other[1] * theirs
         step *= 2
-    return (numerator.reshape(rows, -1), small[1].reshape(rows))
+        if step < size:
+            small = jnp.stack([overall, denominator])
+    return (numerator / denominator[..., None]).reshape(rows, -1)
 
 
 CHUNK = 64
@@ -353,8 +355,7 @@
     small, numerator = project_pass(
         kept_blocks, counts, src_t, tgt_emb, tnorm, tpot, target_features
     )
-    numerator, denominator = halving_merge(small, numerator, "tgt")
-    projected = numerator / denominator[:, None]
+    projected = halving_merge(small, numerator, "tgt")
     return (projected, src_potential, tgt_potential)
 
 

time: 93.5 us -> 94.4 us (level)
  starting transfers between devices: 19.3 us -> 26.3 us
  waiting for transfers between devices: 29 us -> 25 us
  Pallas kernels: 32.7 us -> 31 us
    ppermute x10, starting transfers between devices: 17.6 us -> 21 us  [butterfly_lse(): value = lse_pair(value, lax.ppermute(value, axis, pairs))]
    ppermute x2, starting transfers between devices: 0.4 us -> 3.31 us  [halving_merge(): small_other = lax.ppermute(small_send, axis, pairs)]
    ppermute x2, waiting for transfers between devices: 8.94 us -> 6.81 us  [halving_merge(): num_other = lax.ppermute(num_send, axis, pairs)]
    ppermute x10, waiting for transfers between devices: 20 us -> 18.1 us  [butterfly_lse(): value = lse_pair(value, lax.ppermute(value, axis, pairs))]
    pallas_call x5, Pallas kernels: 32.7 us -> 31 us  [local_call(): pl.pallas_call(kernel, grid_spec=spec, out_shape=outs, compiler_params=pl...]
    div x1 -> x0, other arithmetic: 0.97 us -> none  [shards(): projected = numerator / denominator[:, None]]
    reshape x0 -> x1, other arithmetic: none -> 0.97 us  [halving_merge(): return (numerator / denominator[..., None]).reshape(rows, -1)]
  transfers between devices with their start and end apart: 14 -> 14, of which waited for: 13 -> 11; matrix products, arithmetic and copies ran while one was open for 3% -> 3% of each run, Pallas kernels for 0% -> 0%
where the time goes in v2:
time: 94.4 us; the launch traced here: 94.2 us
  Pallas kernels  31 us (33%)
  starting transfers between devices  26.3 us (28%)
  waiting for transfers between devices  25 us (26%)
  local copies, waits for them, and re-layouts  5.8 us (6%)
  other arithmetic  5.19 us (5%)
  between operations  0.97 us (1%)
    pallas_call x5, Pallas kernels, local_call(): pl.pallas_call(kernel, grid_spec=spec, out_shape=outs, compiler_params=pl...  31 us
    ppermute x10, starting transfers between devices, butterfly_lse(): value = lse_pair(value, lax.ppermute(value, axis, pairs))  21 us
    ppermute x10, waiting for transfers between devices, butterfly_lse(): value = lse_pair(value, lax.ppermute(value, axis, pairs))  18.1 us
    ppermute x2, waiting for transfers between devices, halving_merge(): num_other = lax.ppermute(num_send, axis, pairs)  6.81 us
    unnamed x29, local copies, waits for them, and re-layouts  4.54 us
    ppermute x2, starting transfers between devices, halving_merge(): small_other = lax.ppermute(small_send, axis, pairs)  3.31 us
    ppermute x2, starting transfers between devices, halving_merge(): num_other = lax.ppermute(num_send, axis, pairs)  1.98 us
  transfers between devices with their start and end apart: 14, of which 11 were waited for; matrix products, arithmetic and copies ran while one was open for 3% of the time, Pallas kernels for 0%

profile of v2, /device:TPU:0, one launch (start us, length us, event | category | flops | bytes accessed | tf_op | source)
XLA Modules:
  0.0 94.2 jit_solution(8802493958771899757)
XLA Ops:
  0.6 1.5 %multiply_reduce_fusion = f32[8192]{0:T(1024)S(1)} fusion(bf16[64,8192]{1,0:T(8,128)(2,1)} %tgt_ref.5), kind=kLoop, calls=%fused_computation | loop fusion | flops 1564672 | bytes 1081344 | tf_op jit(solution)/shard_map/reduce_sum | solution.py:335
  5.7 5.5 %shard_map.94 = f32[1,2048]{1,0:T(1,128)S(1)} custom-call(s32[8,8]{1,0:T(8,128)S(1)} %copy-done.7, s32[8]{0:T(128)S(1)} %bitcast.66, bf16[64,2048]{1,0:T(8,128)(2,1)S(1)} %copy-done.2, bf16[64,8192]{1,0:T(8,128)(2,1)S(1)} %copy-done, f32[1,8192]{1,0:T(1,128)S(1)} %bitcast.47, f32[1,8192]{1,0:T(1,128)S(1)} %reshape.179.tpot_ref), custom_call_target="tpu_custom_call" | custom-call | tf_op jit(solution)/shard_map/pallas_call | solution.py:289
  12.5 3.5 %collective-permute-start.1 = (f32[2048]{0:T(1024)S(1)}, f32[2048]{0:T(1024)S(1)}, u32[]{:S(2)}, u32[]{:S(2)}) collective-permute-start(f32[2048]{0:T(1024)S(1)} %log_add_fusion.5), channel_id=1, source_target_pairs={{0,2},{1,3},{2,0},{3,1},{4,6},{5,7},{6,4},{7,5},{8,10},{9,11},{10,... | collective-permute-start | bytes 24584 | tf_op jit(solution)/shard_map/ppermute | solution.py:31
  17.7 5.2 %shard_map.95 = f32[1,8192]{1,0:T(1,128)S(1)} custom-call(s32[8,8]{1,0:T(8,128)S(1)} %copy-done.7, s32[8]{0:T(128)S(1)} %bitcast.67, bf16[64,2048]{1,0:T(8,128)(2,1)S(1)} %copy-done.2, f32[1,2048]{1,0:T(1,128)S(1)} %bitcast.65, bf16[80,8192]{1,0:T(8,128)(2,1)S(1)} %pad_maximum_fusion.tgt_ref, f32[1,8192]{1,0:T(1,128)S(1)} %bitcast.48), custom_call_target="tpu_custom_call" | custom-call | tf_op jit(solution)/shard_map/pallas_call | solution.py:289
  23.0 1.7 %collective-permute-start.2 = (f32[8192]{0:T(1024)S(1)}, f32[8192]{0:T(1024)S(1)}, u32[]{:S(2)}, u32[]{:S(2)}) collective-permute-start(f32[8192]{0:T(1024)S(1)} %bitcast.55), channel_id=1, source_target_pairs={{0,4},{4,0},{8,12},{12,8},{16,20},{20,16},{24,28},{28,24},{1,5},{5... | collective-permute-start | bytes 98312 | tf_op jit(solution)/shard_map/ppermute | solution.py:31
  24.7 2.2 %collective-permute-done.2 = f32[8192]{0:T(1024)S(1)} collective-permute-done((f32[8192]{0:T(1024)S(1)}, f32[8192]{0:T(1024)S(1)}, u32[]{:S(2)}, u32[]{:S(2)}) %collective-permute-start.2) | collective-permute-done | bytes 32800 | tf_op jit(solution)/shard_map/ppermute | solution.py:31
  27.0 1.7 %collective-permute-start.3 = (f32[8192]{0:T(1024)S(1)}, f32[8192]{0:T(1024)S(1)}, u32[]{:S(2)}, u32[]{:S(2)}) collective-permute-start(f32[8192]{0:T(1024)S(1)} %log_add_fusion.3), channel_id=1, source_target_pairs={{0,8},{4,12},{8,0},{12,4},{16,24},{20,28},{24,16},{28,20},{1,9},{5... | collective-permute-start | bytes 98312 | tf_op jit(solution)/shard_map/ppermute | solution.py:31
  28.7 2.3 %collective-permute-done.3 = f32[8192]{0:T(1024)S(1)} collective-permute-done((f32[8192]{0:T(1024)S(1)}, f32[8192]{0:T(1024)S(1)}, u32[]{:S(2)}, u32[]{:S(2)}) %collective-permute-start.3) | collective-permute-done | bytes 32800 | tf_op jit(solution)/shard_map/ppermute | solution.py:31
  31.0 3.8 %collective-permute-start.4 = (f32[8192]{0:T(1024)S(1)}, f32[8192]{0:T(1024)S(1)}, u32[]{:S(2)}, u32[]{:S(2)}) collective-permute-start(f32[8192]{0:T(1024)S(1)} %log_add_fusion.2), channel_id=1, source_target_pairs={{0,16},{4,20},{8,24},{12,28},{16,0},{20,4},{24,8},{28,12},{1,17},{... | collective-permute-start | bytes 98312 | tf_op jit(solution)/shard_map/ppermute | solution.py:31
  34.8 1.9 %collective-permute-done.4 = f32[8192]{0:T(1024)S(1)} collective-permute-done((f32[8192]{0:T(1024)S(1)}, f32[8192]{0:T(1024)S(1)}, u32[]{:S(2)}, u32[]{:S(2)}) %collective-permute-start.4) | collective-permute-done | bytes 32800 | tf_op jit(solution)/shard_map/ppermute | solution.py:31
  36.8 5.5 %shard_map.96 = f32[1,2048]{1,0:T(1,128)S(1)} custom-call(s32[8,8]{1,0:T(8,128)S(1)} %copy-done.7, s32[8]{0:T(128)S(1)} %bitcast.68, bf16[64,2048]{1,0:T(8,128)(2,1)S(1)} %copy-done.2, bf16[64,8192]{1,0:T(8,128)(2,1)S(1)} %copy-done.1, f32[1,8192]{1,0:T(1,128)S(1)} %bitcast.49, f32[1,8192]{1,0:T(1,128)S(1)} %bitcast.59), custom_call_target="tpu_custom_call" | custom-call | tf_op jit(solution)/shard_map/pallas_call | solution.py:289
  43.6 2.5 %collective-permute-start.6 = (f32[2048]{0:T(1024)S(1)}, f32[2048]{0:T(1024)S(1)}, u32[]{:S(2)}, u32[]{:S(2)}) collective-permute-start(f32[2048]{0:T(1024)S(1)} %log_add_fusion.4), channel_id=1, source_target_pairs={{0,2},{1,3},{2,0},{3,1},{4,6},{5,7},{6,4},{7,5},{8,10},{9,11},{10,... | collective-permute-start | bytes 24584 | tf_op jit(solution)/shard_map/ppermute | solution.py:31
  46.1 1.6 %collective-permute-done.6 = f32[2048]{0:T(1024)S(1)} collective-permute-done((f32[2048]{0:T(1024)S(1)}, f32[2048]{0:T(1024)S(1)}, u32[]{:S(2)}, u32[]{:S(2)}) %collective-permute-start.6) | collective-permute-done | bytes 8224 | tf_op jit(solution)/shard_map/ppermute | solution.py:31
  47.8 5.4 %shard_map.97 = f32[1,8192]{1,0:T(1,128)S(1)} custom-call(s32[8,8]{1,0:T(8,128)S(1)} %copy-done.7, s32[8]{0:T(128)S(1)} %bitcast.69, bf16[64,2048]{1,0:T(8,128)(2,1)S(1)} %copy-done.2, f32[1,2048]{1,0:T(1,128)S(1)} %bitcast.64, bf16[80,8192]{1,0:T(8,128)(2,1)S(1)} %pad_maximum_fusion.tgt_ref, f32[1,8192]{1,0:T(1,128)S(1)} %bitcast.50), custom_call_target="tpu_custom_call" | custom-call | tf_op jit(solution)/shard_map/pallas_call | solution.py:289
  53.2 1.7 %collective-permute-start.7 = (f32[8192]{0:T(1024)S(1)}, f32[8192]{0:T(1024)S(1)}, u32[]{:S(2)}, u32[]{:S(2)}) collective-permute-start(f32[8192]{0:T(1024)S(1)} %bitcast.57), channel_id=1, source_target_pairs={{0,4},{4,0},{8,12},{12,8},{16,20},{20,16},{24,28},{28,24},{1,5},{5... | collective-permute-start | bytes 98312 | tf_op jit(solution)/shard_map/ppermute | solution.py:31
  54.9 2.2 %collective-permute-done.7 = f32[8192]{0:T(1024)S(1)} collective-permute-done((f32[8192]{0:T(1024)S(1)}, f32[8192]{0:T(1024)S(1)}, u32[]{:S(2)}, u32[]{:S(2)}) %collective-permute-start.7) | collective-permute-done | bytes 32800 | tf_op jit(solution)/shard_map/ppermute | solution.py:31
  57.2 1.8 %collective-permute-start.8 = (f32[8192]{0:T(1024)S(1)}, f32[8192]{0:T(1024)S(1)}, u32[]{:S(2)}, u32[]{:S(2)}) collective-permute-start(f32[8192]{0:T(1024)S(1)} %log_add_fusion.1), channel_id=1, source_target_pairs={{0,8},{4,12},{8,0},{12,4},{16,24},{20,28},{24,16},{28,20},{1,9},{5... | collective-permute-start | bytes 98312 | tf_op jit(solution)/shard_map/ppermute | solution.py:31
  59.0 2.2 %collective-permute-done.8 = f32[8192]{0:T(1024)S(1)} collective-permute-done((f32[8192]{0:T(1024)S(1)}, f32[8192]{0:T(1024)S(1)}, u32[]{:S(2)}, u32[]{:S(2)}) %collective-permute-start.8) | collective-permute-done | bytes 32800 | tf_op jit(solution)/shard_map/ppermute | solution.py:31
  61.2 4.1 %collective-permute-start.9 = (f32[8192]{0:T(1024)S(1)}, f32[8192]{0:T(1024)}, u32[]{:S(2)}, u32[]{:S(2)}) collective-permute-start(f32[8192]{0:T(1024)S(1)} %log_add_fusion), channel_id=1, source_target_pairs={{0,16},{4,20},{8,24},{12,28},{16,0},{20,4},{24,8},{28,12},{1,17},{... | collective-permute-start | bytes 98312 | tf_op jit(solution)/shard_map/ppermute | solution.py:31
  65.3 2.0 %collective-permute-done.9 = f32[8192]{0:T(1024)} collective-permute-done((f32[8192]{0:T(1024)S(1)}, f32[8192]{0:T(1024)}, u32[]{:S(2)}, u32[]{:S(2)}) %collective-permute-start.9) | collective-permute-done | bytes 32800 | tf_op jit(solution)/shard_map/ppermute | solution.py:31
  68.2 9.2 %shard_map.98 = (f32[2,2048]{1,0:T(2,128)S(1)}, f32[2048,128]{1,0:T(8,128)S(1)}) custom-call(s32[8,8]{1,0:T(8,128)S(1)} %copy-done.8, s32[8]{0:T(128)S(1)} %bitcast.70, bf16[64,2048]{1,0:T(8,128)(2,1)S(1)} %copy-done.3, bf16[64,8192]{1,0:T(8,128)(2,1)S(1)} %copy-done.1, f32[1,8192]{1,0:T(1,128)S(1)} %bitcast.51, f32[1,8192]{1,0:T(1,128)S(1)} %bitcast.54, ...), custom_call_target="tpu_custom_call" | custom-call | tf_op jit(solution)/shard_map/pallas_call | solution.py:289
  80.3 3.2 %collective-permute-start.12 = (f32[2,1,512]{2,1,0:T(1,128)S(1)}, f32[2,1,512]{2,1,0:T(1,128)S(1)}, u32[]{:S(2)}, u32[]{:S(2)}) collective-permute-start(f32[2,1,512]{2,1,0:T(1,128)S(1)} %get-tuple-element.17), channel_id=1, source_target_pairs={{0,2},{1,3},{2,0},{3,1},{4,6},{5,7},{6,4},{7,5},{8,10},{9,11},{10,... | collective-permute-start | bytes 12296 | tf_op jit(solution)/shard_map/ppermute | solution.py:57
  85.0 1.4 %collective-permute-start.13 = (f32[1,512,128]{2,1,0:T(8,128)S(1)}, f32[1,512,128]{2,1,0:T(8,128)S(1)}, u32[]{:S(2)}, u32[]{:S(2)}) collective-permute-start(f32[1,512,128]{2,1,0:T(8,128)S(1)} %constant_dynamic-slice_fusion.1), channel_id=1, source_target_pairs={{0,2},{1,3},{2,0},{3,1},{4,6},{5,7},{6,4},{7,5},{8,10},{9,11},{10,... | collective-permute-start | bytes 786440 | tf_op jit(solution)/shard_map/ppermute | solution.py:58
  86.4 6.8 %collective-permute-done.13 = f32[1,512,128]{2,1,0:T(8,128)S(1)} collective-permute-done((f32[1,512,128]{2,1,0:T(8,128)S(1)}, f32[1,512,128]{2,1,0:T(8,128)S(1)}, u32[]{:S(2)}, u32[]{:S(2)}) %collective-permute-start.13) | collective-permute-done | bytes 262176 | tf_op jit(solution)/shard_map/ppermute | solution.py:58
  (66 shorter events, 13.9 us)
Async XLA Ops:
  2.1 15.6 %copy-start.13 = (f32[2048]{0:T(1024)S(1)}, f32[2048]{0:T(1024)}, u32[]{:S(2)}) copy-start(f32[2048]{0:T(1024)} %param.10) | copy-start | bytes 24580
  2.2 1.2 %copy-start = (bf16[64,8192]{1,0:T(8,128)(2,1)S(1)}, bf16[64,8192]{1,0:T(8,128)(2,1)}, u32[]{:S(2)}) copy-start(bf16[64,8192]{1,0:T(8,128)(2,1)} %tgt_ref.5) | copy-start | bytes 3145732
  11.2 1.2 %collective-permute-start = (f32[2048]{0:T(1024)S(1)}, f32[2048]{0:T(1024)S(1)}, u32[]{:S(2)}, u32[]{:S(2)}) collective-permute-start(f32[2048]{0:T(1024)S(1)} %bitcast.60), channel_id=1, source_target_pairs={{0,1},{1,0},{2,3},{3,2},{4,5},{5,4},{6,7},{7,6},{8,9},{9,8},{10,11... | collective-permute-start | bytes 24584 | tf_op jit(solution)/shard_map/ppermute | solution.py:31
  12.5 24.2 %copy-start.12 = (f32[8192]{0:T(1024)S(1)}, f32[8192]{0:T(1024)}, u32[]{:S(2)}) copy-start(f32[8192]{0:T(1024)} %param.11) | copy-start | bytes 98308
  12.5 24.3 %copy-start.1 = (bf16[64,8192]{1,0:T(8,128)(2,1)S(1)}, bf16[64,8192]{1,0:T(8,128)(2,1)}, u32[]{:S(2)}) copy-start(bf16[64,8192]{1,0:T(8,128)(2,1)} %tgt_ref.5) | copy-start | bytes 3145732
  12.5 5.2 %collective-permute-start.1 = (f32[2048]{0:T(1024)S(1)}, f32[2048]{0:T(1024)S(1)}, u32[]{:S(2)}, u32[]{:S(2)}) collective-permute-start(f32[2048]{0:T(1024)S(1)} %log_add_fusion.5), channel_id=1, source_target_pairs={{0,2},{1,3},{2,0},{3,1},{4,6},{5,7},{6,4},{7,5},{8,10},{9,11},{10,... | collective-permute-start | bytes 24584 | tf_op jit(solution)/shard_map/ppermute | solution.py:31
  22.9 45.2 %copy-start.3 = (bf16[64,2048]{1,0:T(8,128)(2,1)S(1)}, bf16[64,2048]{1,0:T(8,128)(2,1)}, u32[]{:S(2)}) copy-start(bf16[64,2048]{1,0:T(8,128)(2,1)} %src_ref.9) | copy-start | bytes 786436
  23.0 45.2 %copy-start.4 = (bf16[128,8192]{1,0:T(8,128)(2,1)S(1)}, bf16[128,8192]{1,0:T(8,128)(2,1)}, u32[]{:S(2)}) copy-start(bf16[128,8192]{1,0:T(8,128)(2,1)} %feat_ref.1) | copy-start | bytes 6291460
  23.0 45.2 %copy-start.8 = (s32[8,8]{1,0:T(8,128)S(1)}, s32[8,8]{1,0:T(8,128)}, u32[]{:S(2)}) copy-start(s32[8,8]{1,0:T(8,128)} %blocks_ref.9) | copy-start | bytes 772
  23.0 45.2 %copy-start.11 = (s32[8,1]{0,1:T(1,128)S(1)}, s32[8,1]{0,1:T(1,128)}, u32[]{:S(2)}) copy-start(s32[8,1]{0,1:T(1,128)} %param.13) | copy-start | bytes 100
  23.0 4.0 %collective-permute-start.2 = (f32[8192]{0:T(1024)S(1)}, f32[8192]{0:T(1024)S(1)}, u32[]{:S(2)}, u32[]{:S(2)}) collective-permute-start(f32[8192]{0:T(1024)S(1)} %bitcast.55), channel_id=1, source_target_pairs={{0,4},{4,0},{8,12},{12,8},{16,20},{20,16},{24,28},{28,24},{1,5},{5... | collective-permute-start | bytes 98312 | tf_op jit(solution)/shard_map/ppermute | solution.py:31
  27.0 4.0 %collective-permute-start.3 = (f32[8192]{0:T(1024)S(1)}, f32[8192]{0:T(1024)S(1)}, u32[]{:S(2)}, u32[]{:S(2)}) collective-permute-start(f32[8192]{0:T(1024)S(1)} %log_add_fusion.3), channel_id=1, source_target_pairs={{0,8},{4,12},{8,0},{12,4},{16,24},{20,28},{24,16},{28,20},{1,9},{5... | collective-permute-start | bytes 98312 | tf_op jit(solution)/shard_map/ppermute | solution.py:31
  31.0 5.7 %collective-permute-start.4 = (f32[8192]{0:T(1024)S(1)}, f32[8192]{0:T(1024)S(1)}, u32[]{:S(2)}, u32[]{:S(2)}) collective-permute-start(f32[8192]{0:T(1024)S(1)} %log_add_fusion.2), channel_id=1, source_target_pairs={{0,16},{4,20},{8,24},{12,28},{16,0},{20,4},{24,8},{28,12},{1,17},{... | collective-permute-start | bytes 98312 | tf_op jit(solution)/shard_map/ppermute | solution.py:31
  42.3 1.2 %collective-permute-start.5 = (f32[2048]{0:T(1024)S(1)}, f32[2048]{0:T(1024)S(1)}, u32[]{:S(2)}, u32[]{:S(2)}) collective-permute-start(f32[2048]{0:T(1024)S(1)} %bitcast.62), channel_id=1, source_target_pairs={{0,1},{1,0},{2,3},{3,2},{4,5},{5,4},{6,7},{7,6},{8,9},{9,8},{10,11... | collective-permute-start | bytes 24584 | tf_op jit(solution)/shard_map/ppermute | solution.py:31
  43.6 4.1 %collective-permute-start.6 = (f32[2048]{0:T(1024)S(1)}, f32[2048]{0:T(1024)S(1)}, u32[]{:S(2)}, u32[]{:S(2)}) collective-permute-start(f32[2048]{0:T(1024)S(1)} %log_add_fusion.4), channel_id=1, source_target_pairs={{0,2},{1,3},{2,0},{3,1},{4,6},{5,7},{6,4},{7,5},{8,10},{9,11},{10,... | collective-permute-start | bytes 24584 | tf_op jit(solution)/shard_map/ppermute | solution.py:31
  47.8 29.7 %copy-start.9 = (f32[2048]{0:T(1024)}, f32[2048]{0:T(1024)S(1)}, u32[]{:S(2)}) copy-start(f32[2048]{0:T(1024)S(1)} %multiply_subtract_fusion.2) | copy-start | bytes 24580
  53.2 4.0 %collective-permute-start.7 = (f32[8192]{0:T(1024)S(1)}, f32[8192]{0:T(1024)S(1)}, u32[]{:S(2)}, u32[]{:S(2)}) collective-permute-start(f32[8192]{0:T(1024)S(1)} %bitcast.57), channel_id=1, source_target_pairs={{0,4},{4,0},{8,12},{12,8},{16,20},{20,16},{24,28},{28,24},{1,5},{5... | collective-permute-start | bytes 98312 | tf_op jit(solution)/shard_map/ppermute | solution.py:31
  57.2 4.0 %collective-permute-start.8 = (f32[8192]{0:T(1024)S(1)}, f32[8192]{0:T(1024)S(1)}, u32[]{:S(2)}, u32[]{:S(2)}) collective-permute-start(f32[8192]{0:T(1024)S(1)} %log_add_fusion.1), channel_id=1, source_target_pairs={{0,8},{4,12},{8,0},{12,4},{16,24},{20,28},{24,16},{28,20},{1,9},{5... | collective-permute-start | bytes 98312 | tf_op jit(solution)/shard_map/ppermute | solution.py:31
  61.2 6.1 %collective-permute-start.9 = (f32[8192]{0:T(1024)S(1)}, f32[8192]{0:T(1024)}, u32[]{:S(2)}, u32[]{:S(2)}) collective-permute-start(f32[8192]{0:T(1024)S(1)} %log_add_fusion), channel_id=1, source_target_pairs={{0,16},{4,20},{8,24},{12,28},{16,0},{20,4},{24,8},{28,12},{1,17},{... | collective-permute-start | bytes 98312 | tf_op jit(solution)/shard_map/ppermute | solution.py:31
  68.1 11.5 %copy-start.6 = (f32[8192]{0:T(1024)}, f32[8192]{0:T(1024)S(1)}, u32[]{:S(2)}) copy-start(f32[8192]{0:T(1024)S(1)} %multiply_subtract_fusion) | copy-start | bytes 98308
  78.5 1.7 %collective-permute-start.10 = (f32[2,2,512]{2,1,0:T(2,128)S(1)}, f32[2,2,512]{2,1,0:T(2,128)S(1)}, u32[]{:S(2)}, u32[]{:S(2)}) collective-permute-start(f32[2,2,512]{2,1,0:T(2,128)S(1)} %bitcast.71), channel_id=1, source_target_pairs={{0,1},{1,0},{2,3},{3,2},{4,5},{5,4},{6,7},{7,6},{8,9},{9,8},{10,11... | collective-permute-start | bytes 24584 | tf_op jit(solution)/shard_map/ppermute | solution.py:57
  79.7 3.9 %collective-permute-start.11 = (f32[2,512,128]{2,1,0:T(8,128)S(1)}, f32[2,512,128]{2,1,0:T(8,128)S(1)}, u32[]{:S(2)}, u32[]{:S(2)}) collective-permute-start(f32[2,512,128]{2,1,0:T(8,128)S(1)} %dynamic-slice_bitcast_fusion), channel_id=1, source_target_pairs={{0,1},{1,0},{2,3},{3,2},{4,5},{5,4},{6,7},{7,6},{8,9},{9,8},{10,11... | collective-permute-start | bytes 1572872 | tf_op jit(solution)/shard_map/ppermute | solution.py:58
  80.3 6.1 %collective-permute-start.12 = (f32[2,1,512]{2,1,0:T(1,128)S(1)}, f32[2,1,512]{2,1,0:T(1,128)S(1)}, u32[]{:S(2)}, u32[]{:S(2)}) collective-permute-start(f32[2,1,512]{2,1,0:T(1,128)S(1)} %get-tuple-element.17), channel_id=1, source_target_pairs={{0,2},{1,3},{2,0},{3,1},{4,6},{5,7},{6,4},{7,5},{8,10},{9,11},{10,... | collective-permute-start | bytes 12296 | tf_op jit(solution)/shard_map/ppermute | solution.py:57
  85.0 8.3 %collective-permute-start.13 = (f32[1,512,128]{2,1,0:T(8,128)S(1)}, f32[1,512,128]{2,1,0:T(8,128)S(1)}, u32[]{:S(2)}, u32[]{:S(2)}) collective-permute-start(f32[1,512,128]{2,1,0:T(8,128)S(1)} %constant_dynamic-slice_fusion.1), channel_id=1, source_target_pairs={{0,2},{1,3},{2,0},{3,1},{4,6},{5,7},{6,4},{7,5},{8,10},{9,11},{10,... | collective-permute-start | bytes 786440 | tf_op jit(solution)/shard_map/ppermute | solution.py:58
  (4 other events, 3.3 us)

commit v3 on v2

--- a/solution.py
+++ b/solution.py
@@ -31,6 +31,22 @@
         value = lse_pair(value, lax.ppermute(value, axis, pairs))
         step *= 2
     return value
+
+
+def two_round_lse(value, axis):
+    size = lax.axis_size(axis)
+    if size < 4:
+        return butterfly_lse(value, axis)
+    value = lse_pair(value, lax.ppermute(value, axis, [(i, i ^ 1) for i in range(size)]))
+    others = [lax.ppermute(value, axis, [(i, i ^ mask) for i in range(size)])
+              for mask in range(2, size, 2)]
+    overall = value
+    for other in others:
+        overall = jnp.maximum(overall, other)
+    total = jnp.exp(value - overall)
+    for other in others:
+        total = total + jnp.exp(other - overall)
+    return overall + jnp.log(total)
 
 
 def halving_merge(small, numerator, axis):
@@ -348,7 +364,7 @@
         (column_lse,) = column_pass(
             kept_blocks, counts, src_t, src_potential.reshape(1, src_rows), tgt_ones, tnorm
         )
-        column_lse = butterfly_lse(column_lse.reshape(tgt_rows), "src")
+        column_lse = two_round_lse(column_lse.reshape(tgt_rows), "src")
         tgt_potential = EPSILON * jnp.log(tgt_mass) - EPSILON * column_lse
 
     tpot = tgt_potential.reshape(1, tgt_rows)

time: 94.4 us -> 91.8 us (0.972)
  waiting for transfers between devices: 25 us -> 18.9 us
  starting transfers between devices: 26.3 us -> 30 us
  Pallas kernels: 31 us -> 29.9 us
    ppermute x0 -> x8, starting transfers between devices: none -> 17 us  [the longest x6 8.91 us: two_round_lse(): lax.ppermute(value, axis, [(i, i ^ mask) for i in range(size)])]
    ppermute x10 -> x4, starting transfers between devices: 21 us -> 7.51 us  [butterfly_lse(): value = lse_pair(value, lax.ppermute(value, axis, pairs))]
    ppermute x10 -> x4, waiting for transfers between devices: 18.1 us -> 4.9 us  [butterfly_lse(): value = lse_pair(value, lax.ppermute(value, axis, pairs))]
    ppermute x0 -> x8, waiting for transfers between devices: none -> 7.21 us  [the longest x2 3.79 us: two_round_lse(): lax.ppermute(value, axis, [(i, i ^ 1) for i in range(size)])]
    pallas_call x5, Pallas kernels: 31 us -> 29.9 us  [local_call(): pl.pallas_call(kernel, grid_spec=spec, out_shape=outs, compiler_params=pl...]
    unnamed x29 -> x31, local copies, waits for them, and re-layouts: 4.54 us -> 5.15 us
  transfers between devices with their start and end apart: 14 -> 16, of which waited for: 11 -> 12; matrix products, arithmetic and copies ran while one was open for 3% -> 3% of each run, Pallas kernels for 0% -> 0%
where the time goes in v3:
time: 91.8 us; the launch traced here: 91.3 us
  starting transfers between devices  30 us (33%)
  Pallas kernels  29.9 us (33%)
  waiting for transfers between devices  18.9 us (21%)
  local copies, waits for them, and re-layouts  6.42 us (7%)
  other arithmetic  5.18 us (6%)
  between operations  0.95 us (1%)
    pallas_call x5, Pallas kernels, local_call(): pl.pallas_call(kernel, grid_spec=spec, out_shape=outs, compiler_params=pl...  29.9 us
    ppermute x6, starting transfers between devices, two_round_lse(): lax.ppermute(value, axis, [(i, i ^ mask) for i in range(size)])  8.91 us
    ppermute x2, starting transfers between devices, two_round_lse(): lax.ppermute(value, axis, [(i, i ^ 1) for i in range(size)])  8.11 us
    ppermute x4, starting transfers between devices, butterfly_lse(): value = lse_pair(value, lax.ppermute(value, axis, pairs))  7.51 us
    ppermute x2, waiting for transfers between devices, halving_merge(): num_other = lax.ppermute(num_send, axis, pairs)  6.81 us
    unnamed x31, local copies, waits for them, and re-layouts  5.15 us
    ppermute x4, waiting for transfers between devices, butterfly_lse(): value = lse_pair(value, lax.ppermute(value, axis, pairs))  4.9 us
    ppermute x2, waiting for transfers between devices, two_round_lse(): lax.ppermute(value, axis, [(i, i ^ 1) for i in range(size)])  3.79 us
  transfers between devices with their start and end apart: 16, of which 12 were waited for; matrix products, arithmetic and copies ran while one was open for 3% of the time, Pallas kernels for 0%

profile of v3, /device:TPU:0, one launch (start us, length us, event | category | flops | bytes accessed | tf_op | source)
XLA Modules:
  0.0 91.3 jit_solution(5188620720194927897)
XLA Ops:
  0.6 1.5 %multiply_reduce_fusion = f32[8192]{0:T(1024)S(1)} fusion(bf16[64,8192]{1,0:T(8,128)(2,1)} %tgt_ref.5), kind=kLoop, calls=%fused_computation | loop fusion | flops 1564672 | bytes 1081344 | tf_op jit(solution)/shard_map/reduce_sum | solution.py:351
  2.2 1.2 %copy-done = bf16[64,8192]{1,0:T(8,128)(2,1)S(1)} copy-done((bf16[64,8192]{1,0:T(8,128)(2,1)S(1)}, bf16[64,8192]{1,0:T(8,128)(2,1)}, u32[]{:S(2)}) %copy-start) | copy-done | bytes 1048600
  5.7 5.4 %shard_map.94 = f32[1,2048]{1,0:T(1,128)S(1)} custom-call(s32[8,8]{1,0:T(8,128)S(1)} %copy-done.7, s32[8]{0:T(128)S(1)} %bitcast.66, bf16[64,2048]{1,0:T(8,128)(2,1)S(1)} %copy-done.2, bf16[64,8192]{1,0:T(8,128)(2,1)S(1)} %copy-done, f32[1,8192]{1,0:T(1,128)S(1)} %bitcast.47, f32[1,8192]{1,0:T(1,128)S(1)} %reshape.179.tpot_ref), custom_call_target="tpu_custom_call" | custom-call | tf_op jit(solution)/shard_map/pallas_call | solution.py:305
  12.6 3.1 %collective-permute-start.1 = (f32[2048]{0:T(1024)S(1)}, f32[2048]{0:T(1024)S(1)}, u32[]{:S(2)}, u32[]{:S(2)}) collective-permute-start(f32[2048]{0:T(1024)S(1)} %log_add_fusion.3), channel_id=1, source_target_pairs={{0,2},{1,3},{2,0},{3,1},{4,6},{5,7},{6,4},{7,5},{8,10},{9,11},{10,... | collective-permute-start | bytes 24584 | tf_op jit(solution)/shard_map/ppermute | solution.py:31
  16.0 1.4 %collective-permute-done.1 = f32[2048]{0:T(1024)S(1)} collective-permute-done((f32[2048]{0:T(1024)S(1)}, f32[2048]{0:T(1024)S(1)}, u32[]{:S(2)}, u32[]{:S(2)}) %collective-permute-start.1) | collective-permute-done | bytes 8224 | tf_op jit(solution)/shard_map/ppermute | solution.py:31
  17.3 5.1 %shard_map.95 = f32[1,8192]{1,0:T(1,128)S(1)} custom-call(s32[8,8]{1,0:T(8,128)S(1)} %copy-done.7, s32[8]{0:T(128)S(1)} %bitcast.67, bf16[64,2048]{1,0:T(8,128)(2,1)S(1)} %copy-done.2, f32[1,2048]{1,0:T(1,128)S(1)} %bitcast.65, bf16[80,8192]{1,0:T(8,128)(2,1)S(1)} %pad_maximum_fusion.tgt_ref, f32[1,8192]{1,0:T(1,128)S(1)} %bitcast.48), custom_call_target="tpu_custom_call" | custom-call | tf_op jit(solution)/shard_map/pallas_call | solution.py:305
  22.5 4.7 %collective-permute-start.2 = (f32[8192]{0:T(1024)S(1)}, f32[8192]{0:T(1024)S(1)}, u32[]{:S(2)}, u32[]{:S(2)}) collective-permute-start(f32[8192]{0:T(1024)S(1)} %bitcast.55), channel_id=1, source_target_pairs={{0,4},{4,0},{8,12},{12,8},{16,20},{20,16},{24,28},{28,24},{1,5},{5... | collective-permute-start | bytes 98312 | tf_op jit(solution)/shard_map/ppermute | solution.py:40
  27.2 1.9 %collective-permute-done.2 = f32[8192]{0:T(1024)S(1)} collective-permute-done((f32[8192]{0:T(1024)S(1)}, f32[8192]{0:T(1024)S(1)}, u32[]{:S(2)}, u32[]{:S(2)}) %collective-permute-start.2) | collective-permute-done | bytes 32800 | tf_op jit(solution)/shard_map/ppermute | solution.py:40
  30.3 1.3 %collective-permute-start.4 = (f32[8192]{0:T(1024)S(1)}, f32[8192]{0:T(1024)S(1)}, u32[]{:S(2)}, u32[]{:S(2)}) collective-permute-start(f32[8192]{0:T(1024)S(1)} %log_add_fusion.1), channel_id=1, source_target_pairs={{0,16},{4,20},{8,24},{12,28},{16,0},{20,4},{24,8},{28,12},{1,17},{... | collective-permute-start | bytes 98312 | tf_op jit(solution)/shard_map/ppermute | solution.py:41
  31.6 1.9 %collective-permute-start.3 = (f32[8192]{0:T(1024)S(1)}, f32[8192]{0:T(1024)S(1)}, u32[]{:S(2)}, u32[]{:S(2)}) collective-permute-start(f32[8192]{0:T(1024)S(1)} %log_add_fusion.1), channel_id=1, source_target_pairs={{0,8},{4,12},{8,0},{12,4},{16,24},{20,28},{24,16},{28,20},{1,9},{5... | collective-permute-start | bytes 98312 | tf_op jit(solution)/shard_map/ppermute | solution.py:41
  33.6 1.5 %collective-permute-done.5 = f32[8192]{0:T(1024)S(1)} collective-permute-done((f32[8192]{0:T(1024)S(1)}, f32[8192]{0:T(1024)S(1)}, u32[]{:S(2)}, u32[]{:S(2)}) %collective-permute-start.5) | collective-permute-done | bytes 32800 | tf_op jit(solution)/shard_map/ppermute | solution.py:41
  35.7 5.4 %shard_map.96 = f32[1,2048]{1,0:T(1,128)S(1)} custom-call(s32[8,8]{1,0:T(8,128)S(1)} %copy-done.7, s32[8]{0:T(128)S(1)} %bitcast.68, bf16[64,2048]{1,0:T(8,128)(2,1)S(1)} %copy-done.2, bf16[64,8192]{1,0:T(8,128)(2,1)S(1)} %copy-done.1, f32[1,8192]{1,0:T(1,128)S(1)} %bitcast.49, f32[1,8192]{1,0:T(1,128)S(1)} %bitcast.59), custom_call_target="tpu_custom_call" | custom-call | tf_op jit(solution)/shard_map/pallas_call | solution.py:305
  42.3 3.7 %collective-permute-start.7 = (f32[2048]{0:T(1024)S(1)}, f32[2048]{0:T(1024)S(1)}, u32[]{:S(2)}, u32[]{:S(2)}) collective-permute-start(f32[2048]{0:T(1024)S(1)} %log_add_fusion.2), channel_id=1, source_target_pairs={{0,2},{1,3},{2,0},{3,1},{4,6},{5,7},{6,4},{7,5},{8,10},{9,11},{10,... | collective-permute-start | bytes 24584 | tf_op jit(solution)/shard_map/ppermute | solution.py:31
  46.0 1.6 %collective-permute-done.7 = f32[2048]{0:T(1024)S(1)} collective-permute-done((f32[2048]{0:T(1024)S(1)}, f32[2048]{0:T(1024)S(1)}, u32[]{:S(2)}, u32[]{:S(2)}) %collective-permute-start.7) | collective-permute-done | bytes 8224 | tf_op jit(solution)/shard_map/ppermute | solution.py:31
  47.6 5.2 %shard_map.97 = f32[1,8192]{1,0:T(1,128)S(1)} custom-call(s32[8,8]{1,0:T(8,128)S(1)} %copy-done.7, s32[8]{0:T(128)S(1)} %bitcast.69, bf16[64,2048]{1,0:T(8,128)(2,1)S(1)} %copy-done.2, f32[1,2048]{1,0:T(1,128)S(1)} %bitcast.64, bf16[80,8192]{1,0:T(8,128)(2,1)S(1)} %pad_maximum_fusion.tgt_ref, f32[1,8192]{1,0:T(1,128)S(1)} %bitcast.50), custom_call_target="tpu_custom_call" | custom-call | tf_op jit(solution)/shard_map/pallas_call | solution.py:305
  52.9 3.4 %collective-permute-start.8 = (f32[8192]{0:T(1024)S(1)}, f32[8192]{0:T(1024)S(1)}, u32[]{:S(2)}, u32[]{:S(2)}) collective-permute-start(f32[8192]{0:T(1024)S(1)} %bitcast.57), channel_id=1, source_target_pairs={{0,4},{4,0},{8,12},{12,8},{16,20},{20,16},{24,28},{28,24},{1,5},{5... | collective-permute-start | bytes 98312 | tf_op jit(solution)/shard_map/ppermute | solution.py:40
  56.2 1.9 %collective-permute-done.8 = f32[8192]{0:T(1024)S(1)} collective-permute-done((f32[8192]{0:T(1024)S(1)}, f32[8192]{0:T(1024)S(1)}, u32[]{:S(2)}, u32[]{:S(2)}) %collective-permute-start.8) | collective-permute-done | bytes 32800 | tf_op jit(solution)/shard_map/ppermute | solution.py:40
  59.8 2.9 %collective-permute-start.9 = (f32[8192]{0:T(1024)S(1)}, f32[8192]{0:T(1024)}, u32[]{:S(2)}, u32[]{:S(2)}) collective-permute-start(f32[8192]{0:T(1024)S(1)} %log_add_fusion), channel_id=1, source_target_pairs={{0,8},{4,12},{8,0},{12,4},{16,24},{20,28},{24,16},{28,20},{1,9},{5... | collective-permute-start | bytes 98312 | tf_op jit(solution)/shard_map/ppermute | solution.py:41
  62.6 1.3 %collective-permute-done.11 = f32[8192]{0:T(1024)S(1)} collective-permute-done((f32[8192]{0:T(1024)S(1)}, f32[8192]{0:T(1024)S(1)}, u32[]{:S(2)}, u32[]{:S(2)}) %collective-permute-start.11) | collective-permute-done | bytes 32800 | tf_op jit(solution)/shard_map/ppermute | solution.py:41
  65.5 8.8 %shard_map.98 = (f32[2,2048]{1,0:T(2,128)S(1)}, f32[2048,128]{1,0:T(8,128)S(1)}) custom-call(s32[8,8]{1,0:T(8,128)S(1)} %copy-done.8, s32[8]{0:T(128)S(1)} %bitcast.70, bf16[64,2048]{1,0:T(8,128)(2,1)S(1)} %copy-done.3, bf16[64,8192]{1,0:T(8,128)(2,1)S(1)} %copy-done.1, f32[1,8192]{1,0:T(1,128)S(1)} %bitcast.51, f32[1,8192]{1,0:T(1,128)S(1)} %bitcast.54, ...), custom_call_target="tpu_custom_call" | custom-call | tf_op jit(solution)/shard_map/pallas_call | solution.py:305
  77.2 3.4 %collective-permute-start.14 = (f32[2,1,512]{2,1,0:T(1,128)S(1)}, f32[2,1,512]{2,1,0:T(1,128)S(1)}, u32[]{:S(2)}, u32[]{:S(2)}) collective-permute-start(f32[2,1,512]{2,1,0:T(1,128)S(1)} %get-tuple-element.17), channel_id=1, source_target_pairs={{0,2},{1,3},{2,0},{3,1},{4,6},{5,7},{6,4},{7,5},{8,10},{9,11},{10,... | collective-permute-start | bytes 12296 | tf_op jit(solution)/shard_map/ppermute | solution.py:73
  80.7 1.4 %fusion = f32[2,512,128]{2,1,0:T(8,128)S(1)} fusion(f32[2,512,128]{2,1,0:T(8,128)S(1)} %collective-permute-done.13, f32[2,2,512,128]{3,2,1,0:T(8,128)} %bitcast.53, s32[]{:T(128)S(6)} %select_n.43, f32[2,512]{1,0:T(2,128)S(1)} %get-tuple-element.15, f32[2,512]{1,0:T(2,128)S(1)} %get-tuple-element.14), kind=kLoop, calls=%fused_computation.3 | loop fusion | flops 393216 | bytes 1581060 | tf_op jit(solution)/shard_map/add | solution.py:78
  82.1 1.4 %collective-permute-start.15 = (f32[1,512,128]{2,1,0:T(8,128)S(1)}, f32[1,512,128]{2,1,0:T(8,128)S(1)}, u32[]{:S(2)}, u32[]{:S(2)}) collective-permute-start(f32[1,512,128]{2,1,0:T(8,128)S(1)} %constant_dynamic-slice_fusion.1), channel_id=1, source_target_pairs={{0,2},{1,3},{2,0},{3,1},{4,6},{5,7},{6,4},{7,5},{8,10},{9,11},{10,... | collective-permute-start | bytes 786440 | tf_op jit(solution)/shard_map/ppermute | solution.py:74
  83.6 6.8 %collective-permute-done.15 = f32[1,512,128]{2,1,0:T(8,128)S(1)} collective-permute-done((f32[1,512,128]{2,1,0:T(8,128)S(1)}, f32[1,512,128]{2,1,0:T(8,128)S(1)}, u32[]{:S(2)}, u32[]{:S(2)}) %collective-permute-start.15) | collective-permute-done | bytes 262176 | tf_op jit(solution)/shard_map/ppermute | solution.py:74
  (70 shorter events, 14.2 us)
Async XLA Ops:
  2.1 15.2 %copy-start.14 = (f32[2048]{0:T(1024)S(1)}, f32[2048]{0:T(1024)}, u32[]{:S(2)}) copy-start(f32[2048]{0:T(1024)} %param.10) | copy-start | bytes 24580
  11.0 24.6 %copy-start.12 = (f32[8192]{0:T(1024)S(1)}, f32[8192]{0:T(1024)}, u32[]{:S(2)}) copy-start(f32[8192]{0:T(1024)} %param.11) | copy-start | bytes 98308
  11.1 1.5 %collective-permute-start = (f32[2048]{0:T(1024)S(1)}, f32[2048]{0:T(1024)S(1)}, u32[]{:S(2)}, u32[]{:S(2)}) collective-permute-start(f32[2048]{0:T(1024)S(1)} %bitcast.60), channel_id=1, source_target_pairs={{0,1},{1,0},{2,3},{3,2},{4,5},{5,4},{6,7},{7,6},{8,9},{9,8},{10,11... | collective-permute-start | bytes 24584 | tf_op jit(solution)/shard_map/ppermute | solution.py:31
  12.6 23.1 %copy-start.1 = (bf16[64,8192]{1,0:T(8,128)(2,1)S(1)}, bf16[64,8192]{1,0:T(8,128)(2,1)}, u32[]{:S(2)}) copy-start(bf16[64,8192]{1,0:T(8,128)(2,1)} %tgt_ref.5) | copy-start | bytes 3145732
  12.6 4.7 %collective-permute-start.1 = (f32[2048]{0:T(1024)S(1)}, f32[2048]{0:T(1024)S(1)}, u32[]{:S(2)}, u32[]{:S(2)}) collective-permute-start(f32[2048]{0:T(1024)S(1)} %log_add_fusion.3), channel_id=1, source_target_pairs={{0,2},{1,3},{2,0},{3,1},{4,6},{5,7},{6,4},{7,5},{8,10},{9,11},{10,... | collective-permute-start | bytes 24584 | tf_op jit(solution)/shard_map/ppermute | solution.py:31
  22.4 43.1 %copy-start.3 = (bf16[64,2048]{1,0:T(8,128)(2,1)S(1)}, bf16[64,2048]{1,0:T(8,128)(2,1)}, u32[]{:S(2)}) copy-start(bf16[64,2048]{1,0:T(8,128)(2,1)} %src_ref.9) | copy-start | bytes 786436
  22.4 43.1 %copy-start.4 = (bf16[128,8192]{1,0:T(8,128)(2,1)S(1)}, bf16[128,8192]{1,0:T(8,128)(2,1)}, u32[]{:S(2)}) copy-start(bf16[128,8192]{1,0:T(8,128)(2,1)} %feat_ref.1) | copy-start | bytes 6291460
  22.4 43.1 %copy-start.8 = (s32[8,8]{1,0:T(8,128)S(1)}, s32[8,8]{1,0:T(8,128)}, u32[]{:S(2)}) copy-start(s32[8,8]{1,0:T(8,128)} %blocks_ref.9) | copy-start | bytes 772
  22.4 43.1 %copy-start.11 = (s32[8,1]{0,1:T(1,128)S(1)}, s32[8,1]{0,1:T(1,128)}, u32[]{:S(2)}) copy-start(s32[8,1]{0,1:T(1,128)} %param.13) | copy-start | bytes 100
  22.5 6.6 %collective-permute-start.2 = (f32[8192]{0:T(1024)S(1)}, f32[8192]{0:T(1024)S(1)}, u32[]{:S(2)}, u32[]{:S(2)}) collective-permute-start(f32[8192]{0:T(1024)S(1)} %bitcast.55), channel_id=1, source_target_pairs={{0,4},{4,0},{8,12},{12,8},{16,20},{20,16},{24,28},{28,24},{1,5},{5... | collective-permute-start | bytes 98312 | tf_op jit(solution)/shard_map/ppermute | solution.py:40
  29.1 5.9 %collective-permute-start.5 = (f32[8192]{0:T(1024)S(1)}, f32[8192]{0:T(1024)S(1)}, u32[]{:S(2)}, u32[]{:S(2)}) collective-permute-start(f32[8192]{0:T(1024)S(1)} %log_add_fusion.1), channel_id=1, source_target_pairs={{0,24},{4,28},{8,16},{12,20},{16,8},{20,12},{24,0},{28,4},{1,25},{... | collective-permute-start | bytes 98312 | tf_op jit(solution)/shard_map/ppermute | solution.py:41
  30.3 5.0 %collective-permute-start.4 = (f32[8192]{0:T(1024)S(1)}, f32[8192]{0:T(1024)S(1)}, u32[]{:S(2)}, u32[]{:S(2)}) collective-permute-start(f32[8192]{0:T(1024)S(1)} %log_add_fusion.1), channel_id=1, source_target_pairs={{0,16},{4,20},{8,24},{12,28},{16,0},{20,4},{24,8},{28,12},{1,17},{... | collective-permute-start | bytes 98312 | tf_op jit(solution)/shard_map/ppermute | solution.py:41
  31.6 4.0 %collective-permute-start.3 = (f32[8192]{0:T(1024)S(1)}, f32[8192]{0:T(1024)S(1)}, u32[]{:S(2)}, u32[]{:S(2)}) collective-permute-start(f32[8192]{0:T(1024)S(1)} %log_add_fusion.1), channel_id=1, source_target_pairs={{0,8},{4,12},{8,0},{12,4},{16,24},{20,28},{24,16},{28,20},{1,9},{5... | collective-permute-start | bytes 98312 | tf_op jit(solution)/shard_map/ppermute | solution.py:41
  41.0 1.2 %collective-permute-start.6 = (f32[2048]{0:T(1024)S(1)}, f32[2048]{0:T(1024)S(1)}, u32[]{:S(2)}, u32[]{:S(2)}) collective-permute-start(f32[2048]{0:T(1024)S(1)} %bitcast.62), channel_id=1, source_target_pairs={{0,1},{1,0},{2,3},{3,2},{4,5},{5,4},{6,7},{7,6},{8,9},{9,8},{10,11... | collective-permute-start | bytes 24584 | tf_op jit(solution)/shard_map/ppermute | solution.py:31
  42.3 5.3 %collective-permute-start.7 = (f32[2048]{0:T(1024)S(1)}, f32[2048]{0:T(1024)S(1)}, u32[]{:S(2)}, u32[]{:S(2)}) collective-permute-start(f32[2048]{0:T(1024)S(1)} %log_add_fusion.2), channel_id=1, source_target_pairs={{0,2},{1,3},{2,0},{3,1},{4,6},{5,7},{6,4},{7,5},{8,10},{9,11},{10,... | collective-permute-start | bytes 24584 | tf_op jit(solution)/shard_map/ppermute | solution.py:31
  47.6 26.8 %copy-start.9 = (f32[2048]{0:T(1024)}, f32[2048]{0:T(1024)S(1)}, u32[]{:S(2)}) copy-start(f32[2048]{0:T(1024)S(1)} %multiply_subtract_fusion.2) | copy-start | bytes 24580
  52.9 5.3 %collective-permute-start.8 = (f32[8192]{0:T(1024)S(1)}, f32[8192]{0:T(1024)S(1)}, u32[]{:S(2)}, u32[]{:S(2)}) collective-permute-start(f32[8192]{0:T(1024)S(1)} %bitcast.57), channel_id=1, source_target_pairs={{0,4},{4,0},{8,12},{12,8},{16,20},{20,16},{24,28},{28,24},{1,5},{5... | collective-permute-start | bytes 98312 | tf_op jit(solution)/shard_map/ppermute | solution.py:40
  58.2 5.8 %collective-permute-start.11 = (f32[8192]{0:T(1024)S(1)}, f32[8192]{0:T(1024)S(1)}, u32[]{:S(2)}, u32[]{:S(2)}) collective-permute-start(f32[8192]{0:T(1024)S(1)} %log_add_fusion), channel_id=1, source_target_pairs={{0,24},{4,28},{8,16},{12,20},{16,8},{20,12},{24,0},{28,4},{1,25},{... | collective-permute-start | bytes 98312 | tf_op jit(solution)/shard_map/ppermute | solution.py:41
  58.6 5.4 %collective-permute-start.10 = (f32[8192]{0:T(1024)S(1)}, f32[8192]{0:T(1024)}, u32[]{:S(2)}, u32[]{:S(2)}) collective-permute-start(f32[8192]{0:T(1024)S(1)} %log_add_fusion), channel_id=1, source_target_pairs={{0,16},{4,20},{8,24},{12,28},{16,0},{20,4},{24,8},{28,12},{1,17},{... | collective-permute-start | bytes 98312 | tf_op jit(solution)/shard_map/ppermute | solution.py:41
  59.8 4.8 %collective-permute-start.9 = (f32[8192]{0:T(1024)S(1)}, f32[8192]{0:T(1024)}, u32[]{:S(2)}, u32[]{:S(2)}) collective-permute-start(f32[8192]{0:T(1024)S(1)} %log_add_fusion), channel_id=1, source_target_pairs={{0,8},{4,12},{8,0},{12,4},{16,24},{20,28},{24,16},{28,20},{1,9},{5... | collective-permute-start | bytes 98312 | tf_op jit(solution)/shard_map/ppermute | solution.py:41
  75.4 1.7 %collective-permute-start.12 = (f32[2,2,512]{2,1,0:T(2,128)S(1)}, f32[2,2,512]{2,1,0:T(2,128)S(1)}, u32[]{:S(2)}, u32[]{:S(2)}) collective-permute-start(f32[2,2,512]{2,1,0:T(2,128)S(1)} %bitcast.71), channel_id=1, source_target_pairs={{0,1},{1,0},{2,3},{3,2},{4,5},{5,4},{6,7},{7,6},{8,9},{9,8},{10,11... | collective-permute-start | bytes 24584 | tf_op jit(solution)/shard_map/ppermute | solution.py:73
  76.6 4.1 %collective-permute-start.13 = (f32[2,512,128]{2,1,0:T(8,128)S(1)}, f32[2,512,128]{2,1,0:T(8,128)S(1)}, u32[]{:S(2)}, u32[]{:S(2)}) collective-permute-start(f32[2,512,128]{2,1,0:T(8,128)S(1)} %dynamic-slice_bitcast_fusion), channel_id=1, source_target_pairs={{0,1},{1,0},{2,3},{3,2},{4,5},{5,4},{6,7},{7,6},{8,9},{9,8},{10,11... | collective-permute-start | bytes 1572872 | tf_op jit(solution)/shard_map/ppermute | solution.py:74
  77.2 6.3 %collective-permute-start.14 = (f32[2,1,512]{2,1,0:T(1,128)S(1)}, f32[2,1,512]{2,1,0:T(1,128)S(1)}, u32[]{:S(2)}, u32[]{:S(2)}) collective-permute-start(f32[2,1,512]{2,1,0:T(1,128)S(1)} %get-tuple-element.17), channel_id=1, source_target_pairs={{0,2},{1,3},{2,0},{3,1},{4,6},{5,7},{6,4},{7,5},{8,10},{9,11},{10,... | collective-permute-start | bytes 12296 | tf_op jit(solution)/shard_map/ppermute | solution.py:73
  82.1 8.3 %collective-permute-start.15 = (f32[1,512,128]{2,1,0:T(8,128)S(1)}, f32[1,512,128]{2,1,0:T(8,128)S(1)}, u32[]{:S(2)}, u32[]{:S(2)}) collective-permute-start(f32[1,512,128]{2,1,0:T(8,128)S(1)} %constant_dynamic-slice_fusion.1), channel_id=1, source_target_pairs={{0,2},{1,3},{2,0},{3,1},{4,6},{5,7},{6,4},{7,5},{8,10},{9,11},{10,... | collective-permute-start | bytes 786440 | tf_op jit(solution)/shard_map/ppermute | solution.py:74
  (7 other events, 16.2 us)

commit v4 on v3

--- a/solution.py
+++ b/solution.py
@@ -33,13 +33,7 @@
     return value
 
 
-def two_round_lse(value, axis):
-    size = lax.axis_size(axis)
-    if size < 4:
-        return butterfly_lse(value, axis)
-    value = lse_pair(value, lax.ppermute(value, axis, [(i, i ^ 1) for i in range(size)]))
-    others = [lax.ppermute(value, axis, [(i, i ^ mask) for i in range(size)])
-              for mask in range(2, size, 2)]
+def merge_many(value, others):
     overall = value
     for other in others:
         overall = jnp.maximum(overall, other)
@@ -47,6 +41,26 @@
     for other in others:
         total = total + jnp.exp(other - overall)
     return overall + jnp.log(total)
+
+
+def exchange(value, axis, masks):
+    size = lax.axis_size(axis)
+    return [lax.ppermute(value, axis, [(i, i ^ mask) for i in range(size)]) for mask in masks]
+
+
+def two_round_lse(value, axis):
+    size = lax.axis_size(axis)
+    if size < 4:
+        return butterfly_lse(value, axis)
+    value = lse_pair(value, exchange(value, axis, [1])[0])
+    return merge_many(value, exchange(value, axis, range(2, size, 2)))
+
+
+def one_round_lse(value, axis):
+    size = lax.axis_size(axis)
+    if size > 4:
+        return two_round_lse(value, axis)
+    return merge_many(value, exchange(value, axis, range(1, size)))
 
 
 def halving_merge(small, numerator, axis):
@@ -359,7 +373,7 @@
     for iteration in range(ITERS):
         tpot = tgt_potential.reshape(1, tgt_rows)
         (row_lse,) = row_pass(kept_blocks, counts, src_t, tgt_emb, tnorm, tpot)
-        row_lse = butterfly_lse(row_lse.reshape(src_rows), "tgt")
+        row_lse = one_round_lse(row_lse.reshape(src_rows), "tgt")
         src_potential = EPSILON * jnp.log(src_mass) - EPSILON * row_lse
         (column_lse,) = column_pass(
             kept_blocks, counts, src_t, src_potential.reshape(1, src_rows), tgt_ones, tnorm

time: 91.8 us -> 88 us (0.959)
  starting transfers between devices: 30 us -> 16.7 us
  waiting for transfers between devices: 18.9 us -> 26.1 us
  Pallas kernels: 29.9 us -> 32.7 us
    ppermute x12 -> x14, starting transfers between devices: 24.5 us -> 15.3 us  [exchange(): lax.ppermute(value, axis, [(i, i ^ mask) for i in range(size)])]
    ppermute x12 -> x14, waiting for transfers between devices: 12.1 us -> 16.9 us  [exchange(): lax.ppermute(value, axis, [(i, i ^ mask) for i in range(size)])]
    ppermute x2, starting transfers between devices: 3.51 us -> 0.14 us  [halving_merge(): small_other = lax.ppermute(small_send, axis, pairs)]
    pallas_call x5, Pallas kernels: 29.9 us -> 32.7 us  [local_call(): pl.pallas_call(kernel, grid_spec=spec, out_shape=outs, compiler_params=pl...]
    ppermute x2, waiting for transfers between devices: 6.81 us -> 9.18 us  [halving_merge(): num_other = lax.ppermute(num_send, axis, pairs)]
  transfers between devices with their start and end apart: 16 -> 18, of which waited for: 12 -> 14; matrix products, arithmetic and copies ran while one was open for 3% -> 3% of each run, Pallas kernels for 0% -> 0%
where the time goes in v4:
time: 88 us; the launch traced here: 87.6 us
  Pallas kernels  32.7 us (37%)
  waiting for transfers between devices  26.1 us (30%)
  starting transfers between devices  16.7 us (19%)
  local copies, waits for them, and re-layouts  5.96 us (7%)
  other arithmetic  5.16 us (6%)
  between operations  0.96 us (1%)
    pallas_call x5, Pallas kernels, local_call(): pl.pallas_call(kernel, grid_spec=spec, out_shape=outs, compiler_params=pl...  32.7 us
    ppermute x14, waiting for transfers between devices, exchange(): lax.ppermute(value, axis, [(i, i ^ mask) for i in range(size)])  16.9 us
    ppermute x14, starting transfers between devices, exchange(): lax.ppermute(value, axis, [(i, i ^ mask) for i in range(size)])  15.3 us
    ppermute x2, waiting for transfers between devices, halving_merge(): num_other = lax.ppermute(num_send, axis, pairs)  9.18 us
    unnamed x31, local copies, waits for them, and re-layouts  4.7 us
  transfers between devices with their start and end apart: 18, of which 14 were waited for; matrix products, arithmetic and copies ran while one was open for 3% of the time, Pallas kernels for 0%

profile of v4, /device:TPU:0, one launch (start us, length us, event | category | flops | bytes accessed | tf_op | source)
XLA Modules:
  0.0 87.6 jit_solution(10391421749854572663)
XLA Ops:
  0.6 1.5 %multiply_reduce_fusion = f32[8192]{0:T(1024)S(1)} fusion(bf16[64,8192]{1,0:T(8,128)(2,1)} %tgt_ref.5), kind=kLoop, calls=%fused_computation | loop fusion | flops 1564672 | bytes 1081344 | tf_op jit(solution)/shard_map/reduce_sum | solution.py:365
  2.2 1.2 %copy-done = bf16[64,8192]{1,0:T(8,128)(2,1)S(1)} copy-done((bf16[64,8192]{1,0:T(8,128)(2,1)S(1)}, bf16[64,8192]{1,0:T(8,128)(2,1)}, u32[]{:S(2)}) %copy-start) | copy-done | bytes 1048600
  5.7 5.9 %shard_map.94 = f32[1,2048]{1,0:T(1,128)S(1)} custom-call(s32[8,8]{1,0:T(8,128)S(1)} %copy-done.7, s32[8]{0:T(128)S(1)} %bitcast.70, bf16[64,2048]{1,0:T(8,128)(2,1)S(1)} %copy-done.2, bf16[64,8192]{1,0:T(8,128)(2,1)S(1)} %copy-done, f32[1,8192]{1,0:T(1,128)S(1)} %bitcast.47, f32[1,8192]{1,0:T(1,128)S(1)} %reshape.179.tpot_ref), custom_call_target="tpu_custom_call" | custom-call | tf_op jit(solution)/shard_map/pallas_call | solution.py:319
  11.6 2.7 %collective-permute-start.2 = (f32[2048]{0:T(1024)S(1)}, f32[2048]{0:T(1024)S(1)}, u32[]{:S(2)}, u32[]{:S(2)}) collective-permute-start(f32[2048]{0:T(1024)S(1)} %bitcast.61), channel_id=1, source_target_pairs={{0,3},{1,2},{2,1},{3,0},{4,7},{5,6},{6,5},{7,4},{8,11},{9,10},{10,... | collective-permute-start | bytes 24584 | tf_op jit(solution)/shard_map/ppermute | solution.py:48
  15.6 2.3 %collective-permute-done.1 = f32[2048]{0:T(1024)S(1)} collective-permute-done((f32[2048]{0:T(1024)S(1)}, f32[2048]{0:T(1024)S(1)}, u32[]{:S(2)}, u32[]{:S(2)}) %collective-permute-start.1) | collective-permute-done | bytes 8224 | tf_op jit(solution)/shard_map/ppermute | solution.py:48
  17.9 5.5 %shard_map.95 = f32[1,8192]{1,0:T(1,128)S(1)} custom-call(s32[8,8]{1,0:T(8,128)S(1)} %copy-done.7, s32[8]{0:T(128)S(1)} %bitcast.71, bf16[64,2048]{1,0:T(8,128)(2,1)S(1)} %copy-done.2, f32[1,2048]{1,0:T(1,128)S(1)} %bitcast.69, bf16[80,8192]{1,0:T(8,128)(2,1)S(1)} %pad_maximum_fusion.tgt_ref, f32[1,8192]{1,0:T(1,128)S(1)} %bitcast.48), custom_call_target="tpu_custom_call" | custom-call | tf_op jit(solution)/shard_map/pallas_call | solution.py:319
  24.5 2.9 %collective-permute-done.3 = f32[8192]{0:T(1024)S(1)} collective-permute-done((f32[8192]{0:T(1024)S(1)}, f32[8192]{0:T(1024)S(1)}, u32[]{:S(2)}, u32[]{:S(2)}) %collective-permute-start.3) | collective-permute-done | bytes 32800 | tf_op jit(solution)/shard_map/ppermute | solution.py:48
  27.5 3.2 %collective-permute-start.6 = (f32[8192]{0:T(1024)S(1)}, f32[8192]{0:T(1024)S(1)}, u32[]{:S(2)}, u32[]{:S(2)}) collective-permute-start(f32[8192]{0:T(1024)S(1)} %log_add_fusion.1), channel_id=1, source_target_pairs={{0,24},{4,28},{8,16},{12,20},{16,8},{20,12},{24,0},{28,4},{1,25},{... | collective-permute-start | bytes 98312 | tf_op jit(solution)/shard_map/ppermute | solution.py:48
  30.7 1.2 %collective-permute-start.4 = (f32[8192]{0:T(1024)S(1)}, f32[8192]{0:T(1024)S(1)}, u32[]{:S(2)}, u32[]{:S(2)}) collective-permute-start(f32[8192]{0:T(1024)S(1)} %log_add_fusion.1), channel_id=1, source_target_pairs={{0,8},{4,12},{8,0},{12,4},{16,24},{20,28},{24,16},{28,20},{1,9},{5... | collective-permute-start | bytes 98312 | tf_op jit(solution)/shard_map/ppermute | solution.py:48
  31.9 1.3 %collective-permute-done.6 = f32[8192]{0:T(1024)S(1)} collective-permute-done((f32[8192]{0:T(1024)S(1)}, f32[8192]{0:T(1024)S(1)}, u32[]{:S(2)}, u32[]{:S(2)}) %collective-permute-start.6) | collective-permute-done | bytes 32800 | tf_op jit(solution)/shard_map/ppermute | solution.py:48
  33.3 2.3 %collective-permute-done.5 = f32[8192]{0:T(1024)S(1)} collective-permute-done((f32[8192]{0:T(1024)S(1)}, f32[8192]{0:T(1024)S(1)}, u32[]{:S(2)}, u32[]{:S(2)}) %collective-permute-start.5) | collective-permute-done | bytes 32800 | tf_op jit(solution)/shard_map/ppermute | solution.py:48
  35.6 5.9 %shard_map.96 = f32[1,2048]{1,0:T(1,128)S(1)} custom-call(s32[8,8]{1,0:T(8,128)S(1)} %copy-done.7, s32[8]{0:T(128)S(1)} %bitcast.72, bf16[64,2048]{1,0:T(8,128)(2,1)S(1)} %copy-done.2, bf16[64,8192]{1,0:T(8,128)(2,1)S(1)} %copy-done.1, f32[1,8192]{1,0:T(1,128)S(1)} %bitcast.49, f32[1,8192]{1,0:T(1,128)S(1)} %bitcast.59), custom_call_target="tpu_custom_call" | custom-call | tf_op jit(solution)/shard_map/pallas_call | solution.py:319
  42.0 1.3 %collective-permute-start.7 = (f32[2048]{0:T(1024)S(1)}, f32[2048]{0:T(1024)S(1)}, u32[]{:S(2)}, u32[]{:S(2)}) collective-permute-start(f32[2048]{0:T(1024)S(1)} %bitcast.67), channel_id=1, source_target_pairs={{0,1},{1,0},{2,3},{3,2},{4,5},{5,4},{6,7},{7,6},{8,9},{9,8},{10,11... | collective-permute-start | bytes 24584 | tf_op jit(solution)/shard_map/ppermute | solution.py:48
  43.4 1.2 %collective-permute-done.9 = f32[2048]{0:T(1024)S(1)} collective-permute-done((f32[2048]{0:T(1024)S(1)}, f32[2048]{0:T(1024)S(1)}, u32[]{:S(2)}, u32[]{:S(2)}) %collective-permute-start.9) | collective-permute-done | bytes 8224 | tf_op jit(solution)/shard_map/ppermute | solution.py:48
  45.3 5.7 %shard_map.97 = f32[1,8192]{1,0:T(1,128)S(1)} custom-call(s32[8,8]{1,0:T(8,128)S(1)} %copy-done.7, s32[8]{0:T(128)S(1)} %bitcast.73, bf16[64,2048]{1,0:T(8,128)(2,1)S(1)} %copy-done.2, f32[1,2048]{1,0:T(1,128)S(1)} %bitcast.60, bf16[80,8192]{1,0:T(8,128)(2,1)S(1)} %pad_maximum_fusion.tgt_ref, f32[1,8192]{1,0:T(1,128)S(1)} %bitcast.50), custom_call_target="tpu_custom_call" | custom-call | tf_op jit(solution)/shard_map/pallas_call | solution.py:319
  51.6 3.4 %collective-permute-done.10 = f32[8192]{0:T(1024)S(1)} collective-permute-done((f32[8192]{0:T(1024)S(1)}, f32[8192]{0:T(1024)S(1)}, u32[]{:S(2)}, u32[]{:S(2)}) %collective-permute-start.10) | collective-permute-done | bytes 32800 | tf_op jit(solution)/shard_map/ppermute | solution.py:48
  55.0 1.1 %collective-permute-start.13 = (f32[8192]{0:T(1024)S(1)}, f32[8192]{0:T(1024)S(1)}, u32[]{:S(2)}, u32[]{:S(2)}) collective-permute-start(f32[8192]{0:T(1024)S(1)} %log_add_fusion), channel_id=1, source_target_pairs={{0,24},{4,28},{8,16},{12,20},{16,8},{20,12},{24,0},{28,4},{1,25},{... | collective-permute-start | bytes 98312 | tf_op jit(solution)/shard_map/ppermute | solution.py:48
  57.1 2.4 %collective-permute-start.11 = (f32[8192]{0:T(1024)S(1)}, f32[8192]{0:T(1024)}, u32[]{:S(2)}, u32[]{:S(2)}) collective-permute-start(f32[8192]{0:T(1024)S(1)} %log_add_fusion), channel_id=1, source_target_pairs={{0,8},{4,12},{8,0},{12,4},{16,24},{20,28},{24,16},{28,20},{1,9},{5... | collective-permute-start | bytes 98312 | tf_op jit(solution)/shard_map/ppermute | solution.py:48
  59.5 1.3 %collective-permute-done.13 = f32[8192]{0:T(1024)S(1)} collective-permute-done((f32[8192]{0:T(1024)S(1)}, f32[8192]{0:T(1024)S(1)}, u32[]{:S(2)}, u32[]{:S(2)}) %collective-permute-start.13) | collective-permute-done | bytes 32800 | tf_op jit(solution)/shard_map/ppermute | solution.py:48
  62.5 9.8 %shard_map.98 = (f32[2,2048]{1,0:T(2,128)S(1)}, f32[2048,128]{1,0:T(8,128)S(1)}) custom-call(s32[8,8]{1,0:T(8,128)S(1)} %copy-done.8, s32[8]{0:T(128)S(1)} %bitcast.74, bf16[64,2048]{1,0:T(8,128)(2,1)S(1)} %copy-done.3, bf16[64,8192]{1,0:T(8,128)(2,1)S(1)} %copy-done.1, f32[1,8192]{1,0:T(1,128)S(1)} %bitcast.51, f32[1,8192]{1,0:T(1,128)S(1)} %bitcast.54, ...), custom_call_target="tpu_custom_call" | custom-call | tf_op jit(solution)/shard_map/pallas_call | solution.py:319
  73.4 1.1 %dynamic-slice_bitcast_fusion = f32[2,512,128]{2,1,0:T(8,128)S(1)} fusion(f32[2,2,512,128]{3,2,1,0:T(8,128)} %bitcast.52, s32[]{:T(128)S(6)} %select_n.44), kind=kLoop, calls=%fused_computation.4 | loop fusion | bytes 1048580 | tf_op jit(solution)/shard_map/jit(dynamic_index_in_dim)/squeeze | solution.py:82
  75.2 1.3 %collective-permute-done.15 = f32[2,512,128]{2,1,0:T(8,128)S(1)} collective-permute-done((f32[2,512,128]{2,1,0:T(8,128)S(1)}, f32[2,512,128]{2,1,0:T(8,128)S(1)}, u32[]{:S(2)}, u32[]{:S(2)}) %collective-permute-start.15) | collective-permute-done | bytes 524320 | tf_op jit(solution)/shard_map/ppermute | solution.py:88
  76.6 1.4 %fusion = f32[2,512,128]{2,1,0:T(8,128)S(1)} fusion(f32[2,512,128]{2,1,0:T(8,128)S(1)} %collective-permute-done.15, f32[2,2,512,128]{3,2,1,0:T(8,128)} %bitcast.53, s32[]{:T(128)S(6)} %select_n.43, f32[2,512]{1,0:T(2,128)S(1)} %get-tuple-element.15, f32[2,512]{1,0:T(2,128)S(1)} %get-tuple-element.14), kind=kLoop, calls=%fused_computation.3 | loop fusion | flops 393216 | bytes 1581060 | tf_op jit(solution)/shard_map/add | solution.py:92
  78.8 7.8 %collective-permute-done.17 = f32[1,512,128]{2,1,0:T(8,128)S(1)} collective-permute-done((f32[1,512,128]{2,1,0:T(8,128)S(1)}, f32[1,512,128]{2,1,0:T(8,128)S(1)}, u32[]{:S(2)}, u32[]{:S(2)}) %collective-permute-start.17) | collective-permute-done | bytes 262176 | tf_op jit(solution)/shard_map/ppermute | solution.py:88
  (72 shorter events, 13.0 us)
Async XLA Ops:
  11.5 24.0 %copy-start.12 = (f32[8192]{0:T(1024)S(1)}, f32[8192]{0:T(1024)}, u32[]{:S(2)}) copy-start(f32[8192]{0:T(1024)} %param.11) | copy-start | bytes 98308
  11.6 4.1 %collective-permute-start.2 = (f32[2048]{0:T(1024)S(1)}, f32[2048]{0:T(1024)S(1)}, u32[]{:S(2)}, u32[]{:S(2)}) collective-permute-start(f32[2048]{0:T(1024)S(1)} %bitcast.61), channel_id=1, source_target_pairs={{0,3},{1,2},{2,1},{3,0},{4,7},{5,6},{6,5},{7,4},{8,11},{9,10},{10,... | collective-permute-start | bytes 24584 | tf_op jit(solution)/shard_map/ppermute | solution.py:48
  14.2 3.7 %collective-permute-start.1 = (f32[2048]{0:T(1024)S(1)}, f32[2048]{0:T(1024)S(1)}, u32[]{:S(2)}, u32[]{:S(2)}) collective-permute-start(f32[2048]{0:T(1024)S(1)} %bitcast.62), channel_id=1, source_target_pairs={{0,2},{1,3},{2,0},{3,1},{4,6},{5,7},{6,4},{7,5},{8,10},{9,11},{10,... | collective-permute-start | bytes 24584 | tf_op jit(solution)/shard_map/ppermute | solution.py:48
  14.2 3.7 %collective-permute-start = (f32[2048]{0:T(1024)S(1)}, f32[2048]{0:T(1024)S(1)}, u32[]{:S(2)}, u32[]{:S(2)}) collective-permute-start(f32[2048]{0:T(1024)S(1)} %bitcast.63), channel_id=1, source_target_pairs={{0,1},{1,0},{2,3},{3,2},{4,5},{5,4},{6,7},{7,6},{8,9},{9,8},{10,11... | collective-permute-start | bytes 24584 | tf_op jit(solution)/shard_map/ppermute | solution.py:48
  23.4 39.0 %copy-start.3 = (bf16[64,2048]{1,0:T(8,128)(2,1)S(1)}, bf16[64,2048]{1,0:T(8,128)(2,1)}, u32[]{:S(2)}) copy-start(bf16[64,2048]{1,0:T(8,128)(2,1)} %src_ref.9) | copy-start | bytes 786436
  23.4 39.0 %copy-start.4 = (bf16[128,8192]{1,0:T(8,128)(2,1)S(1)}, bf16[128,8192]{1,0:T(8,128)(2,1)}, u32[]{:S(2)}) copy-start(bf16[128,8192]{1,0:T(8,128)(2,1)} %feat_ref.1) | copy-start | bytes 6291460
  23.4 39.0 %copy-start.8 = (s32[8,8]{1,0:T(8,128)S(1)}, s32[8,8]{1,0:T(8,128)}, u32[]{:S(2)}) copy-start(s32[8,8]{1,0:T(8,128)} %blocks_ref.9) | copy-start | bytes 772
  23.5 39.0 %copy-start.11 = (s32[8,1]{0,1:T(1,128)S(1)}, s32[8,1]{0,1:T(1,128)}, u32[]{:S(2)}) copy-start(s32[8,1]{0,1:T(1,128)} %param.13) | copy-start | bytes 100
  23.5 4.0 %collective-permute-start.3 = (f32[8192]{0:T(1024)S(1)}, f32[8192]{0:T(1024)S(1)}, u32[]{:S(2)}, u32[]{:S(2)}) collective-permute-start(f32[8192]{0:T(1024)S(1)} %bitcast.55), channel_id=1, source_target_pairs={{0,4},{4,0},{8,12},{12,8},{16,20},{20,16},{24,28},{28,24},{1,5},{5... | collective-permute-start | bytes 98312 | tf_op jit(solution)/shard_map/ppermute | solution.py:48
  27.5 5.8 %collective-permute-start.6 = (f32[8192]{0:T(1024)S(1)}, f32[8192]{0:T(1024)S(1)}, u32[]{:S(2)}, u32[]{:S(2)}) collective-permute-start(f32[8192]{0:T(1024)S(1)} %log_add_fusion.1), channel_id=1, source_target_pairs={{0,24},{4,28},{8,16},{12,20},{16,8},{20,12},{24,0},{28,4},{1,25},{... | collective-permute-start | bytes 98312 | tf_op jit(solution)/shard_map/ppermute | solution.py:48
  30.7 4.8 %collective-permute-start.5 = (f32[8192]{0:T(1024)S(1)}, f32[8192]{0:T(1024)S(1)}, u32[]{:S(2)}, u32[]{:S(2)}) collective-permute-start(f32[8192]{0:T(1024)S(1)} %log_add_fusion.1), channel_id=1, source_target_pairs={{0,16},{4,20},{8,24},{12,28},{16,0},{20,4},{24,8},{28,12},{1,17},{... | collective-permute-start | bytes 98312 | tf_op jit(solution)/shard_map/ppermute | solution.py:48
  30.7 4.8 %collective-permute-start.4 = (f32[8192]{0:T(1024)S(1)}, f32[8192]{0:T(1024)S(1)}, u32[]{:S(2)}, u32[]{:S(2)}) collective-permute-start(f32[8192]{0:T(1024)S(1)} %log_add_fusion.1), channel_id=1, source_target_pairs={{0,8},{4,12},{8,0},{12,4},{16,24},{20,28},{24,16},{28,20},{1,9},{5... | collective-permute-start | bytes 98312 | tf_op jit(solution)/shard_map/ppermute | solution.py:48
  41.4 3.1 %collective-permute-start.9 = (f32[2048]{0:T(1024)S(1)}, f32[2048]{0:T(1024)S(1)}, u32[]{:S(2)}, u32[]{:S(2)}) collective-permute-start(f32[2048]{0:T(1024)S(1)} %bitcast.65), channel_id=1, source_target_pairs={{0,3},{1,2},{2,1},{3,0},{4,7},{5,6},{6,5},{7,4},{8,11},{9,10},{10,... | collective-permute-start | bytes 24584 | tf_op jit(solution)/shard_map/ppermute | solution.py:48
  41.5 3.7 %collective-permute-start.8 = (f32[2048]{0:T(1024)S(1)}, f32[2048]{0:T(1024)S(1)}, u32[]{:S(2)}, u32[]{:S(2)}) collective-permute-start(f32[2048]{0:T(1024)S(1)} %bitcast.66), channel_id=1, source_target_pairs={{0,2},{1,3},{2,0},{3,1},{4,6},{5,7},{6,4},{7,5},{8,10},{9,11},{10,... | collective-permute-start | bytes 24584 | tf_op jit(solution)/shard_map/ppermute | solution.py:48
  42.0 3.2 %collective-permute-start.7 = (f32[2048]{0:T(1024)S(1)}, f32[2048]{0:T(1024)S(1)}, u32[]{:S(2)}, u32[]{:S(2)}) collective-permute-start(f32[2048]{0:T(1024)S(1)} %bitcast.67), channel_id=1, source_target_pairs={{0,1},{1,0},{2,3},{3,2},{4,5},{5,4},{6,7},{7,6},{8,9},{9,8},{10,11... | collective-permute-start | bytes 24584 | tf_op jit(solution)/shard_map/ppermute | solution.py:48
  45.3 27.0 %copy-start.9 = (f32[2048]{0:T(1024)}, f32[2048]{0:T(1024)S(1)}, u32[]{:S(2)}) copy-start(f32[2048]{0:T(1024)S(1)} %multiply_subtract_fusion.2) | copy-start | bytes 24580
  51.0 4.0 %collective-permute-start.10 = (f32[8192]{0:T(1024)S(1)}, f32[8192]{0:T(1024)S(1)}, u32[]{:S(2)}, u32[]{:S(2)}) collective-permute-start(f32[8192]{0:T(1024)S(1)} %bitcast.57), channel_id=1, source_target_pairs={{0,4},{4,0},{8,12},{12,8},{16,20},{20,16},{24,28},{28,24},{1,5},{5... | collective-permute-start | bytes 98312 | tf_op jit(solution)/shard_map/ppermute | solution.py:48
  55.0 5.8 %collective-permute-start.13 = (f32[8192]{0:T(1024)S(1)}, f32[8192]{0:T(1024)S(1)}, u32[]{:S(2)}, u32[]{:S(2)}) collective-permute-start(f32[8192]{0:T(1024)S(1)} %log_add_fusion), channel_id=1, source_target_pairs={{0,24},{4,28},{8,16},{12,20},{16,8},{20,12},{24,0},{28,4},{1,25},{... | collective-permute-start | bytes 98312 | tf_op jit(solution)/shard_map/ppermute | solution.py:48
  56.1 5.1 %collective-permute-start.12 = (f32[8192]{0:T(1024)S(1)}, f32[8192]{0:T(1024)}, u32[]{:S(2)}, u32[]{:S(2)}) collective-permute-start(f32[8192]{0:T(1024)S(1)} %log_add_fusion), channel_id=1, source_target_pairs={{0,16},{4,20},{8,24},{12,28},{16,0},{20,4},{24,8},{28,12},{1,17},{... | collective-permute-start | bytes 98312 | tf_op jit(solution)/shard_map/ppermute | solution.py:48
  57.1 4.5 %collective-permute-start.11 = (f32[8192]{0:T(1024)S(1)}, f32[8192]{0:T(1024)}, u32[]{:S(2)}, u32[]{:S(2)}) collective-permute-start(f32[8192]{0:T(1024)S(1)} %log_add_fusion), channel_id=1, source_target_pairs={{0,8},{4,12},{8,0},{12,4},{16,24},{20,28},{24,16},{28,20},{1,9},{5... | collective-permute-start | bytes 98312 | tf_op jit(solution)/shard_map/ppermute | solution.py:48
  73.3 1.7 %collective-permute-start.14 = (f32[2,2,512]{2,1,0:T(2,128)S(1)}, f32[2,2,512]{2,1,0:T(2,128)S(1)}, u32[]{:S(2)}, u32[]{:S(2)}) collective-permute-start(f32[2,2,512]{2,1,0:T(2,128)S(1)} %bitcast.75), channel_id=1, source_target_pairs={{0,1},{1,0},{2,3},{3,2},{4,5},{5,4},{6,7},{7,6},{8,9},{9,8},{10,11... | collective-permute-start | bytes 24584 | tf_op jit(solution)/shard_map/ppermute | solution.py:87
  74.5 2.1 %collective-permute-start.15 = (f32[2,512,128]{2,1,0:T(8,128)S(1)}, f32[2,512,128]{2,1,0:T(8,128)S(1)}, u32[]{:S(2)}, u32[]{:S(2)}) collective-permute-start(f32[2,512,128]{2,1,0:T(8,128)S(1)} %dynamic-slice_bitcast_fusion), channel_id=1, source_target_pairs={{0,1},{1,0},{2,3},{3,2},{4,5},{5,4},{6,7},{7,6},{8,9},{9,8},{10,11... | collective-permute-start | bytes 1572872 | tf_op jit(solution)/shard_map/ppermute | solution.py:88
  75.1 3.7 %collective-permute-start.16 = (f32[2,1,512]{2,1,0:T(1,128)S(1)}, f32[2,1,512]{2,1,0:T(1,128)S(1)}, u32[]{:S(2)}, u32[]{:S(2)}) collective-permute-start(f32[2,1,512]{2,1,0:T(1,128)S(1)} %get-tuple-element.17), channel_id=1, source_target_pairs={{0,2},{1,3},{2,0},{3,1},{4,6},{5,7},{6,4},{7,5},{8,10},{9,11},{10,... | collective-permute-start | bytes 12296 | tf_op jit(solution)/shard_map/ppermute | solution.py:87
  78.0 8.7 %collective-permute-start.17 = (f32[1,512,128]{2,1,0:T(8,128)S(1)}, f32[1,512,128]{2,1,0:T(8,128)S(1)}, u32[]{:S(2)}, u32[]{:S(2)}) collective-permute-start(f32[1,512,128]{2,1,0:T(8,128)S(1)} %constant_dynamic-slice_fusion.1), channel_id=1, source_target_pairs={{0,2},{1,3},{2,0},{3,1},{4,6},{5,7},{6,4},{7,5},{8,10},{9,11},{10,... | collective-permute-start | bytes 786440 | tf_op jit(solution)/shard_map/ppermute | solution.py:88
  (9 other events, 54.0 us)

commit v5 on v4

--- a/solution.py
+++ b/solution.py
@@ -50,6 +50,9 @@
 
 def two_round_lse(value, axis):
     size = lax.axis_size(axis)
+    if size == 8:
+        value = merge_many(value, exchange(value, axis, [1, 2, 3]))
+        return lse_pair(value, exchange(value, axis, [4])[0])
     if size < 4:
         return butterfly_lse(value, axis)
     value = lse_pair(value, exchange(value, axis, [1])[0])

time: 88 us -> 86.8 us (0.986)
  starting transfers between devices: 16.7 us -> 21.3 us
  waiting for transfers between devices: 26.1 us -> 23.2 us
  Pallas kernels: 32.7 us -> 30 us
    ppermute x14, starting transfers between devices: 15.3 us -> 19.8 us  [exchange(): lax.ppermute(value, axis, [(i, i ^ mask) for i in range(size)])]
    ppermute x14, waiting for transfers between devices: 16.9 us -> 14 us  [exchange(): lax.ppermute(value, axis, [(i, i ^ mask) for i in range(size)])]
    pallas_call x5, Pallas kernels: 32.7 us -> 30 us  [local_call(): pl.pallas_call(kernel, grid_spec=spec, out_shape=outs, compiler_params=pl...]
    unnamed x31 -> x29, local copies, waits for them, and re-layouts: 4.7 us -> 4.53 us
where the time goes in v5:
time: 86.8 us; the launch traced here: 86.4 us
  Pallas kernels  30 us (35%)
  waiting for transfers between devices  23.2 us (27%)
  starting transfers between devices  21.3 us (25%)
  local copies, waits for them, and re-layouts  5.8 us (7%)
  other arithmetic  5.13 us (6%)
  between operations  0.94 us (1%)
    pallas_call x5, Pallas kernels, local_call(): pl.pallas_call(kernel, grid_spec=spec, out_shape=outs, compiler_params=pl...  30 us
    ppermute x14, starting transfers between devices, exchange(): lax.ppermute(value, axis, [(i, i ^ mask) for i in range(size)])  19.8 us
    ppermute x14, waiting for transfers between devices, exchange(): lax.ppermute(value, axis, [(i, i ^ mask) for i in range(size)])  14 us
    ppermute x2, waiting for transfers between devices, halving_merge(): num_other = lax.ppermute(num_send, axis, pairs)  9.13 us
    unnamed x29, local copies, waits for them, and re-layouts  4.53 us
  transfers between devices with their start and end apart: 18, of which 14 were waited for; matrix products, arithmetic and copies ran while one was open for 3% of the time, Pallas kernels for 0%

profile of v5, /device:TPU:0, one launch (start us, length us, event | category | flops | bytes accessed | tf_op | source)
XLA Modules:
  0.0 86.4 jit_solution(15690345645148744960)
XLA Ops:
  0.6 1.5 %multiply_reduce_fusion = f32[8192]{0:T(1024)S(1)} fusion(bf16[64,8192]{1,0:T(8,128)(2,1)} %tgt_ref.5), kind=kLoop, calls=%fused_computation | loop fusion | flops 1564672 | bytes 1081344 | tf_op jit(solution)/shard_map/reduce_sum | solution.py:368
  2.2 1.2 %copy-done = bf16[64,8192]{1,0:T(8,128)(2,1)S(1)} copy-done((bf16[64,8192]{1,0:T(8,128)(2,1)S(1)}, bf16[64,8192]{1,0:T(8,128)(2,1)}, u32[]{:S(2)}) %copy-start) | copy-done | bytes 1048600
  5.7 5.4 %shard_map.94 = f32[1,2048]{1,0:T(1,128)S(1)} custom-call(s32[8,8]{1,0:T(8,128)S(1)} %copy-done.7, s32[8]{0:T(128)S(1)} %bitcast.74, bf16[64,2048]{1,0:T(8,128)(2,1)S(1)} %copy-done.2, bf16[64,8192]{1,0:T(8,128)(2,1)S(1)} %copy-done, f32[1,8192]{1,0:T(1,128)S(1)} %bitcast.47, f32[1,8192]{1,0:T(1,128)S(1)} %reshape.179.tpot_ref), custom_call_target="tpu_custom_call" | custom-call | tf_op jit(solution)/shard_map/pallas_call | solution.py:322
  11.1 2.8 %collective-permute-start.2 = (f32[2048]{0:T(1024)S(1)}, f32[2048]{0:T(1024)S(1)}, u32[]{:S(2)}, u32[]{:S(2)}) collective-permute-start(f32[2048]{0:T(1024)S(1)} %bitcast.65), channel_id=1, source_target_pairs={{0,3},{1,2},{2,1},{3,0},{4,7},{5,6},{6,5},{7,4},{8,11},{9,10},{10,... | collective-permute-start | bytes 24584 | tf_op jit(solution)/shard_map/ppermute | solution.py:48
  15.3 2.2 %collective-permute-done.1 = f32[2048]{0:T(1024)S(1)} collective-permute-done((f32[2048]{0:T(1024)S(1)}, f32[2048]{0:T(1024)S(1)}, u32[]{:S(2)}, u32[]{:S(2)}) %collective-permute-start.1) | collective-permute-done | bytes 8224 | tf_op jit(solution)/shard_map/ppermute | solution.py:48
  17.5 5.1 %shard_map.95 = f32[1,8192]{1,0:T(1,128)S(1)} custom-call(s32[8,8]{1,0:T(8,128)S(1)} %copy-done.7, s32[8]{0:T(128)S(1)} %bitcast.75, bf16[64,2048]{1,0:T(8,128)(2,1)S(1)} %copy-done.2, f32[1,2048]{1,0:T(1,128)S(1)} %bitcast.73, bf16[80,8192]{1,0:T(8,128)(2,1)S(1)} %pad_maximum_fusion.tgt_ref, f32[1,8192]{1,0:T(1,128)S(1)} %bitcast.48), custom_call_target="tpu_custom_call" | custom-call | tf_op jit(solution)/shard_map/pallas_call | solution.py:322
  22.7 2.9 %collective-permute-start.5 = (f32[8192]{0:T(1024)S(1)}, f32[8192]{0:T(1024)S(1)}, u32[]{:S(2)}, u32[]{:S(2)}) collective-permute-start(f32[8192]{0:T(1024)S(1)} %bitcast.55), channel_id=1, source_target_pairs={{0,12},{4,8},{8,4},{12,0},{16,28},{20,24},{24,20},{28,16},{1,13},{... | collective-permute-start | bytes 98312 | tf_op jit(solution)/shard_map/ppermute | solution.py:48
  26.3 1.5 %collective-permute-done.5 = f32[8192]{0:T(1024)S(1)} collective-permute-done((f32[8192]{0:T(1024)S(1)}, f32[8192]{0:T(1024)S(1)}, u32[]{:S(2)}, u32[]{:S(2)}) %collective-permute-start.5) | collective-permute-done | bytes 32800 | tf_op jit(solution)/shard_map/ppermute | solution.py:48
  27.8 1.8 %collective-permute-done.4 = f32[8192]{0:T(1024)S(1)} collective-permute-done((f32[8192]{0:T(1024)S(1)}, f32[8192]{0:T(1024)S(1)}, u32[]{:S(2)}, u32[]{:S(2)}) %collective-permute-start.4) | collective-permute-done | bytes 32800 | tf_op jit(solution)/shard_map/ppermute | solution.py:48
  29.6 3.8 %collective-permute-start.6 = (f32[8192]{0:T(1024)S(1)}, f32[8192]{0:T(1024)S(1)}, u32[]{:S(2)}, u32[]{:S(2)}) collective-permute-start(f32[8192]{0:T(1024)S(1)} %log_add_fusion.1), channel_id=1, source_target_pairs={{0,16},{4,20},{8,24},{12,28},{16,0},{20,4},{24,8},{28,12},{1,17},{... | collective-permute-start | bytes 98312 | tf_op jit(solution)/shard_map/ppermute | solution.py:48
  33.3 1.9 %collective-permute-done.6 = f32[8192]{0:T(1024)S(1)} collective-permute-done((f32[8192]{0:T(1024)S(1)}, f32[8192]{0:T(1024)S(1)}, u32[]{:S(2)}, u32[]{:S(2)}) %collective-permute-start.6) | collective-permute-done | bytes 32800 | tf_op jit(solution)/shard_map/ppermute | solution.py:48
  35.3 5.4 %shard_map.96 = f32[1,2048]{1,0:T(1,128)S(1)} custom-call(s32[8,8]{1,0:T(8,128)S(1)} %copy-done.7, s32[8]{0:T(128)S(1)} %bitcast.76, bf16[64,2048]{1,0:T(8,128)(2,1)S(1)} %copy-done.2, bf16[64,8192]{1,0:T(8,128)(2,1)S(1)} %copy-done.1, f32[1,8192]{1,0:T(1,128)S(1)} %bitcast.49, f32[1,8192]{1,0:T(1,128)S(1)} %bitcast.63), custom_call_target="tpu_custom_call" | custom-call | tf_op jit(solution)/shard_map/pallas_call | solution.py:322
  40.8 1.8 %collective-permute-start.7 = (f32[2048]{0:T(1024)S(1)}, f32[2048]{0:T(1024)S(1)}, u32[]{:S(2)}, u32[]{:S(2)}) collective-permute-start(f32[2048]{0:T(1024)S(1)} %bitcast.71), channel_id=1, source_target_pairs={{0,1},{1,0},{2,3},{3,2},{4,5},{5,4},{6,7},{7,6},{8,9},{9,8},{10,11... | collective-permute-start | bytes 24584 | tf_op jit(solution)/shard_map/ppermute | solution.py:48
  42.6 1.2 %collective-permute-done.9 = f32[2048]{0:T(1024)S(1)} collective-permute-done((f32[2048]{0:T(1024)S(1)}, f32[2048]{0:T(1024)S(1)}, u32[]{:S(2)}, u32[]{:S(2)}) %collective-permute-start.9) | collective-permute-done | bytes 8224 | tf_op jit(solution)/shard_map/ppermute | solution.py:48
  44.5 5.3 %shard_map.97 = f32[1,8192]{1,0:T(1,128)S(1)} custom-call(s32[8,8]{1,0:T(8,128)S(1)} %copy-done.7, s32[8]{0:T(128)S(1)} %bitcast.77, bf16[64,2048]{1,0:T(8,128)(2,1)S(1)} %copy-done.2, f32[1,2048]{1,0:T(1,128)S(1)} %bitcast.64, bf16[80,8192]{1,0:T(8,128)(2,1)S(1)} %pad_maximum_fusion.tgt_ref, f32[1,8192]{1,0:T(1,128)S(1)} %bitcast.50), custom_call_target="tpu_custom_call" | custom-call | tf_op jit(solution)/shard_map/pallas_call | solution.py:322
  49.8 1.3 %collective-permute-start.12 = (f32[8192]{0:T(1024)S(1)}, f32[8192]{0:T(1024)S(1)}, u32[]{:S(2)}, u32[]{:S(2)}) collective-permute-start(f32[8192]{0:T(1024)S(1)} %bitcast.59), channel_id=1, source_target_pairs={{0,12},{4,8},{8,4},{12,0},{16,28},{20,24},{24,20},{28,16},{1,13},{... | collective-permute-start | bytes 98312 | tf_op jit(solution)/shard_map/ppermute | solution.py:48
  51.3 2.1 %collective-permute-start.10 = (f32[8192]{0:T(1024)S(1)}, f32[8192]{0:T(1024)S(1)}, u32[]{:S(2)}, u32[]{:S(2)}) collective-permute-start(f32[8192]{0:T(1024)S(1)} %bitcast.61), channel_id=1, source_target_pairs={{0,4},{4,0},{8,12},{12,8},{16,20},{20,16},{24,28},{28,24},{1,5},{5... | collective-permute-start | bytes 98312 | tf_op jit(solution)/shard_map/ppermute | solution.py:48
  53.4 1.3 %collective-permute-done.12 = f32[8192]{0:T(1024)S(1)} collective-permute-done((f32[8192]{0:T(1024)S(1)}, f32[8192]{0:T(1024)S(1)}, u32[]{:S(2)}, u32[]{:S(2)}) %collective-permute-start.12) | collective-permute-done | bytes 32800 | tf_op jit(solution)/shard_map/ppermute | solution.py:48
  55.3 4.0 %collective-permute-start.13 = (f32[8192]{0:T(1024)S(1)}, f32[8192]{0:T(1024)}, u32[]{:S(2)}, u32[]{:S(2)}) collective-permute-start(f32[8192]{0:T(1024)S(1)} %log_add_fusion), channel_id=1, source_target_pairs={{0,16},{4,20},{8,24},{12,28},{16,0},{20,4},{24,8},{28,12},{1,17},{... | collective-permute-start | bytes 98312 | tf_op jit(solution)/shard_map/ppermute | solution.py:48
  59.3 2.0 %collective-permute-done.13 = f32[8192]{0:T(1024)} collective-permute-done((f32[8192]{0:T(1024)S(1)}, f32[8192]{0:T(1024)}, u32[]{:S(2)}, u32[]{:S(2)}) %collective-permute-start.13) | collective-permute-done | bytes 32800 | tf_op jit(solution)/shard_map/ppermute | solution.py:48
  62.2 8.8 %shard_map.98 = (f32[2,2048]{1,0:T(2,128)S(1)}, f32[2048,128]{1,0:T(8,128)S(1)}) custom-call(s32[8,8]{1,0:T(8,128)S(1)} %copy-done.8, s32[8]{0:T(128)S(1)} %bitcast.78, bf16[64,2048]{1,0:T(8,128)(2,1)S(1)} %copy-done.3, bf16[64,8192]{1,0:T(8,128)(2,1)S(1)} %copy-done.1, f32[1,8192]{1,0:T(1,128)S(1)} %bitcast.51, f32[1,8192]{1,0:T(1,128)S(1)} %bitcast.54, ...), custom_call_target="tpu_custom_call" | custom-call | tf_op jit(solution)/shard_map/pallas_call | solution.py:322
  74.0 1.3 %collective-permute-done.15 = f32[2,512,128]{2,1,0:T(8,128)S(1)} collective-permute-done((f32[2,512,128]{2,1,0:T(8,128)S(1)}, f32[2,512,128]{2,1,0:T(8,128)S(1)}, u32[]{:S(2)}, u32[]{:S(2)}) %collective-permute-start.15) | collective-permute-done | bytes 524320 | tf_op jit(solution)/shard_map/ppermute | solution.py:91
  75.3 1.4 %fusion = f32[2,512,128]{2,1,0:T(8,128)S(1)} fusion(f32[2,512,128]{2,1,0:T(8,128)S(1)} %collective-permute-done.15, f32[2,2,512,128]{3,2,1,0:T(8,128)} %bitcast.53, s32[]{:T(128)S(6)} %select_n.43, f32[2,512]{1,0:T(2,128)S(1)} %get-tuple-element.15, f32[2,512]{1,0:T(2,128)S(1)} %get-tuple-element.14), kind=kLoop, calls=%fused_computation.3 | loop fusion | flops 393216 | bytes 1581060 | tf_op jit(solution)/shard_map/add | solution.py:95
  77.6 7.8 %collective-permute-done.17 = f32[1,512,128]{2,1,0:T(8,128)S(1)} collective-permute-done((f32[1,512,128]{2,1,0:T(8,128)S(1)}, f32[1,512,128]{2,1,0:T(8,128)S(1)}, u32[]{:S(2)}, u32[]{:S(2)}) %collective-permute-start.17) | collective-permute-done | bytes 262176 | tf_op jit(solution)/shard_map/ppermute | solution.py:91
  (70 shorter events, 11.7 us)
Async XLA Ops:
  11.1 4.2 %collective-permute-start.2 = (f32[2048]{0:T(1024)S(1)}, f32[2048]{0:T(1024)S(1)}, u32[]{:S(2)}, u32[]{:S(2)}) collective-permute-start(f32[2048]{0:T(1024)S(1)} %bitcast.65), channel_id=1, source_target_pairs={{0,3},{1,2},{2,1},{3,0},{4,7},{5,6},{6,5},{7,4},{8,11},{9,10},{10,... | collective-permute-start | bytes 24584 | tf_op jit(solution)/shard_map/ppermute | solution.py:48
  13.9 3.7 %collective-permute-start.1 = (f32[2048]{0:T(1024)S(1)}, f32[2048]{0:T(1024)S(1)}, u32[]{:S(2)}, u32[]{:S(2)}) collective-permute-start(f32[2048]{0:T(1024)S(1)} %bitcast.66), channel_id=1, source_target_pairs={{0,2},{1,3},{2,0},{3,1},{4,6},{5,7},{6,4},{7,5},{8,10},{9,11},{10,... | collective-permute-start | bytes 24584 | tf_op jit(solution)/shard_map/ppermute | solution.py:48
  13.9 3.7 %collective-permute-start = (f32[2048]{0:T(1024)S(1)}, f32[2048]{0:T(1024)S(1)}, u32[]{:S(2)}, u32[]{:S(2)}) collective-permute-start(f32[2048]{0:T(1024)S(1)} %bitcast.67), channel_id=1, source_target_pairs={{0,1},{1,0},{2,3},{3,2},{4,5},{5,4},{6,7},{7,6},{8,9},{9,8},{10,11... | collective-permute-start | bytes 24584 | tf_op jit(solution)/shard_map/ppermute | solution.py:48
  14.1 21.1 %copy-start.1 = (bf16[64,8192]{1,0:T(8,128)(2,1)S(1)}, bf16[64,8192]{1,0:T(8,128)(2,1)}, u32[]{:S(2)}) copy-start(bf16[64,8192]{1,0:T(8,128)(2,1)} %tgt_ref.5) | copy-start | bytes 3145732
  22.7 39.5 %copy-start.3 = (bf16[64,2048]{1,0:T(8,128)(2,1)S(1)}, bf16[64,2048]{1,0:T(8,128)(2,1)}, u32[]{:S(2)}) copy-start(bf16[64,2048]{1,0:T(8,128)(2,1)} %src_ref.9) | copy-start | bytes 786436
  22.7 39.5 %copy-start.4 = (bf16[128,8192]{1,0:T(8,128)(2,1)S(1)}, bf16[128,8192]{1,0:T(8,128)(2,1)}, u32[]{:S(2)}) copy-start(bf16[128,8192]{1,0:T(8,128)(2,1)} %feat_ref.1) | copy-start | bytes 6291460
  22.7 39.4 %copy-start.8 = (s32[8,8]{1,0:T(8,128)S(1)}, s32[8,8]{1,0:T(8,128)}, u32[]{:S(2)}) copy-start(s32[8,8]{1,0:T(8,128)} %blocks_ref.9) | copy-start | bytes 772
  22.7 39.4 %copy-start.11 = (s32[8,1]{0,1:T(1,128)S(1)}, s32[8,1]{0,1:T(1,128)}, u32[]{:S(2)}) copy-start(s32[8,1]{0,1:T(1,128)} %param.13) | copy-start | bytes 100
  22.7 5.0 %collective-permute-start.5 = (f32[8192]{0:T(1024)S(1)}, f32[8192]{0:T(1024)S(1)}, u32[]{:S(2)}, u32[]{:S(2)}) collective-permute-start(f32[8192]{0:T(1024)S(1)} %bitcast.55), channel_id=1, source_target_pairs={{0,12},{4,8},{8,4},{12,0},{16,28},{20,24},{24,20},{28,16},{1,13},{... | collective-permute-start | bytes 98312 | tf_op jit(solution)/shard_map/ppermute | solution.py:48
  25.6 3.9 %collective-permute-start.4 = (f32[8192]{0:T(1024)S(1)}, f32[8192]{0:T(1024)S(1)}, u32[]{:S(2)}, u32[]{:S(2)}) collective-permute-start(f32[8192]{0:T(1024)S(1)} %bitcast.56), channel_id=1, source_target_pairs={{0,8},{4,12},{8,0},{12,4},{16,24},{20,28},{24,16},{28,20},{1,9},{5... | collective-permute-start | bytes 98312 | tf_op jit(solution)/shard_map/ppermute | solution.py:48
  25.6 3.9 %collective-permute-start.3 = (f32[8192]{0:T(1024)S(1)}, f32[8192]{0:T(1024)S(1)}, u32[]{:S(2)}, u32[]{:S(2)}) collective-permute-start(f32[8192]{0:T(1024)S(1)} %bitcast.57), channel_id=1, source_target_pairs={{0,4},{4,0},{8,12},{12,8},{16,20},{20,16},{24,28},{28,24},{1,5},{5... | collective-permute-start | bytes 98312 | tf_op jit(solution)/shard_map/ppermute | solution.py:48
  29.6 5.7 %collective-permute-start.6 = (f32[8192]{0:T(1024)S(1)}, f32[8192]{0:T(1024)S(1)}, u32[]{:S(2)}, u32[]{:S(2)}) collective-permute-start(f32[8192]{0:T(1024)S(1)} %log_add_fusion.1), channel_id=1, source_target_pairs={{0,16},{4,20},{8,24},{12,28},{16,0},{20,4},{24,8},{28,12},{1,17},{... | collective-permute-start | bytes 98312 | tf_op jit(solution)/shard_map/ppermute | solution.py:48
  40.7 3.1 %collective-permute-start.9 = (f32[2048]{0:T(1024)S(1)}, f32[2048]{0:T(1024)S(1)}, u32[]{:S(2)}, u32[]{:S(2)}) collective-permute-start(f32[2048]{0:T(1024)S(1)} %bitcast.69), channel_id=1, source_target_pairs={{0,3},{1,2},{2,1},{3,0},{4,7},{5,6},{6,5},{7,4},{8,11},{9,10},{10,... | collective-permute-start | bytes 24584 | tf_op jit(solution)/shard_map/ppermute | solution.py:48
  40.8 3.7 %collective-permute-start.8 = (f32[2048]{0:T(1024)S(1)}, f32[2048]{0:T(1024)S(1)}, u32[]{:S(2)}, u32[]{:S(2)}) collective-permute-start(f32[2048]{0:T(1024)S(1)} %bitcast.70), channel_id=1, source_target_pairs={{0,2},{1,3},{2,0},{3,1},{4,6},{5,7},{6,4},{7,5},{8,10},{9,11},{10,... | collective-permute-start | bytes 24584 | tf_op jit(solution)/shard_map/ppermute | solution.py:48
  40.8 3.6 %collective-permute-start.7 = (f32[2048]{0:T(1024)S(1)}, f32[2048]{0:T(1024)S(1)}, u32[]{:S(2)}, u32[]{:S(2)}) collective-permute-start(f32[2048]{0:T(1024)S(1)} %bitcast.71), channel_id=1, source_target_pairs={{0,1},{1,0},{2,3},{3,2},{4,5},{5,4},{6,7},{7,6},{8,9},{9,8},{10,11... | collective-permute-start | bytes 24584 | tf_op jit(solution)/shard_map/ppermute | solution.py:48
  44.5 26.5 %copy-start.9 = (f32[2048]{0:T(1024)}, f32[2048]{0:T(1024)S(1)}, u32[]{:S(2)}) copy-start(f32[2048]{0:T(1024)S(1)} %multiply_subtract_fusion.2) | copy-start | bytes 24580
  49.8 4.9 %collective-permute-start.12 = (f32[8192]{0:T(1024)S(1)}, f32[8192]{0:T(1024)S(1)}, u32[]{:S(2)}, u32[]{:S(2)}) collective-permute-start(f32[8192]{0:T(1024)S(1)} %bitcast.59), channel_id=1, source_target_pairs={{0,12},{4,8},{8,4},{12,0},{16,28},{20,24},{24,20},{28,16},{1,13},{... | collective-permute-start | bytes 98312 | tf_op jit(solution)/shard_map/ppermute | solution.py:48
  51.1 3.9 %collective-permute-start.11 = (f32[8192]{0:T(1024)S(1)}, f32[8192]{0:T(1024)S(1)}, u32[]{:S(2)}, u32[]{:S(2)}) collective-permute-start(f32[8192]{0:T(1024)S(1)} %bitcast.60), channel_id=1, source_target_pairs={{0,8},{4,12},{8,0},{12,4},{16,24},{20,28},{24,16},{28,20},{1,9},{5... | collective-permute-start | bytes 98312 | tf_op jit(solution)/shard_map/ppermute | solution.py:48
  51.3 4.0 %collective-permute-start.10 = (f32[8192]{0:T(1024)S(1)}, f32[8192]{0:T(1024)S(1)}, u32[]{:S(2)}, u32[]{:S(2)}) collective-permute-start(f32[8192]{0:T(1024)S(1)} %bitcast.61), channel_id=1, source_target_pairs={{0,4},{4,0},{8,12},{12,8},{16,20},{20,16},{24,28},{28,24},{1,5},{5... | collective-permute-start | bytes 98312 | tf_op jit(solution)/shard_map/ppermute | solution.py:48
  55.3 6.0 %collective-permute-start.13 = (f32[8192]{0:T(1024)S(1)}, f32[8192]{0:T(1024)}, u32[]{:S(2)}, u32[]{:S(2)}) collective-permute-start(f32[8192]{0:T(1024)S(1)} %log_add_fusion), channel_id=1, source_target_pairs={{0,16},{4,20},{8,24},{12,28},{16,0},{20,4},{24,8},{28,12},{1,17},{... | collective-permute-start | bytes 98312 | tf_op jit(solution)/shard_map/ppermute | solution.py:48
  72.1 1.7 %collective-permute-start.14 = (f32[2,2,512]{2,1,0:T(2,128)S(1)}, f32[2,2,512]{2,1,0:T(2,128)S(1)}, u32[]{:S(2)}, u32[]{:S(2)}) collective-permute-start(f32[2,2,512]{2,1,0:T(2,128)S(1)} %bitcast.79), channel_id=1, source_target_pairs={{0,1},{1,0},{2,3},{3,2},{4,5},{5,4},{6,7},{7,6},{8,9},{9,8},{10,11... | collective-permute-start | bytes 24584 | tf_op jit(solution)/shard_map/ppermute | solution.py:90
  73.2 2.1 %collective-permute-start.15 = (f32[2,512,128]{2,1,0:T(8,128)S(1)}, f32[2,512,128]{2,1,0:T(8,128)S(1)}, u32[]{:S(2)}, u32[]{:S(2)}) collective-permute-start(f32[2,512,128]{2,1,0:T(8,128)S(1)} %dynamic-slice_bitcast_fusion), channel_id=1, source_target_pairs={{0,1},{1,0},{2,3},{3,2},{4,5},{5,4},{6,7},{7,6},{8,9},{9,8},{10,11... | collective-permute-start | bytes 1572872 | tf_op jit(solution)/shard_map/ppermute | solution.py:91
  73.9 3.7 %collective-permute-start.16 = (f32[2,1,512]{2,1,0:T(1,128)S(1)}, f32[2,1,512]{2,1,0:T(1,128)S(1)}, u32[]{:S(2)}, u32[]{:S(2)}) collective-permute-start(f32[2,1,512]{2,1,0:T(1,128)S(1)} %get-tuple-element.17), channel_id=1, source_target_pairs={{0,2},{1,3},{2,0},{3,1},{4,6},{5,7},{6,4},{7,5},{8,10},{9,11},{10,... | collective-permute-start | bytes 12296 | tf_op jit(solution)/shard_map/ppermute | solution.py:90
  76.7 8.7 %collective-permute-start.17 = (f32[1,512,128]{2,1,0:T(8,128)S(1)}, f32[1,512,128]{2,1,0:T(8,128)S(1)}, u32[]{:S(2)}, u32[]{:S(2)}) collective-permute-start(f32[1,512,128]{2,1,0:T(8,128)S(1)} %constant_dynamic-slice_fusion.1), channel_id=1, source_target_pairs={{0,2},{1,3},{2,0},{3,1},{4,6},{5,7},{6,4},{7,5},{8,10},{9,11},{10,... | collective-permute-start | bytes 786440 | tf_op jit(solution)/shard_map/ppermute | solution.py:91
  (8 other events, 52.1 us)

commit v6 on v4

--- a/solution.py
+++ b/solution.py
@@ -97,7 +97,7 @@
     return (numerator / denominator[..., None]).reshape(rows, -1)
 
 
-CHUNK = 64
+CHUNK = 128
 EXTRA = 16
 VMEM_LIMIT = 24 * 1024 * 1024
 

time: 88 us -> 88.8 us (level)
  Pallas kernels: 32.7 us -> 33.7 us
    pallas_call x5, Pallas kernels: 32.7 us -> 33.7 us  [local_call(): pl.pallas_call(kernel, grid_spec=spec, out_shape=outs, compiler_params=pl...]
  transfers between devices with their start and end apart: 18 -> 18, of which waited for: 14 -> 11; matrix products, arithmetic and copies ran while one was open for 3% -> 3% of each run, Pallas kernels for 0% -> 0%
where the time goes in v6:
time: 88.8 us; the launch traced here: 89.2 us
  Pallas kernels  33.7 us (38%)
  waiting for transfers between devices  25.5 us (29%)
  starting transfers between devices  17.5 us (20%)
  local copies, waits for them, and re-layouts  6.41 us (7%)
  other arithmetic  5.16 us (6%)
  between operations  0.94 us (1%)
    pallas_call x5, Pallas kernels, local_call(): pl.pallas_call(kernel, grid_spec=spec, out_shape=outs, compiler_params=pl...  33.7 us
    ppermute x14, waiting for transfers between devices, exchange(): lax.ppermute(value, axis, [(i, i ^ mask) for i in range(size)])  17 us
    ppermute x14, starting transfers between devices, exchange(): lax.ppermute(value, axis, [(i, i ^ mask) for i in range(size)])  15.2 us
    ppermute x2, waiting for transfers between devices, halving_merge(): num_other = lax.ppermute(num_send, axis, pairs)  8.44 us
    unnamed x31, local copies, waits for them, and re-layouts  5.14 us
  transfers between devices with their start and end apart: 18, of which 11 were waited for; matrix products, arithmetic and copies ran while one was open for 3% of the time, Pallas kernels for 0%

profile of v6, /device:TPU:0, one launch (start us, length us, event | category | flops | bytes accessed | tf_op | source)
XLA Modules:
  0.0 89.2 jit_solution(14577508090423944927)
XLA Ops:
  0.6 1.5 %multiply_reduce_fusion = f32[8192]{0:T(1024)S(1)} fusion(bf16[64,8192]{1,0:T(8,128)(2,1)} %tgt_ref.5), kind=kLoop, calls=%fused_computation | loop fusion | flops 1564672 | bytes 1081344 | tf_op jit(solution)/shard_map/reduce_sum | solution.py:365
  2.2 1.2 %copy-done = bf16[64,8192]{1,0:T(8,128)(2,1)S(1)} copy-done((bf16[64,8192]{1,0:T(8,128)(2,1)S(1)}, bf16[64,8192]{1,0:T(8,128)(2,1)}, u32[]{:S(2)}) %copy-start) | copy-done | bytes 1048600
  5.7 6.1 %shard_map.94 = f32[1,2048]{1,0:T(1,128)S(1)} custom-call(s32[8,8]{1,0:T(8,128)S(1)} %copy-done.7, s32[8]{0:T(128)S(1)} %bitcast.70, bf16[64,2048]{1,0:T(8,128)(2,1)S(1)} %copy-done.2, bf16[64,8192]{1,0:T(8,128)(2,1)S(1)} %copy-done, f32[1,8192]{1,0:T(1,128)S(1)} %bitcast.47, f32[1,8192]{1,0:T(1,128)S(1)} %reshape.179.tpot_ref), custom_call_target="tpu_custom_call" | custom-call | tf_op jit(solution)/shard_map/pallas_call | solution.py:319
  11.8 2.0 %collective-permute-start.2 = (f32[2048]{0:T(1024)S(1)}, f32[2048]{0:T(1024)S(1)}, u32[]{:S(2)}, u32[]{:S(2)}) collective-permute-start(f32[2048]{0:T(1024)S(1)} %bitcast.61), channel_id=1, source_target_pairs={{0,3},{1,2},{2,1},{3,0},{4,7},{5,6},{6,5},{7,4},{8,11},{9,10},{10,... | collective-permute-start | bytes 24584 | tf_op jit(solution)/shard_map/ppermute | solution.py:48
  13.8 1.1 %collective-permute-start.1 = (f32[2048]{0:T(1024)S(1)}, f32[2048]{0:T(1024)S(1)}, u32[]{:S(2)}, u32[]{:S(2)}) collective-permute-start(f32[2048]{0:T(1024)S(1)} %bitcast.62), channel_id=1, source_target_pairs={{0,2},{1,3},{2,0},{3,1},{4,6},{5,7},{6,4},{7,5},{8,10},{9,11},{10,... | collective-permute-start | bytes 24584 | tf_op jit(solution)/shard_map/ppermute | solution.py:48
  15.3 2.2 %collective-permute-done.1 = f32[2048]{0:T(1024)S(1)} collective-permute-done((f32[2048]{0:T(1024)S(1)}, f32[2048]{0:T(1024)S(1)}, u32[]{:S(2)}, u32[]{:S(2)}) %collective-permute-start.1) | collective-permute-done | bytes 8224 | tf_op jit(solution)/shard_map/ppermute | solution.py:48
  17.5 5.6 %shard_map.95 = f32[1,8192]{1,0:T(1,128)S(1)} custom-call(s32[8,8]{1,0:T(8,128)S(1)} %copy-done.7, s32[8]{0:T(128)S(1)} %bitcast.71, bf16[64,2048]{1,0:T(8,128)(2,1)S(1)} %copy-done.2, f32[1,2048]{1,0:T(1,128)S(1)} %bitcast.69, bf16[80,8192]{1,0:T(8,128)(2,1)S(1)} %pad_maximum_fusion.tgt_ref, f32[1,8192]{1,0:T(1,128)S(1)} %bitcast.48), custom_call_target="tpu_custom_call" | custom-call | tf_op jit(solution)/shard_map/pallas_call | solution.py:319
  24.0 3.1 %collective-permute-done.3 = f32[8192]{0:T(1024)S(1)} collective-permute-done((f32[8192]{0:T(1024)S(1)}, f32[8192]{0:T(1024)S(1)}, u32[]{:S(2)}, u32[]{:S(2)}) %collective-permute-start.3) | collective-permute-done | bytes 32800 | tf_op jit(solution)/shard_map/ppermute | solution.py:48
  27.1 3.8 %collective-permute-start.6 = (f32[8192]{0:T(1024)S(1)}, f32[8192]{0:T(1024)S(1)}, u32[]{:S(2)}, u32[]{:S(2)}) collective-permute-start(f32[8192]{0:T(1024)S(1)} %log_add_fusion.1), channel_id=1, source_target_pairs={{0,24},{4,28},{8,16},{12,20},{16,8},{20,12},{24,0},{28,4},{1,25},{... | collective-permute-start | bytes 98312 | tf_op jit(solution)/shard_map/ppermute | solution.py:48
  31.6 1.7 %collective-permute-done.6 = f32[8192]{0:T(1024)S(1)} collective-permute-done((f32[8192]{0:T(1024)S(1)}, f32[8192]{0:T(1024)S(1)}, u32[]{:S(2)}, u32[]{:S(2)}) %collective-permute-start.6) | collective-permute-done | bytes 32800 | tf_op jit(solution)/shard_map/ppermute | solution.py:48
  33.3 2.8 %collective-permute-done.5 = f32[8192]{0:T(1024)S(1)} collective-permute-done((f32[8192]{0:T(1024)S(1)}, f32[8192]{0:T(1024)S(1)}, u32[]{:S(2)}, u32[]{:S(2)}) %collective-permute-start.5) | collective-permute-done | bytes 32800 | tf_op jit(solution)/shard_map/ppermute | solution.py:48
  36.1 6.1 %shard_map.96 = f32[1,2048]{1,0:T(1,128)S(1)} custom-call(s32[8,8]{1,0:T(8,128)S(1)} %copy-done.7, s32[8]{0:T(128)S(1)} %bitcast.72, bf16[64,2048]{1,0:T(8,128)(2,1)S(1)} %copy-done.2, bf16[64,8192]{1,0:T(8,128)(2,1)S(1)} %copy-done.1, f32[1,8192]{1,0:T(1,128)S(1)} %bitcast.49, f32[1,8192]{1,0:T(1,128)S(1)} %bitcast.59), custom_call_target="tpu_custom_call" | custom-call | tf_op jit(solution)/shard_map/pallas_call | solution.py:319
  42.7 1.4 %collective-permute-start.7 = (f32[2048]{0:T(1024)S(1)}, f32[2048]{0:T(1024)S(1)}, u32[]{:S(2)}, u32[]{:S(2)}) collective-permute-start(f32[2048]{0:T(1024)S(1)} %bitcast.67), channel_id=1, source_target_pairs={{0,1},{1,0},{2,3},{3,2},{4,5},{5,4},{6,7},{7,6},{8,9},{9,8},{10,11... | collective-permute-start | bytes 24584 | tf_op jit(solution)/shard_map/ppermute | solution.py:48
  44.1 1.2 %collective-permute-done.9 = f32[2048]{0:T(1024)S(1)} collective-permute-done((f32[2048]{0:T(1024)S(1)}, f32[2048]{0:T(1024)S(1)}, u32[]{:S(2)}, u32[]{:S(2)}) %collective-permute-start.9) | collective-permute-done | bytes 8224 | tf_op jit(solution)/shard_map/ppermute | solution.py:48
  46.1 5.8 %shard_map.97 = f32[1,8192]{1,0:T(1,128)S(1)} custom-call(s32[8,8]{1,0:T(8,128)S(1)} %copy-done.7, s32[8]{0:T(128)S(1)} %bitcast.73, bf16[64,2048]{1,0:T(8,128)(2,1)S(1)} %copy-done.2, f32[1,2048]{1,0:T(1,128)S(1)} %bitcast.60, bf16[80,8192]{1,0:T(8,128)(2,1)S(1)} %pad_maximum_fusion.tgt_ref, f32[1,8192]{1,0:T(1,128)S(1)} %bitcast.50), custom_call_target="tpu_custom_call" | custom-call | tf_op jit(solution)/shard_map/pallas_call | solution.py:319
  52.2 3.6 %collective-permute-done.10 = f32[8192]{0:T(1024)S(1)} collective-permute-done((f32[8192]{0:T(1024)S(1)}, f32[8192]{0:T(1024)S(1)}, u32[]{:S(2)}, u32[]{:S(2)}) %collective-permute-start.10) | collective-permute-done | bytes 32800 | tf_op jit(solution)/shard_map/ppermute | solution.py:48
  56.5 2.2 %collective-permute-start.12 = (f32[8192]{0:T(1024)S(1)}, f32[8192]{0:T(1024)}, u32[]{:S(2)}, u32[]{:S(2)}) collective-permute-start(f32[8192]{0:T(1024)S(1)} %log_add_fusion), channel_id=1, source_target_pairs={{0,16},{4,20},{8,24},{12,28},{16,0},{20,4},{24,8},{28,12},{1,17},{... | collective-permute-start | bytes 98312 | tf_op jit(solution)/shard_map/ppermute | solution.py:48
  58.7 1.6 %collective-permute-start.11 = (f32[8192]{0:T(1024)S(1)}, f32[8192]{0:T(1024)}, u32[]{:S(2)}, u32[]{:S(2)}) collective-permute-start(f32[8192]{0:T(1024)S(1)} %log_add_fusion), channel_id=1, source_target_pairs={{0,8},{4,12},{8,0},{12,4},{16,24},{20,28},{24,16},{28,20},{1,9},{5... | collective-permute-start | bytes 98312 | tf_op jit(solution)/shard_map/ppermute | solution.py:48
  60.3 1.4 %collective-permute-done.13 = f32[8192]{0:T(1024)S(1)} collective-permute-done((f32[8192]{0:T(1024)S(1)}, f32[8192]{0:T(1024)S(1)}, u32[]{:S(2)}, u32[]{:S(2)}) %collective-permute-start.13) | collective-permute-done | bytes 32800 | tf_op jit(solution)/shard_map/ppermute | solution.py:48
  63.6 10.2 %shard_map.98 = (f32[2,2048]{1,0:T(2,128)S(1)}, f32[2048,128]{1,0:T(8,128)S(1)}) custom-call(s32[8,8]{1,0:T(8,128)S(1)} %copy-done.8, s32[8]{0:T(128)S(1)} %bitcast.74, bf16[64,2048]{1,0:T(8,128)(2,1)S(1)} %copy-done.3, bf16[64,8192]{1,0:T(8,128)(2,1)S(1)} %copy-done.1, f32[1,8192]{1,0:T(1,128)S(1)} %bitcast.51, f32[1,8192]{1,0:T(1,128)S(1)} %bitcast.54, ...), custom_call_target="tpu_custom_call" | custom-call | tf_op jit(solution)/shard_map/pallas_call | solution.py:319
  74.9 1.1 %dynamic-slice_bitcast_fusion = f32[2,512,128]{2,1,0:T(8,128)S(1)} fusion(f32[2,2,512,128]{3,2,1,0:T(8,128)} %bitcast.52, s32[]{:T(128)S(6)} %select_n.44), kind=kLoop, calls=%fused_computation.4 | loop fusion | bytes 1048580 | tf_op jit(solution)/shard_map/jit(dynamic_index_in_dim)/squeeze | solution.py:82
  78.1 1.4 %fusion = f32[2,512,128]{2,1,0:T(8,128)S(1)} fusion(f32[2,512,128]{2,1,0:T(8,128)S(1)} %collective-permute-done.15, f32[2,2,512,128]{3,2,1,0:T(8,128)} %bitcast.53, s32[]{:T(128)S(6)} %select_n.43, f32[2,512]{1,0:T(2,128)S(1)} %get-tuple-element.15, f32[2,512]{1,0:T(2,128)S(1)} %get-tuple-element.14), kind=kLoop, calls=%fused_computation.3 | loop fusion | flops 393216 | bytes 1581060 | tf_op jit(solution)/shard_map/add | solution.py:92
  80.4 7.8 %collective-permute-done.17 = f32[1,512,128]{2,1,0:T(8,128)S(1)} collective-permute-done((f32[1,512,128]{2,1,0:T(8,128)S(1)}, f32[1,512,128]{2,1,0:T(8,128)S(1)}, u32[]{:S(2)}, u32[]{:S(2)}) %collective-permute-start.17) | collective-permute-done | bytes 262176 | tf_op jit(solution)/shard_map/ppermute | solution.py:88
  88.2 1.0 %divide_bitcast_fusion = f32[512,128]{1,0:T(8,128)} fusion(f32[1,512,128]{2,1,0:T(8,128)S(1)} %collective-permute-done.17, f32[2,512,128]{2,1,0:T(8,128)S(1)} %fusion, s32[]{:T(128)S(6)} %select_n.47, f32[512]{0:T(512)S(1)} %get-tuple-element.7, f32[512]{0:T(512)S(1)} %get-tuple-element.9, f32[512]{0:T(512)S(1)} %get-tuple-element.8), kind=kLoop, calls=%fused_computation.5 | loop fusion | flops 262144 | bytes 792580 | tf_op jit(solution)/shard_map/reshape | solution.py:97
  (72 shorter events, 12.6 us)
Async XLA Ops:
  11.8 24.3 %copy-start.12 = (f32[8192]{0:T(1024)S(1)}, f32[8192]{0:T(1024)}, u32[]{:S(2)}) copy-start(f32[8192]{0:T(1024)} %param.11) | copy-start | bytes 98308
  11.8 3.5 %collective-permute-start.2 = (f32[2048]{0:T(1024)S(1)}, f32[2048]{0:T(1024)S(1)}, u32[]{:S(2)}, u32[]{:S(2)}) collective-permute-start(f32[2048]{0:T(1024)S(1)} %bitcast.61), channel_id=1, source_target_pairs={{0,3},{1,2},{2,1},{3,0},{4,7},{5,6},{6,5},{7,4},{8,11},{9,10},{10,... | collective-permute-start | bytes 24584 | tf_op jit(solution)/shard_map/ppermute | solution.py:48
  13.8 3.7 %collective-permute-start.1 = (f32[2048]{0:T(1024)S(1)}, f32[2048]{0:T(1024)S(1)}, u32[]{:S(2)}, u32[]{:S(2)}) collective-permute-start(f32[2048]{0:T(1024)S(1)} %bitcast.62), channel_id=1, source_target_pairs={{0,2},{1,3},{2,0},{3,1},{4,6},{5,7},{6,4},{7,5},{8,10},{9,11},{10,... | collective-permute-start | bytes 24584 | tf_op jit(solution)/shard_map/ppermute | solution.py:48
  14.9 2.6 %collective-permute-start = (f32[2048]{0:T(1024)S(1)}, f32[2048]{0:T(1024)S(1)}, u32[]{:S(2)}, u32[]{:S(2)}) collective-permute-start(f32[2048]{0:T(1024)S(1)} %bitcast.63), channel_id=1, source_target_pairs={{0,1},{1,0},{2,3},{3,2},{4,5},{5,4},{6,7},{7,6},{8,9},{9,8},{10,11... | collective-permute-start | bytes 24584 | tf_op jit(solution)/shard_map/ppermute | solution.py:48
  23.1 40.5 %copy-start.3 = (bf16[64,2048]{1,0:T(8,128)(2,1)S(1)}, bf16[64,2048]{1,0:T(8,128)(2,1)}, u32[]{:S(2)}) copy-start(bf16[64,2048]{1,0:T(8,128)(2,1)} %src_ref.9) | copy-start | bytes 786436
  23.1 40.5 %copy-start.4 = (bf16[128,8192]{1,0:T(8,128)(2,1)S(1)}, bf16[128,8192]{1,0:T(8,128)(2,1)}, u32[]{:S(2)}) copy-start(bf16[128,8192]{1,0:T(8,128)(2,1)} %feat_ref.1) | copy-start | bytes 6291460
  23.1 40.5 %copy-start.8 = (s32[8,8]{1,0:T(8,128)S(1)}, s32[8,8]{1,0:T(8,128)}, u32[]{:S(2)}) copy-start(s32[8,8]{1,0:T(8,128)} %blocks_ref.9) | copy-start | bytes 772
  23.1 40.5 %copy-start.11 = (s32[8,1]{0,1:T(1,128)S(1)}, s32[8,1]{0,1:T(1,128)}, u32[]{:S(2)}) copy-start(s32[8,1]{0,1:T(1,128)} %param.13) | copy-start | bytes 100
  23.1 4.0 %collective-permute-start.3 = (f32[8192]{0:T(1024)S(1)}, f32[8192]{0:T(1024)S(1)}, u32[]{:S(2)}, u32[]{:S(2)}) collective-permute-start(f32[8192]{0:T(1024)S(1)} %bitcast.55), channel_id=1, source_target_pairs={{0,4},{4,0},{8,12},{12,8},{16,20},{20,16},{24,28},{28,24},{1,5},{5... | collective-permute-start | bytes 98312 | tf_op jit(solution)/shard_map/ppermute | solution.py:48
  27.1 6.2 %collective-permute-start.6 = (f32[8192]{0:T(1024)S(1)}, f32[8192]{0:T(1024)S(1)}, u32[]{:S(2)}, u32[]{:S(2)}) collective-permute-start(f32[8192]{0:T(1024)S(1)} %log_add_fusion.1), channel_id=1, source_target_pairs={{0,24},{4,28},{8,16},{12,20},{16,8},{20,12},{24,0},{28,4},{1,25},{... | collective-permute-start | bytes 98312 | tf_op jit(solution)/shard_map/ppermute | solution.py:48
  30.9 5.2 %collective-permute-start.5 = (f32[8192]{0:T(1024)S(1)}, f32[8192]{0:T(1024)S(1)}, u32[]{:S(2)}, u32[]{:S(2)}) collective-permute-start(f32[8192]{0:T(1024)S(1)} %log_add_fusion.1), channel_id=1, source_target_pairs={{0,16},{4,20},{8,24},{12,28},{16,0},{20,4},{24,8},{28,12},{1,17},{... | collective-permute-start | bytes 98312 | tf_op jit(solution)/shard_map/ppermute | solution.py:48
  31.0 5.1 %collective-permute-start.4 = (f32[8192]{0:T(1024)S(1)}, f32[8192]{0:T(1024)S(1)}, u32[]{:S(2)}, u32[]{:S(2)}) collective-permute-start(f32[8192]{0:T(1024)S(1)} %log_add_fusion.1), channel_id=1, source_target_pairs={{0,8},{4,12},{8,0},{12,4},{16,24},{20,28},{24,16},{28,20},{1,9},{5... | collective-permute-start | bytes 98312 | tf_op jit(solution)/shard_map/ppermute | solution.py:48
  42.2 3.1 %collective-permute-start.9 = (f32[2048]{0:T(1024)S(1)}, f32[2048]{0:T(1024)S(1)}, u32[]{:S(2)}, u32[]{:S(2)}) collective-permute-start(f32[2048]{0:T(1024)S(1)} %bitcast.65), channel_id=1, source_target_pairs={{0,3},{1,2},{2,1},{3,0},{4,7},{5,6},{6,5},{7,4},{8,11},{9,10},{10,... | collective-permute-start | bytes 24584 | tf_op jit(solution)/shard_map/ppermute | solution.py:48
  42.3 3.7 %collective-permute-start.8 = (f32[2048]{0:T(1024)S(1)}, f32[2048]{0:T(1024)S(1)}, u32[]{:S(2)}, u32[]{:S(2)}) collective-permute-start(f32[2048]{0:T(1024)S(1)} %bitcast.66), channel_id=1, source_target_pairs={{0,2},{1,3},{2,0},{3,1},{4,6},{5,7},{6,4},{7,5},{8,10},{9,11},{10,... | collective-permute-start | bytes 24584 | tf_op jit(solution)/shard_map/ppermute | solution.py:48
  42.7 3.3 %collective-permute-start.7 = (f32[2048]{0:T(1024)S(1)}, f32[2048]{0:T(1024)S(1)}, u32[]{:S(2)}, u32[]{:S(2)}) collective-permute-start(f32[2048]{0:T(1024)S(1)} %bitcast.67), channel_id=1, source_target_pairs={{0,1},{1,0},{2,3},{3,2},{4,5},{5,4},{6,7},{7,6},{8,9},{9,8},{10,11... | collective-permute-start | bytes 24584 | tf_op jit(solution)/shard_map/ppermute | solution.py:48
  46.0 27.8 %copy-start.9 = (f32[2048]{0:T(1024)}, f32[2048]{0:T(1024)S(1)}, u32[]{:S(2)}) copy-start(f32[2048]{0:T(1024)S(1)} %multiply_subtract_fusion.2) | copy-start | bytes 24580
  51.8 4.0 %collective-permute-start.10 = (f32[8192]{0:T(1024)S(1)}, f32[8192]{0:T(1024)S(1)}, u32[]{:S(2)}, u32[]{:S(2)}) collective-permute-start(f32[8192]{0:T(1024)S(1)} %bitcast.57), channel_id=1, source_target_pairs={{0,4},{4,0},{8,12},{12,8},{16,20},{20,16},{24,28},{28,24},{1,5},{5... | collective-permute-start | bytes 98312 | tf_op jit(solution)/shard_map/ppermute | solution.py:48
  55.9 5.8 %collective-permute-start.13 = (f32[8192]{0:T(1024)S(1)}, f32[8192]{0:T(1024)S(1)}, u32[]{:S(2)}, u32[]{:S(2)}) collective-permute-start(f32[8192]{0:T(1024)S(1)} %log_add_fusion), channel_id=1, source_target_pairs={{0,24},{4,28},{8,16},{12,20},{16,8},{20,12},{24,0},{28,4},{1,25},{... | collective-permute-start | bytes 98312 | tf_op jit(solution)/shard_map/ppermute | solution.py:48
  56.5 5.2 %collective-permute-start.12 = (f32[8192]{0:T(1024)S(1)}, f32[8192]{0:T(1024)}, u32[]{:S(2)}, u32[]{:S(2)}) collective-permute-start(f32[8192]{0:T(1024)S(1)} %log_add_fusion), channel_id=1, source_target_pairs={{0,16},{4,20},{8,24},{12,28},{16,0},{20,4},{24,8},{28,12},{1,17},{... | collective-permute-start | bytes 98312 | tf_op jit(solution)/shard_map/ppermute | solution.py:48
  58.7 4.0 %collective-permute-start.11 = (f32[8192]{0:T(1024)S(1)}, f32[8192]{0:T(1024)}, u32[]{:S(2)}, u32[]{:S(2)}) collective-permute-start(f32[8192]{0:T(1024)S(1)} %log_add_fusion), channel_id=1, source_target_pairs={{0,8},{4,12},{8,0},{12,4},{16,24},{20,28},{24,16},{28,20},{1,9},{5... | collective-permute-start | bytes 98312 | tf_op jit(solution)/shard_map/ppermute | solution.py:48
  74.9 1.7 %collective-permute-start.14 = (f32[2,2,512]{2,1,0:T(2,128)S(1)}, f32[2,2,512]{2,1,0:T(2,128)S(1)}, u32[]{:S(2)}, u32[]{:S(2)}) collective-permute-start(f32[2,2,512]{2,1,0:T(2,128)S(1)} %bitcast.75), channel_id=1, source_target_pairs={{0,1},{1,0},{2,3},{3,2},{4,5},{5,4},{6,7},{7,6},{8,9},{9,8},{10,11... | collective-permute-start | bytes 24584 | tf_op jit(solution)/shard_map/ppermute | solution.py:87
  76.0 2.1 %collective-permute-start.15 = (f32[2,512,128]{2,1,0:T(8,128)S(1)}, f32[2,512,128]{2,1,0:T(8,128)S(1)}, u32[]{:S(2)}, u32[]{:S(2)}) collective-permute-start(f32[2,512,128]{2,1,0:T(8,128)S(1)} %dynamic-slice_bitcast_fusion), channel_id=1, source_target_pairs={{0,1},{1,0},{2,3},{3,2},{4,5},{5,4},{6,7},{7,6},{8,9},{9,8},{10,11... | collective-permute-start | bytes 1572872 | tf_op jit(solution)/shard_map/ppermute | solution.py:88
  76.7 3.7 %collective-permute-start.16 = (f32[2,1,512]{2,1,0:T(1,128)S(1)}, f32[2,1,512]{2,1,0:T(1,128)S(1)}, u32[]{:S(2)}, u32[]{:S(2)}) collective-permute-start(f32[2,1,512]{2,1,0:T(1,128)S(1)} %get-tuple-element.17), channel_id=1, source_target_pairs={{0,2},{1,3},{2,0},{3,1},{4,6},{5,7},{6,4},{7,5},{8,10},{9,11},{10,... | collective-permute-start | bytes 12296 | tf_op jit(solution)/shard_map/ppermute | solution.py:87
  79.5 8.7 %collective-permute-start.17 = (f32[1,512,128]{2,1,0:T(8,128)S(1)}, f32[1,512,128]{2,1,0:T(8,128)S(1)}, u32[]{:S(2)}, u32[]{:S(2)}) collective-permute-start(f32[1,512,128]{2,1,0:T(8,128)S(1)} %constant_dynamic-slice_fusion.1), channel_id=1, source_target_pairs={{0,2},{1,3},{2,0},{3,1},{4,6},{5,7},{6,4},{7,5},{8,10},{9,11},{10,... | collective-permute-start | bytes 786440 | tf_op jit(solution)/shard_map/ppermute | solution.py:88
  (9 other events, 54.0 us)

commit v7 on v6

--- a/solution.py
+++ b/solution.py
@@ -97,7 +97,7 @@
     return (numerator / denominator[..., None]).reshape(rows, -1)
 
 
-CHUNK = 128
+CHUNK = 32
 EXTRA = 16
 VMEM_LIMIT = 24 * 1024 * 1024
 

time: 88.8 us -> 87.6 us (0.986)
  waiting for transfers between devices: 25.5 us -> 22.5 us
  starting transfers between devices: 17.5 us -> 18.9 us
    ppermute x14, waiting for transfers between devices: 17 us -> 13.3 us  [exchange(): lax.ppermute(value, axis, [(i, i ^ mask) for i in range(size)])]
    ppermute x14, starting transfers between devices: 15.2 us -> 17.4 us  [exchange(): lax.ppermute(value, axis, [(i, i ^ mask) for i in range(size)])]
  transfers between devices with their start and end apart: 18 -> 18, of which waited for: 11 -> 13; matrix products, arithmetic and copies ran while one was open for 3% -> 3% of each run, Pallas kernels for 0% -> 0%
where the time goes in v7:
time: 87.6 us; the launch traced here: 87.7 us
  Pallas kernels  33.8 us (39%)
  waiting for transfers between devices  22.5 us (26%)
  starting transfers between devices  18.9 us (22%)
  local copies, waits for them, and re-layouts  6.41 us (7%)
  other arithmetic  5.16 us (6%)
  between operations  0.96 us (1%)
    pallas_call x5, Pallas kernels, local_call(): pl.pallas_call(kernel, grid_spec=spec, out_shape=outs, compiler_params=pl...  33.8 us
    ppermute x14, starting transfers between devices, exchange(): lax.ppermute(value, axis, [(i, i ^ mask) for i in range(size)])  17.4 us
    ppermute x14, waiting for transfers between devices, exchange(): lax.ppermute(value, axis, [(i, i ^ mask) for i in range(size)])  13.3 us
    ppermute x2, waiting for transfers between devices, halving_merge(): num_other = lax.ppermute(num_send, axis, pairs)  9.18 us
    unnamed x31, local copies, waits for them, and re-layouts  5.14 us
  transfers between devices with their start and end apart: 18, of which 13 were waited for; matrix products, arithmetic and copies ran while one was open for 3% of the time, Pallas kernels for 0%

profile of v7, /device:TPU:0, one launch (start us, length us, event | category | flops | bytes accessed | tf_op | source)
XLA Modules:
  0.0 87.7 jit_solution(18116148116821793015)
XLA Ops:
  0.6 1.5 %multiply_reduce_fusion = f32[8192]{0:T(1024)S(1)} fusion(bf16[64,8192]{1,0:T(8,128)(2,1)} %tgt_ref.5), kind=kLoop, calls=%fused_computation | loop fusion | flops 1564672 | bytes 1081344 | tf_op jit(solution)/shard_map/reduce_sum | solution.py:365
  2.2 1.2 %copy-done = bf16[64,8192]{1,0:T(8,128)(2,1)S(1)} copy-done((bf16[64,8192]{1,0:T(8,128)(2,1)S(1)}, bf16[64,8192]{1,0:T(8,128)(2,1)}, u32[]{:S(2)}) %copy-start) | copy-done | bytes 1048600
  5.7 6.0 %shard_map.94 = f32[1,2048]{1,0:T(1,128)S(1)} custom-call(s32[8,8]{1,0:T(8,128)S(1)} %copy-done.7, s32[8]{0:T(128)S(1)} %bitcast.70, bf16[64,2048]{1,0:T(8,128)(2,1)S(1)} %copy-done.2, bf16[64,8192]{1,0:T(8,128)(2,1)S(1)} %copy-done, f32[1,8192]{1,0:T(1,128)S(1)} %bitcast.47, f32[1,8192]{1,0:T(1,128)S(1)} %reshape.179.tpot_ref), custom_call_target="tpu_custom_call" | custom-call | tf_op jit(solution)/shard_map/pallas_call | solution.py:319
  11.7 2.5 %collective-permute-start.2 = (f32[2048]{0:T(1024)S(1)}, f32[2048]{0:T(1024)S(1)}, u32[]{:S(2)}, u32[]{:S(2)}) collective-permute-start(f32[2048]{0:T(1024)S(1)} %bitcast.61), channel_id=1, source_target_pairs={{0,3},{1,2},{2,1},{3,0},{4,7},{5,6},{6,5},{7,4},{8,11},{9,10},{10,... | collective-permute-start | bytes 24584 | tf_op jit(solution)/shard_map/ppermute | solution.py:48
  15.6 2.3 %collective-permute-done.1 = f32[2048]{0:T(1024)S(1)} collective-permute-done((f32[2048]{0:T(1024)S(1)}, f32[2048]{0:T(1024)S(1)}, u32[]{:S(2)}, u32[]{:S(2)}) %collective-permute-start.1) | collective-permute-done | bytes 8224 | tf_op jit(solution)/shard_map/ppermute | solution.py:48
  18.0 5.7 %shard_map.95 = f32[1,8192]{1,0:T(1,128)S(1)} custom-call(s32[8,8]{1,0:T(8,128)S(1)} %copy-done.7, s32[8]{0:T(128)S(1)} %bitcast.71, bf16[64,2048]{1,0:T(8,128)(2,1)S(1)} %copy-done.2, f32[1,2048]{1,0:T(1,128)S(1)} %bitcast.69, bf16[80,8192]{1,0:T(8,128)(2,1)S(1)} %pad_maximum_fusion.tgt_ref, f32[1,8192]{1,0:T(1,128)S(1)} %bitcast.48), custom_call_target="tpu_custom_call" | custom-call | tf_op jit(solution)/shard_map/pallas_call | solution.py:319
  23.7 1.6 %collective-permute-start.3 = (f32[8192]{0:T(1024)S(1)}, f32[8192]{0:T(1024)S(1)}, u32[]{:S(2)}, u32[]{:S(2)}) collective-permute-start(f32[8192]{0:T(1024)S(1)} %bitcast.55), channel_id=1, source_target_pairs={{0,4},{4,0},{8,12},{12,8},{16,20},{20,16},{24,28},{28,24},{1,5},{5... | collective-permute-start | bytes 98312 | tf_op jit(solution)/shard_map/ppermute | solution.py:48
  25.4 2.3 %collective-permute-done.3 = f32[8192]{0:T(1024)S(1)} collective-permute-done((f32[8192]{0:T(1024)S(1)}, f32[8192]{0:T(1024)S(1)}, u32[]{:S(2)}, u32[]{:S(2)}) %collective-permute-start.3) | collective-permute-done | bytes 32800 | tf_op jit(solution)/shard_map/ppermute | solution.py:48
  27.7 2.4 %collective-permute-start.6 = (f32[8192]{0:T(1024)S(1)}, f32[8192]{0:T(1024)S(1)}, u32[]{:S(2)}, u32[]{:S(2)}) collective-permute-start(f32[8192]{0:T(1024)S(1)} %log_add_fusion.1), channel_id=1, source_target_pairs={{0,24},{4,28},{8,16},{12,20},{16,8},{20,12},{24,0},{28,4},{1,25},{... | collective-permute-start | bytes 98312 | tf_op jit(solution)/shard_map/ppermute | solution.py:48
  30.1 2.1 %collective-permute-start.4 = (f32[8192]{0:T(1024)S(1)}, f32[8192]{0:T(1024)S(1)}, u32[]{:S(2)}, u32[]{:S(2)}) collective-permute-start(f32[8192]{0:T(1024)S(1)} %log_add_fusion.1), channel_id=1, source_target_pairs={{0,8},{4,12},{8,0},{12,4},{16,24},{20,28},{24,16},{28,20},{1,9},{5... | collective-permute-start | bytes 98312 | tf_op jit(solution)/shard_map/ppermute | solution.py:48
  32.2 1.3 %collective-permute-done.6 = f32[8192]{0:T(1024)S(1)} collective-permute-done((f32[8192]{0:T(1024)S(1)}, f32[8192]{0:T(1024)S(1)}, u32[]{:S(2)}, u32[]{:S(2)}) %collective-permute-start.6) | collective-permute-done | bytes 32800 | tf_op jit(solution)/shard_map/ppermute | solution.py:48
  33.5 1.4 %collective-permute-done.5 = f32[8192]{0:T(1024)S(1)} collective-permute-done((f32[8192]{0:T(1024)S(1)}, f32[8192]{0:T(1024)S(1)}, u32[]{:S(2)}, u32[]{:S(2)}) %collective-permute-start.5) | collective-permute-done | bytes 32800 | tf_op jit(solution)/shard_map/ppermute | solution.py:48
  35.0 6.0 %shard_map.96 = f32[1,2048]{1,0:T(1,128)S(1)} custom-call(s32[8,8]{1,0:T(8,128)S(1)} %copy-done.7, s32[8]{0:T(128)S(1)} %bitcast.72, bf16[64,2048]{1,0:T(8,128)(2,1)S(1)} %copy-done.2, bf16[64,8192]{1,0:T(8,128)(2,1)S(1)} %copy-done.1, f32[1,8192]{1,0:T(1,128)S(1)} %bitcast.49, f32[1,8192]{1,0:T(1,128)S(1)} %bitcast.59), custom_call_target="tpu_custom_call" | custom-call | tf_op jit(solution)/shard_map/pallas_call | solution.py:319
  41.2 1.8 %collective-permute-start.7 = (f32[2048]{0:T(1024)S(1)}, f32[2048]{0:T(1024)S(1)}, u32[]{:S(2)}, u32[]{:S(2)}) collective-permute-start(f32[2048]{0:T(1024)S(1)} %bitcast.67), channel_id=1, source_target_pairs={{0,1},{1,0},{2,3},{3,2},{4,5},{5,4},{6,7},{7,6},{8,9},{9,8},{10,11... | collective-permute-start | bytes 24584 | tf_op jit(solution)/shard_map/ppermute | solution.py:48
  43.0 1.2 %collective-permute-done.9 = f32[2048]{0:T(1024)S(1)} collective-permute-done((f32[2048]{0:T(1024)S(1)}, f32[2048]{0:T(1024)S(1)}, u32[]{:S(2)}, u32[]{:S(2)}) %collective-permute-start.9) | collective-permute-done | bytes 8224 | tf_op jit(solution)/shard_map/ppermute | solution.py:48
  44.9 5.9 %shard_map.97 = f32[1,8192]{1,0:T(1,128)S(1)} custom-call(s32[8,8]{1,0:T(8,128)S(1)} %copy-done.7, s32[8]{0:T(128)S(1)} %bitcast.73, bf16[64,2048]{1,0:T(8,128)(2,1)S(1)} %copy-done.2, f32[1,2048]{1,0:T(1,128)S(1)} %bitcast.60, bf16[80,8192]{1,0:T(8,128)(2,1)S(1)} %pad_maximum_fusion.tgt_ref, f32[1,8192]{1,0:T(1,128)S(1)} %bitcast.50), custom_call_target="tpu_custom_call" | custom-call | tf_op jit(solution)/shard_map/pallas_call | solution.py:319
  50.8 2.2 %collective-permute-start.10 = (f32[8192]{0:T(1024)S(1)}, f32[8192]{0:T(1024)S(1)}, u32[]{:S(2)}, u32[]{:S(2)}) collective-permute-start(f32[8192]{0:T(1024)S(1)} %bitcast.57), channel_id=1, source_target_pairs={{0,4},{4,0},{8,12},{12,8},{16,20},{20,16},{24,28},{28,24},{1,5},{5... | collective-permute-start | bytes 98312 | tf_op jit(solution)/shard_map/ppermute | solution.py:48
  53.0 1.9 %collective-permute-done.10 = f32[8192]{0:T(1024)S(1)} collective-permute-done((f32[8192]{0:T(1024)S(1)}, f32[8192]{0:T(1024)S(1)}, u32[]{:S(2)}, u32[]{:S(2)}) %collective-permute-start.10) | collective-permute-done | bytes 32800 | tf_op jit(solution)/shard_map/ppermute | solution.py:48
  55.5 3.8 %collective-permute-start.11 = (f32[8192]{0:T(1024)S(1)}, f32[8192]{0:T(1024)}, u32[]{:S(2)}, u32[]{:S(2)}) collective-permute-start(f32[8192]{0:T(1024)S(1)} %log_add_fusion), channel_id=1, source_target_pairs={{0,8},{4,12},{8,0},{12,4},{16,24},{20,28},{24,16},{28,20},{1,9},{5... | collective-permute-start | bytes 98312 | tf_op jit(solution)/shard_map/ppermute | solution.py:48
  59.4 1.3 %collective-permute-done.13 = f32[8192]{0:T(1024)S(1)} collective-permute-done((f32[8192]{0:T(1024)S(1)}, f32[8192]{0:T(1024)S(1)}, u32[]{:S(2)}, u32[]{:S(2)}) %collective-permute-start.13) | collective-permute-done | bytes 32800 | tf_op jit(solution)/shard_map/ppermute | solution.py:48
  62.2 10.1 %shard_map.98 = (f32[2,2048]{1,0:T(2,128)S(1)}, f32[2048,128]{1,0:T(8,128)S(1)}) custom-call(s32[8,8]{1,0:T(8,128)S(1)} %copy-done.8, s32[8]{0:T(128)S(1)} %bitcast.74, bf16[64,2048]{1,0:T(8,128)(2,1)S(1)} %copy-done.3, bf16[64,8192]{1,0:T(8,128)(2,1)S(1)} %copy-done.1, f32[1,8192]{1,0:T(1,128)S(1)} %bitcast.51, f32[1,8192]{1,0:T(1,128)S(1)} %bitcast.54, ...), custom_call_target="tpu_custom_call" | custom-call | tf_op jit(solution)/shard_map/pallas_call | solution.py:319
  75.3 1.3 %collective-permute-done.15 = f32[2,512,128]{2,1,0:T(8,128)S(1)} collective-permute-done((f32[2,512,128]{2,1,0:T(8,128)S(1)}, f32[2,512,128]{2,1,0:T(8,128)S(1)}, u32[]{:S(2)}, u32[]{:S(2)}) %collective-permute-start.15) | collective-permute-done | bytes 524320 | tf_op jit(solution)/shard_map/ppermute | solution.py:88
  76.6 1.4 %fusion = f32[2,512,128]{2,1,0:T(8,128)S(1)} fusion(f32[2,512,128]{2,1,0:T(8,128)S(1)} %collective-permute-done.15, f32[2,2,512,128]{3,2,1,0:T(8,128)} %bitcast.53, s32[]{:T(128)S(6)} %select_n.43, f32[2,512]{1,0:T(2,128)S(1)} %get-tuple-element.15, f32[2,512]{1,0:T(2,128)S(1)} %get-tuple-element.14), kind=kLoop, calls=%fused_computation.3 | loop fusion | flops 393216 | bytes 1581060 | tf_op jit(solution)/shard_map/add | solution.py:92
  78.9 7.8 %collective-permute-done.17 = f32[1,512,128]{2,1,0:T(8,128)S(1)} collective-permute-done((f32[1,512,128]{2,1,0:T(8,128)S(1)}, f32[1,512,128]{2,1,0:T(8,128)S(1)}, u32[]{:S(2)}, u32[]{:S(2)}) %collective-permute-start.17) | collective-permute-done | bytes 262176 | tf_op jit(solution)/shard_map/ppermute | solution.py:88
  (72 shorter events, 11.5 us)
Async XLA Ops:
  11.7 23.2 %copy-start.12 = (f32[8192]{0:T(1024)S(1)}, f32[8192]{0:T(1024)}, u32[]{:S(2)}) copy-start(f32[8192]{0:T(1024)} %param.11) | copy-start | bytes 98308
  11.7 3.9 %collective-permute-start.2 = (f32[2048]{0:T(1024)S(1)}, f32[2048]{0:T(1024)S(1)}, u32[]{:S(2)}, u32[]{:S(2)}) collective-permute-start(f32[2048]{0:T(1024)S(1)} %bitcast.61), channel_id=1, source_target_pairs={{0,3},{1,2},{2,1},{3,0},{4,7},{5,6},{6,5},{7,4},{8,11},{9,10},{10,... | collective-permute-start | bytes 24584 | tf_op jit(solution)/shard_map/ppermute | solution.py:48
  14.3 3.7 %collective-permute-start.1 = (f32[2048]{0:T(1024)S(1)}, f32[2048]{0:T(1024)S(1)}, u32[]{:S(2)}, u32[]{:S(2)}) collective-permute-start(f32[2048]{0:T(1024)S(1)} %bitcast.62), channel_id=1, source_target_pairs={{0,2},{1,3},{2,0},{3,1},{4,6},{5,7},{6,4},{7,5},{8,10},{9,11},{10,... | collective-permute-start | bytes 24584 | tf_op jit(solution)/shard_map/ppermute | solution.py:48
  14.3 3.7 %collective-permute-start = (f32[2048]{0:T(1024)S(1)}, f32[2048]{0:T(1024)S(1)}, u32[]{:S(2)}, u32[]{:S(2)}) collective-permute-start(f32[2048]{0:T(1024)S(1)} %bitcast.63), channel_id=1, source_target_pairs={{0,1},{1,0},{2,3},{3,2},{4,5},{5,4},{6,7},{7,6},{8,9},{9,8},{10,11... | collective-permute-start | bytes 24584 | tf_op jit(solution)/shard_map/ppermute | solution.py:48
  23.7 38.5 %copy-start.3 = (bf16[64,2048]{1,0:T(8,128)(2,1)S(1)}, bf16[64,2048]{1,0:T(8,128)(2,1)}, u32[]{:S(2)}) copy-start(bf16[64,2048]{1,0:T(8,128)(2,1)} %src_ref.9) | copy-start | bytes 786436
  23.7 38.5 %copy-start.4 = (bf16[128,8192]{1,0:T(8,128)(2,1)S(1)}, bf16[128,8192]{1,0:T(8,128)(2,1)}, u32[]{:S(2)}) copy-start(bf16[128,8192]{1,0:T(8,128)(2,1)} %feat_ref.1) | copy-start | bytes 6291460
  23.7 38.5 %copy-start.8 = (s32[8,8]{1,0:T(8,128)S(1)}, s32[8,8]{1,0:T(8,128)}, u32[]{:S(2)}) copy-start(s32[8,8]{1,0:T(8,128)} %blocks_ref.9) | copy-start | bytes 772
  23.7 38.5 %copy-start.11 = (s32[8,1]{0,1:T(1,128)S(1)}, s32[8,1]{0,1:T(1,128)}, u32[]{:S(2)}) copy-start(s32[8,1]{0,1:T(1,128)} %param.13) | copy-start | bytes 100
  23.7 4.0 %collective-permute-start.3 = (f32[8192]{0:T(1024)S(1)}, f32[8192]{0:T(1024)S(1)}, u32[]{:S(2)}, u32[]{:S(2)}) collective-permute-start(f32[8192]{0:T(1024)S(1)} %bitcast.55), channel_id=1, source_target_pairs={{0,4},{4,0},{8,12},{12,8},{16,20},{20,16},{24,28},{28,24},{1,5},{5... | collective-permute-start | bytes 98312 | tf_op jit(solution)/shard_map/ppermute | solution.py:48
  27.7 5.8 %collective-permute-start.6 = (f32[8192]{0:T(1024)S(1)}, f32[8192]{0:T(1024)S(1)}, u32[]{:S(2)}, u32[]{:S(2)}) collective-permute-start(f32[8192]{0:T(1024)S(1)} %log_add_fusion.1), channel_id=1, source_target_pairs={{0,24},{4,28},{8,16},{12,20},{16,8},{20,12},{24,0},{28,4},{1,25},{... | collective-permute-start | bytes 98312 | tf_op jit(solution)/shard_map/ppermute | solution.py:48
  30.1 4.8 %collective-permute-start.5 = (f32[8192]{0:T(1024)S(1)}, f32[8192]{0:T(1024)S(1)}, u32[]{:S(2)}, u32[]{:S(2)}) collective-permute-start(f32[8192]{0:T(1024)S(1)} %log_add_fusion.1), channel_id=1, source_target_pairs={{0,16},{4,20},{8,24},{12,28},{16,0},{20,4},{24,8},{28,12},{1,17},{... | collective-permute-start | bytes 98312 | tf_op jit(solution)/shard_map/ppermute | solution.py:48
  30.1 4.8 %collective-permute-start.4 = (f32[8192]{0:T(1024)S(1)}, f32[8192]{0:T(1024)S(1)}, u32[]{:S(2)}, u32[]{:S(2)}) collective-permute-start(f32[8192]{0:T(1024)S(1)} %log_add_fusion.1), channel_id=1, source_target_pairs={{0,8},{4,12},{8,0},{12,4},{16,24},{20,28},{24,16},{28,20},{1,9},{5... | collective-permute-start | bytes 98312 | tf_op jit(solution)/shard_map/ppermute | solution.py:48
  41.0 3.1 %collective-permute-start.9 = (f32[2048]{0:T(1024)S(1)}, f32[2048]{0:T(1024)S(1)}, u32[]{:S(2)}, u32[]{:S(2)}) collective-permute-start(f32[2048]{0:T(1024)S(1)} %bitcast.65), channel_id=1, source_target_pairs={{0,3},{1,2},{2,1},{3,0},{4,7},{5,6},{6,5},{7,4},{8,11},{9,10},{10,... | collective-permute-start | bytes 24584 | tf_op jit(solution)/shard_map/ppermute | solution.py:48
  41.1 3.7 %collective-permute-start.8 = (f32[2048]{0:T(1024)S(1)}, f32[2048]{0:T(1024)S(1)}, u32[]{:S(2)}, u32[]{:S(2)}) collective-permute-start(f32[2048]{0:T(1024)S(1)} %bitcast.66), channel_id=1, source_target_pairs={{0,2},{1,3},{2,0},{3,1},{4,6},{5,7},{6,4},{7,5},{8,10},{9,11},{10,... | collective-permute-start | bytes 24584 | tf_op jit(solution)/shard_map/ppermute | solution.py:48
  41.2 3.6 %collective-permute-start.7 = (f32[2048]{0:T(1024)S(1)}, f32[2048]{0:T(1024)S(1)}, u32[]{:S(2)}, u32[]{:S(2)}) collective-permute-start(f32[2048]{0:T(1024)S(1)} %bitcast.67), channel_id=1, source_target_pairs={{0,1},{1,0},{2,3},{3,2},{4,5},{5,4},{6,7},{7,6},{8,9},{9,8},{10,11... | collective-permute-start | bytes 24584 | tf_op jit(solution)/shard_map/ppermute | solution.py:48
  44.9 27.5 %copy-start.9 = (f32[2048]{0:T(1024)}, f32[2048]{0:T(1024)S(1)}, u32[]{:S(2)}) copy-start(f32[2048]{0:T(1024)S(1)} %multiply_subtract_fusion.2) | copy-start | bytes 24580
  50.8 4.1 %collective-permute-start.10 = (f32[8192]{0:T(1024)S(1)}, f32[8192]{0:T(1024)S(1)}, u32[]{:S(2)}, u32[]{:S(2)}) collective-permute-start(f32[8192]{0:T(1024)S(1)} %bitcast.57), channel_id=1, source_target_pairs={{0,4},{4,0},{8,12},{12,8},{16,20},{20,16},{24,28},{28,24},{1,5},{5... | collective-permute-start | bytes 98312 | tf_op jit(solution)/shard_map/ppermute | solution.py:48
  54.9 5.8 %collective-permute-start.13 = (f32[8192]{0:T(1024)S(1)}, f32[8192]{0:T(1024)S(1)}, u32[]{:S(2)}, u32[]{:S(2)}) collective-permute-start(f32[8192]{0:T(1024)S(1)} %log_add_fusion), channel_id=1, source_target_pairs={{0,24},{4,28},{8,16},{12,20},{16,8},{20,12},{24,0},{28,4},{1,25},{... | collective-permute-start | bytes 98312 | tf_op jit(solution)/shard_map/ppermute | solution.py:48
  55.3 5.4 %collective-permute-start.12 = (f32[8192]{0:T(1024)S(1)}, f32[8192]{0:T(1024)}, u32[]{:S(2)}, u32[]{:S(2)}) collective-permute-start(f32[8192]{0:T(1024)S(1)} %log_add_fusion), channel_id=1, source_target_pairs={{0,16},{4,20},{8,24},{12,28},{16,0},{20,4},{24,8},{28,12},{1,17},{... | collective-permute-start | bytes 98312 | tf_op jit(solution)/shard_map/ppermute | solution.py:48
  55.5 5.8 %collective-permute-start.11 = (f32[8192]{0:T(1024)S(1)}, f32[8192]{0:T(1024)}, u32[]{:S(2)}, u32[]{:S(2)}) collective-permute-start(f32[8192]{0:T(1024)S(1)} %log_add_fusion), channel_id=1, source_target_pairs={{0,8},{4,12},{8,0},{12,4},{16,24},{20,28},{24,16},{28,20},{1,9},{5... | collective-permute-start | bytes 98312 | tf_op jit(solution)/shard_map/ppermute | solution.py:48
  73.4 1.7 %collective-permute-start.14 = (f32[2,2,512]{2,1,0:T(2,128)S(1)}, f32[2,2,512]{2,1,0:T(2,128)S(1)}, u32[]{:S(2)}, u32[]{:S(2)}) collective-permute-start(f32[2,2,512]{2,1,0:T(2,128)S(1)} %bitcast.75), channel_id=1, source_target_pairs={{0,1},{1,0},{2,3},{3,2},{4,5},{5,4},{6,7},{7,6},{8,9},{9,8},{10,11... | collective-permute-start | bytes 24584 | tf_op jit(solution)/shard_map/ppermute | solution.py:87
  74.6 2.1 %collective-permute-start.15 = (f32[2,512,128]{2,1,0:T(8,128)S(1)}, f32[2,512,128]{2,1,0:T(8,128)S(1)}, u32[]{:S(2)}, u32[]{:S(2)}) collective-permute-start(f32[2,512,128]{2,1,0:T(8,128)S(1)} %dynamic-slice_bitcast_fusion), channel_id=1, source_target_pairs={{0,1},{1,0},{2,3},{3,2},{4,5},{5,4},{6,7},{7,6},{8,9},{9,8},{10,11... | collective-permute-start | bytes 1572872 | tf_op jit(solution)/shard_map/ppermute | solution.py:88
  75.2 3.7 %collective-permute-start.16 = (f32[2,1,512]{2,1,0:T(1,128)S(1)}, f32[2,1,512]{2,1,0:T(1,128)S(1)}, u32[]{:S(2)}, u32[]{:S(2)}) collective-permute-start(f32[2,1,512]{2,1,0:T(1,128)S(1)} %get-tuple-element.17), channel_id=1, source_target_pairs={{0,2},{1,3},{2,0},{3,1},{4,6},{5,7},{6,4},{7,5},{8,10},{9,11},{10,... | collective-permute-start | bytes 12296 | tf_op jit(solution)/shard_map/ppermute | solution.py:87
  78.1 8.7 %collective-permute-start.17 = (f32[1,512,128]{2,1,0:T(8,128)S(1)}, f32[1,512,128]{2,1,0:T(8,128)S(1)}, u32[]{:S(2)}, u32[]{:S(2)}) collective-permute-start(f32[1,512,128]{2,1,0:T(8,128)S(1)} %constant_dynamic-slice_fusion.1), channel_id=1, source_target_pairs={{0,2},{1,3},{2,0},{3,1},{4,6},{5,7},{6,4},{7,5},{8,10},{9,11},{10,... | collective-permute-start | bytes 786440 | tf_op jit(solution)/shard_map/ppermute | solution.py:88
  (9 other events, 53.7 us)
